TPU v7x, 32 devices: a whole 2x2x4 slice. The times are simulated.
32 devices in a mesh: dp: 8 (over y, x, core), tensor: 4 (over z).
Axes of the slice: x: 2, y: 2, z: 4, core: 2. Of those that a mesh axis runs over, the one named last changes fastest.
Arguments:
- tokens: bfloat16 [24576, 768], P(('dp', 'tensor')), may hold values from -6 to 6
- lengths: int32 [40], replicated, may hold values from 257 to 1024, as said below
- dealing: int32 [40], replicated, may hold values from 0 to 39, as said below
- w_query: bfloat16 [768, 768], P('dp', 'tensor'), may hold values from -0.4375 to 0.4375
- w_key: bfloat16 [768, 768], P('dp', 'tensor'), may hold values from -0.21875 to 0.21875
- w_value: bfloat16 [768, 768], P('dp', 'tensor'), may hold values from -0.21875 to 0.21875
- w_out: bfloat16 [768, 768], P('tensor', 'dp'), may hold values from -1.75 to 1.75
- w_inner: bfloat16 [768, 3072], P('dp', 'tensor'), may hold values from -0.21875 to 0.21875
- w_outer: bfloat16 [3072, 768], P('tensor', 'dp'), may hold values from -0.109375 to 0.109375
- b_query: bfloat16 [768], replicated, may hold values from -3 to 3
- b_value: bfloat16 [768], replicated, may hold values from -3 to 3
- b_out: bfloat16 [768], replicated, may hold values from -3 to 3
- b_inner: bfloat16 [3072], replicated, may hold values from -3 to 3
- b_outer: bfloat16 [768], replicated, may hold values from -3 to 3
- gain_attn: bfloat16 [768], replicated, may hold values from 0.5 to 1.5
- shift_attn: bfloat16 [768], replicated, may hold values from -2 to 2
- gain_ffn: bfloat16 [768], replicated, may hold values from 0.5 to 1.5
- shift_ffn: bfloat16 [768], replicated, may hold values from -2 to 2
- grad_out: bfloat16 [24576, 768], P(('dp', 'tensor')), may hold values from -6 to 6
Outputs:
- layer_out: bfloat16 [24576, 768], P(('dp', 'tensor'))
- grad_tokens: float32 [24576, 768], P(('dp', 'tensor'))
- grad_w_query: float32 [768, 768], P('dp', 'tensor')
- grad_w_key: float32 [768, 768], P('dp', 'tensor')
- grad_w_value: float32 [768, 768], P('dp', 'tensor')
- grad_w_out: float32 [768, 768], P('tensor', 'dp')
- grad_w_inner: float32 [768, 3072], P('dp', 'tensor')
- grad_w_outer: float32 [3072, 768], P('tensor', 'dp')
- grad_b_query: float32 [768], P(('dp', 'tensor'))
- grad_b_value: float32 [768], P(('dp', 'tensor'))
- grad_b_out: float32 [768], P(('dp', 'tensor'))
- grad_b_inner: float32 [3072], P(('dp', 'tensor'))
- grad_b_outer: float32 [768], P(('dp', 'tensor'))
- grad_gain_attn: float32 [768], P(('dp', 'tensor'))
- grad_shift_attn: float32 [768], P(('dp', 'tensor'))
- grad_gain_ffn: float32 [768], P(('dp', 'tensor'))
- grad_shift_ffn: float32 [768], P(('dp', 'tensor'))
Inputs may be any that keep to these rules, and one draw needn't show every extreme that they name: In every data group one dealt sequence has exactly 1024 tokens, and the lengths of the 5 sequences dealt to a group sum to 3072. `dealing`: A permutation of the sequences.
All inputs are finite; a program needn't handle non-finite values.
Results may differ from a plain program's by a relative error of at most 0.02.
Values may be sent and summed in bfloat16 or wider, within the bound.
No kernel may reach another device: no remote copies, remote signals or barrier semaphores. Data moves between devices by JAX's collectives and lax.ppermute only.
A program may use at most 128 MiB of HBM per device.

v0:
```python
import math

import jax
import jax.numpy as jnp
from jax import lax
from jax.sharding import PartitionSpec as P

HEAD_DIM = 64
SEQ_GRP = 5


def norm_forward(values, gain, shift):
    center = jnp.mean(values, axis=-1, keepdims=True)
    offsets = values - center
    spread = jnp.mean(offsets * offsets, axis=-1, keepdims=True)
    inverse = lax.rsqrt(spread + 1e-06)
    normed = offsets * inverse
    return (normed * gain + shift, normed, inverse)


def norm_backward(grad_y, normed, inverse, gain):
    grad_normed = grad_y * gain
    mean_one = jnp.mean(grad_normed, axis=-1, keepdims=True)
    mean_two = jnp.mean(grad_normed * normed, axis=-1, keepdims=True)
    return inverse * (grad_normed - mean_one - normed * mean_two)


def activate(values):
    return jax.nn.gelu(values, approximate=False)


def contract_last(left, right):
    return lax.dot_general(
        left, right, (((1,), (1,)), ((), ())), preferred_element_type=jnp.float32
    )


def contract_first(left, right):
    return lax.dot_general(
        left, right, (((0,), (0,)), ((), ())), preferred_element_type=jnp.float32
    )


def column_sum(values):
    return jnp.sum(values.astype(jnp.float32), axis=0)


def group_segments(lengths, dealing, group_index, group_rows):
    picked = lax.dynamic_slice_in_dim(dealing, group_index * SEQ_GRP, SEQ_GRP)
    match = picked[:, None] == jnp.arange(lengths.shape[0], dtype=jnp.int32)[None, :]
    chosen = jnp.sum(jnp.where(match, lengths[None, :], 0), axis=1)
    ends = jnp.cumsum(chosen)
    starts = ends - chosen
    places = jnp.arange(group_rows, dtype=jnp.int32)
    segment_ids = jnp.sum((places[:, None] >= ends[None, :]).astype(jnp.int32), axis=1)
    return (segment_ids, starts, ends)


def block_windows(segment_ids, starts, ends, block_rows):
    count = segment_ids.shape[0] // block_rows
    id_blocks = segment_ids.reshape(count, block_rows)
    first_ids = id_blocks[:, 0]
    last_ids = id_blocks[:, block_rows - 1]
    labels = jnp.arange(starts.shape[0], dtype=jnp.int32)
    lowest = jnp.sum(jnp.where(labels[None, :] == first_ids[:, None], starts[None, :], 0), axis=1)
    highest = jnp.sum(jnp.where(labels[None, :] == last_ids[:, None], ends[None, :], 0), axis=1) - 1
    return (lowest // block_rows, highest // block_rows)


def take_block(values, block_index, block_rows):
    return lax.dynamic_slice_in_dim(values, block_index * block_rows, block_rows, 0)


def block_scores(query_rows, key_part, row_ids, key_ids):
    score_scale = 1.0 / math.sqrt(HEAD_DIM)
    raw = (
        jnp.einsum("qhd,khd->hqk", query_rows, key_part, preferred_element_type=jnp.float32)
        * score_scale
    )
    return (raw, (row_ids[:, None] == key_ids[None, :])[None])


def attention_forward(query, key_rows, value_rows, segment_ids, windows, heads_here):
    total = query.shape[0]
    block_rows = 512
    count = total // block_rows
    query_blocks = query.reshape(count, block_rows, heads_here, HEAD_DIM)
    key_heads = key_rows.reshape(total, heads_here, HEAD_DIM)
    value_heads = value_rows.reshape(total, heads_here, HEAD_DIM)
    first_blocks, last_blocks = windows

    def one_block(element):
        query_rows, row_ids, first_block, last_block = element

        def stat_step(block_index, state):
            highest, totals = state
            key_part = take_block(key_heads, block_index, block_rows)
            key_ids = take_block(segment_ids, block_index, block_rows)
            raw, key_mask = block_scores(query_rows, key_part, row_ids, key_ids)
            block_max = jnp.max(jnp.where(key_mask, raw, -1e30), axis=-1)
            new_max = jnp.maximum(highest, block_max)
            expon = jnp.where(key_mask, jnp.exp(raw - new_max[..., None]), 0.0)
            return (new_max, totals * jnp.exp(highest - new_max) + jnp.sum(expon, axis=-1))

        begin_state = (
            jnp.full((heads_here, block_rows), -1e30, jnp.float32),
            jnp.zeros((heads_here, block_rows), jnp.float32),
        )
        highest, totals = lax.fori_loop(first_block, last_block + 1, stat_step, begin_state)
        log_totals = highest + jnp.log(totals)

        def value_step(block_index, summed):
            key_part = take_block(key_heads, block_index, block_rows)
            value_part = take_block(value_heads, block_index, block_rows)
            key_ids = take_block(segment_ids, block_index, block_rows)
            raw, key_mask = block_scores(query_rows, key_part, row_ids, key_ids)
            probs = jnp.where(key_mask, jnp.exp(raw - log_totals[..., None]), 0.0).astype(
                jnp.bfloat16
            )
            return summed + jnp.einsum(
                "hqk,khd->qhd", probs, value_part, preferred_element_type=jnp.float32
            )

        summed = lax.fori_loop(
            first_block,
            last_block + 1,
            value_step,
            jnp.zeros((block_rows, heads_here, HEAD_DIM), jnp.float32),
        )
        return (summed.astype(jnp.bfloat16), log_totals)

    context, log_totals = lax.map(
        one_block, (query_blocks, segment_ids.reshape(count, block_rows), first_blocks, last_blocks)
    )
    return (context.reshape(total, heads_here * HEAD_DIM), log_totals)


def add_block(summed, part, block_index, block_rows):
    current = take_block(summed, block_index, block_rows)
    return lax.dynamic_update_slice_in_dim(summed, current + part, block_index * block_rows, 0)


def attention_backward(
    query, key_rows, value_rows, segment_ids, windows, log_totals, grad_context, heads_here
):
    total = query.shape[0]
    count = log_totals.shape[0]
    block_rows = total // count
    score_scale = 1.0 / math.sqrt(HEAD_DIM)
    query_blocks = query.reshape(count, block_rows, heads_here, HEAD_DIM)
    grad_blocks = grad_context.reshape(count, block_rows, heads_here, HEAD_DIM)
    key_heads = key_rows.reshape(total, heads_here, HEAD_DIM)
    value_heads = value_rows.reshape(total, heads_here, HEAD_DIM)
    first_blocks, last_blocks = windows

    def one_block(sums, element):
        query_rows, row_ids, first_block, last_block, row_lse, grad_rows = element

        def probs_at(block_index):
            key_part = take_block(key_heads, block_index, block_rows)
            value_part = take_block(value_heads, block_index, block_rows)
            key_ids = take_block(segment_ids, block_index, block_rows)
            raw, key_mask = block_scores(query_rows, key_part, row_ids, key_ids)
            probs = jnp.where(key_mask, jnp.exp(raw - row_lse[..., None]), 0.0)
            grad_probs = jnp.einsum(
                "qhd,khd->hqk", grad_rows, value_part, preferred_element_type=jnp.float32
            )
            return (probs, grad_probs, key_part)

        def delta_step(block_index, row_delta):
            probs, grad_probs, key_part = probs_at(block_index)
            return row_delta + jnp.sum(grad_probs * probs, axis=-1)

        row_delta = lax.fori_loop(
            first_block,
            last_block + 1,
            delta_step,
            jnp.zeros((heads_here, block_rows), jnp.float32),
        )

        def grad_step(block_index, state):
            grad_query, grad_keys, grad_values = state
            probs, grad_probs, key_part = probs_at(block_index)
            grad_scores = (probs * (grad_probs - row_delta[..., None])).astype(jnp.bfloat16)
            value_term = jnp.einsum(
                "hqk,qhd->khd",
                probs.astype(jnp.bfloat16),
                grad_rows,
                preferred_element_type=jnp.float32,
            )
            key_term = (
                jnp.einsum(
                    "hqk,qhd->khd", grad_scores, query_rows, preferred_element_type=jnp.float32
                )
                * score_scale
            )
            grad_query = (
                grad_query
                + jnp.einsum(
                    "hqk,khd->qhd", grad_scores, key_part, preferred_element_type=jnp.float32
                )
                * score_scale
            )
            grad_keys = add_block(grad_keys, key_term, block_index, block_rows)
            grad_values = add_block(grad_values, value_term, block_index, block_rows)
            return (grad_query, grad_keys, grad_values)

        begin_state = (jnp.zeros((block_rows, heads_here, HEAD_DIM), jnp.float32), sums[0], sums[1])
        grad_query, grad_keys, grad_values = lax.fori_loop(
            first_block, last_block + 1, grad_step, begin_state
        )
        return ((grad_keys, grad_values), grad_query)

    zeros_heads = jnp.zeros((total, heads_here, HEAD_DIM), jnp.float32)
    (grad_keys, grad_values), grad_query = lax.scan(
        one_block,
        (zeros_heads, zeros_heads),
        (
            query_blocks,
            segment_ids.reshape(count, block_rows),
            first_blocks,
            last_blocks,
            log_totals,
            grad_blocks,
        ),
    )
    columns = heads_here * HEAD_DIM
    return (
        grad_query.reshape(total, columns),
        grad_keys.reshape(total, columns),
        grad_values.reshape(total, columns),
    )


def shards(
    tokens,
    lengths,
    dealing,
    w_query,
    w_key,
    w_value,
    w_out,
    w_inner,
    w_outer,
    b_query,
    b_value,
    b_out,
    b_inner,
    b_outer,
    gain_attn,
    shift_attn,
    gain_ffn,
    shift_ffn,
    grad_out,
):
    tens_count = lax.axis_size("tensor")
    tens_index = lax.axis_index("tensor")
    group_index = lax.axis_index("dp")
    rows_here = tokens.shape[0]
    width = tokens.shape[1]
    head_cols = w_query.shape[1]
    inner_cols = w_inner.shape[1]
    heads_here = head_cols // HEAD_DIM
    group_rows = rows_here * tens_count
    block_rows = 512
    segment_ids, starts, ends = group_segments(lengths, dealing, group_index, group_rows)
    windows = block_windows(segment_ids, starts, ends, block_rows)
    query_bias = lax.dynamic_slice_in_dim(b_query, tens_index * head_cols, head_cols).astype(
        jnp.float32
    )
    value_bias = lax.dynamic_slice_in_dim(b_value, tens_index * head_cols, head_cols).astype(
        jnp.float32
    )
    inner_bias = lax.dynamic_slice_in_dim(b_inner, tens_index * inner_cols, inner_cols).astype(
        jnp.float32
    )
    gain_one = gain_attn.astype(jnp.float32)
    gain_two = gain_ffn.astype(jnp.float32)
    query_full, key_full, value_full, out_full = (
        lax.all_gather(w_query, "dp", axis=0, tiled=True),
        lax.all_gather(w_key, "dp", axis=0, tiled=True),
        lax.all_gather(w_value, "dp", axis=0, tiled=True),
        lax.all_gather(w_out, "dp", axis=1, tiled=True),
    )
    whole = lax.all_gather(tokens, "tensor", axis=0, tiled=True)
    query = (jnp.dot(whole, query_full, preferred_element_type=jnp.float32) + query_bias).astype(
        jnp.bfloat16
    )
    key_rows = jnp.dot(whole, key_full, preferred_element_type=jnp.float32).astype(jnp.bfloat16)
    value_rows = (
        jnp.dot(whole, value_full, preferred_element_type=jnp.float32) + value_bias
    ).astype(jnp.bfloat16)
    context, log_totals = attention_forward(
        query, key_rows, value_rows, segment_ids, windows, heads_here
    )
    attn = lax.psum_scatter(
        jnp.dot(context, out_full, preferred_element_type=jnp.float32).astype(jnp.bfloat16),
        "tensor",
        scatter_dimension=0,
        tiled=True,
    ).astype(jnp.float32) + b_out.astype(jnp.float32)
    hidden, norm_one, inverse_one = norm_forward(
        tokens.astype(jnp.float32) + attn, gain_one, shift_attn.astype(jnp.float32)
    )
    inner_full, outer_full = (
        lax.all_gather(w_inner, "dp", axis=0, tiled=True),
        lax.all_gather(w_outer, "dp", axis=1, tiled=True),
    )
    hidden_all = lax.all_gather(hidden.astype(jnp.bfloat16), "tensor", axis=0, tiled=True)
    pre_act = jnp.dot(hidden_all, inner_full, preferred_element_type=jnp.float32) + inner_bias
    act = activate(pre_act).astype(jnp.bfloat16)
    ffn = lax.psum_scatter(
        jnp.dot(act, outer_full, preferred_element_type=jnp.float32).astype(jnp.bfloat16),
        "tensor",
        scatter_dimension=0,
        tiled=True,
    ).astype(jnp.float32) + b_outer.astype(jnp.float32)
    output, norm_two, inverse_two = norm_forward(
        hidden + ffn, gain_two, shift_ffn.astype(jnp.float32)
    )
    grad_y = grad_out.astype(jnp.float32)
    grad_resid_two = norm_backward(grad_y, norm_two, inverse_two, gain_two)
    grad_ffn = grad_resid_two.astype(jnp.bfloat16)
    grad_ffn_all = lax.all_gather(grad_ffn, "tensor", axis=0, tiled=True)
    grad_act = contract_last(grad_ffn_all, outer_full)
    unused, gelu_pull = jax.vjp(activate, pre_act)
    grad_pre = gelu_pull(grad_act)[0].astype(jnp.bfloat16)
    grad_outer_w = contract_first(act, grad_ffn_all)
    grad_inner_w = contract_first(hidden_all, grad_pre)
    grad_hidden = grad_resid_two + lax.psum_scatter(
        contract_last(grad_pre, inner_full).astype(jnp.bfloat16),
        "tensor",
        scatter_dimension=0,
        tiled=True,
    ).astype(jnp.float32)
    grad_resid_one = norm_backward(grad_hidden, norm_one, inverse_one, gain_one)
    grad_attn = grad_resid_one.astype(jnp.bfloat16)
    grad_attn_all = lax.all_gather(grad_attn, "tensor", axis=0, tiled=True)
    grad_context = contract_last(grad_attn_all, out_full).astype(jnp.bfloat16)
    grad_out_w = contract_first(context, grad_attn_all)
    grad_q_sum, grad_k_sum, grad_v_sum = attention_backward(
        query, key_rows, value_rows, segment_ids, windows, log_totals, grad_context, heads_here
    )
    grad_query = grad_q_sum.astype(jnp.bfloat16)
    grad_key = grad_k_sum.astype(jnp.bfloat16)
    grad_value = grad_v_sum.astype(jnp.bfloat16)
    grad_query_w = contract_first(whole, grad_query)
    grad_key_w = contract_first(whole, grad_key)
    grad_value_w = contract_first(whole, grad_value)
    part_query = contract_last(grad_query, query_full)
    part_key = contract_last(grad_key, key_full)
    part_value = contract_last(grad_value, value_full)
    grad_tokens = grad_resid_one + lax.psum_scatter(
        (part_query + part_key + part_value).astype(jnp.bfloat16),
        "tensor",
        scatter_dimension=0,
        tiled=True,
    ).astype(jnp.float32)
    summed_query, summed_key, summed_value, summed_out, summed_inner, summed_outer = (
        lax.psum_scatter(grad_query_w, "dp", scatter_dimension=0, tiled=True),
        lax.psum_scatter(grad_key_w, "dp", scatter_dimension=0, tiled=True),
        lax.psum_scatter(grad_value_w, "dp", scatter_dimension=0, tiled=True),
        lax.psum_scatter(grad_out_w, "dp", scatter_dimension=1, tiled=True),
        lax.psum_scatter(grad_inner_w, "dp", scatter_dimension=0, tiled=True),
        lax.psum_scatter(grad_outer_w, "dp", scatter_dimension=1, tiled=True),
    )
    zeros_width = jnp.zeros((width,), jnp.float32)
    query_bias_grad = lax.dynamic_update_slice_in_dim(
        zeros_width, column_sum(grad_query), tens_index * head_cols, 0
    )
    value_bias_grad = lax.dynamic_update_slice_in_dim(
        zeros_width, column_sum(grad_value), tens_index * head_cols, 0
    )
    inner_bias_grad = lax.dynamic_update_slice_in_dim(
        jnp.zeros((b_inner.shape[0],), jnp.float32),
        column_sum(grad_pre),
        tens_index * inner_cols,
        0,
    )
    small_sums = (
        lax.psum_scatter(query_bias_grad, ("dp", "tensor"), scatter_dimension=0, tiled=True),
        lax.psum_scatter(value_bias_grad, ("dp", "tensor"), scatter_dimension=0, tiled=True),
        lax.psum_scatter(column_sum(grad_attn), ("dp", "tensor"), scatter_dimension=0, tiled=True),
        lax.psum_scatter(inner_bias_grad, ("dp", "tensor"), scatter_dimension=0, tiled=True),
        lax.psum_scatter(column_sum(grad_ffn), ("dp", "tensor"), scatter_dimension=0, tiled=True),
        lax.psum_scatter(
            jnp.sum(grad_hidden * norm_one, axis=0),
            ("dp", "tensor"),
            scatter_dimension=0,
            tiled=True,
        ),
        lax.psum_scatter(
            jnp.sum(grad_hidden, axis=0), ("dp", "tensor"), scatter_dimension=0, tiled=True
        ),
        lax.psum_scatter(
            jnp.sum(grad_y * norm_two, axis=0), ("dp", "tensor"), scatter_dimension=0, tiled=True
        ),
        lax.psum_scatter(
            jnp.sum(grad_y, axis=0), ("dp", "tensor"), scatter_dimension=0, tiled=True
        ),
    )
    return (
        output.astype(jnp.bfloat16),
        grad_tokens,
        summed_query,
        summed_key,
        summed_value,
        summed_out,
        summed_inner,
        summed_outer,
        small_sums[0],
        small_sums[1],
        small_sums[2],
        small_sums[3],
        small_sums[4],
        small_sums[5],
        small_sums[6],
        small_sums[7],
        small_sums[8],
    )


def solution(mesh):
    return jax.shard_map(
        shards,
        mesh=mesh,
        in_specs=(
            P(("dp", "tensor"), None),
            P(),
            P(),
            P("dp", "tensor"),
            P("dp", "tensor"),
            P("dp", "tensor"),
            P("tensor", "dp"),
            P("dp", "tensor"),
            P("tensor", "dp"),
            P(),
            P(),
            P(),
            P(),
            P(),
            P(),
            P(),
            P(),
            P(),
            P(("dp", "tensor"), None),
        ),
        out_specs=(
            P(("dp", "tensor"), None),
            P(("dp", "tensor"), None),
            P("dp", "tensor"),
            P("dp", "tensor"),
            P("dp", "tensor"),
            P("tensor", "dp"),
            P("dp", "tensor"),
            P("tensor", "dp"),
            P(("dp", "tensor")),
            P(("dp", "tensor")),
            P(("dp", "tensor")),
            P(("dp", "tensor")),
            P(("dp", "tensor")),
            P(("dp", "tensor")),
            P(("dp", "tensor")),
            P(("dp", "tensor")),
            P(("dp", "tensor")),
        ),
        check_vma=False,
    )
```

profile of v0, /device:TPU:4, one launch (start us, length us, event | category | flops | bytes accessed | tf_op | source)
XLA Modules:
  0.0 1595.9 jit_solution(13351160271243572995)
XLA Ops:
  51.2 49.8 %all-gather.7.cloned.1.call-done = bf16[3072,768]{1,0:T(8,128)(2,1)} async-done(((bf16[768,768]{1,0:T(8,128)(2,1)}), bf16[3072,768]{1,0:T(8,128)(2,1)}) %all-gather.7.cloned.1.call-update) | async-done | bytes 4718608 | tf_op jit(solution)/shard_map/all_gather | solution.py:285
  116.1 160.6 %while.74 = (s32[]{:T(128)}, bf16[6,512,3,64]{1,3,2,0:T(8,128)(2,1)}, f32[6,3,512]{2,1,0:T(4,128)}, s32[6]{0:T(128)S(1)}, s32[6]{0:T(128)S(1)}, /*index=5*/bf16[...) while((s32[]{:T(128)}, ...), condition=%wide.region_12.13_spmd, body=%wide.region_5.12_spmd.sunk | while | flops 311366144 | bytes 10898215 | solution.py:132
  144.7 19.9 %while.79 = (s32[]{:T(128)}, f32[512,3,64]{0,2,1:T(8,128)S(1)}, s32[]{:T(128)}, bf16[3072,3,64]{0,2,1:T(8,128)(2,1)}, s32[512]{0:T(512)S(1)}, /*index=5*/s32[307...) while((s32[]{:T(128)}, f32[512,3,64]{0,2,1:T(8,128)S(1)}, ...), condition=%wide.region_11.11_spmd, body=%wide.region_10.10_spmd.sunk | while | flops 204832768 | bytes 1918127 | solution.py:124
  174.0 15.1 while.79
  202.3 24.7 %while.79 = (s32[]{:T(128)}, f32[512,3,64]{0,2,1:T(8,128)S(1)}, s32[]{:T(128)}, bf16[3072,3,64]{0,2,1:T(8,128)(2,1)}, s32[512]{0:T(512)S(1)}, /*index=5*/s32[307...) while((s32[]{:T(128)}, f32[512,3,64]{0,2,1:T(8,128)S(1)}, ...), condition=%wide.region_11.11_spmd, body=%wide.region_10.10_spmd.sunk | while | flops 204832768 | bytes 1918127 | solution.py:124
  236.4 15.1 while.79
  261.0 15.1 while.79
  285.9 82.4 %reduce-scatter.19.cloned.1.call-done = bf16[768,768]{1,0:T(8,128)(2,1)} async-done(((bf16[3072,768]{1,0:T(8,128)(2,1)}), bf16[768,768]{1,0:T(8,128)(2,1)}) %reduce-scatter.19.cloned.1.call-update) | async-done | bytes 1179664 | tf_op jit(solution)/shard_map/reduce_scatter | solution.py:296
  374.5 87.9 %all-gather.9.cloned.1.call-done = bf16[3072,768]{1,0:T(8,128)(2,1)} async-done(((bf16[768,768]{1,0:T(8,128)(2,1)}), bf16[3072,768]{1,0:T(8,128)(2,1)}) %all-gather.9.cloned.1.call-update) | async-done | bytes 4718608 | tf_op jit(solution)/shard_map/all_gather | solution.py:309
  462.4 26.8 %multiply_convert_fusion = (bf16[3072,768]{1,0:T(8,128)(2,1)}, f32[3072,768]{1,0:T(8,128)}, f32[3072,768]{1,0:T(8,128)}) fusion(f32[768]{0:T(1024)} %dynamic-slice_convert_fusion, bf16[3072,768]{1,0:T(8,128)(2,1)} %all-gather.9.cloned.1.call-done, bf16[768,768]{1,0:T(8,128)(2,1)} %all-gather.11.cloned.1.call-done), kind=kOutput, calls=%fused_computation.72 | convolution fusion | flops 3779592192 | bytes 29494272 | tf_op jit(solution)/shard_map/dot_general | solution.py:310
  502.3 79.5 %reduce-scatter.21.cloned.1.call-done = bf16[768,768]{1,0:T(8,128)(2,1)} async-done(((bf16[3072,768]{1,0:T(8,128)(2,1)}), bf16[768,768]{1,0:T(8,128)(2,1)}) %reduce-scatter.21.cloned.1.call-update) | async-done | bytes 1179664 | tf_op jit(solution)/shard_map/reduce_scatter | solution.py:312
  590.5 90.0 %all-gather.15.cloned.1.call-done = bf16[3072,768]{1,0:T(8,128)(2,1)} async-done(((bf16[768,768]{1,0:T(8,128)(2,1)}), bf16[3072,768]{1,0:T(8,128)(2,1)}) %all-gather.15.cloned.1.call-update) | async-done | bytes 4718608 | tf_op jit(solution)/shard_map/all_gather | solution.py:324
  680.5 13.6 convert_reduce_fusion
  701.8 83.7 %reduce-scatter.23.cloned.1.call-done = bf16[768,768]{1,0:T(8,128)(2,1)} async-done(((bf16[3072,768]{1,0:T(8,128)(2,1)}), bf16[768,768]{1,0:T(8,128)(2,1)}) %reduce-scatter.23.cloned.1.call-update) | async-done | bytes 1179664 | tf_op jit(solution)/shard_map/reduce_scatter | solution.py:330
  793.0 89.8 %all-gather.17.cloned.1.call-done = bf16[3072,768]{1,0:T(8,128)(2,1)} async-done(((bf16[768,768]{1,0:T(8,128)(2,1)}), bf16[3072,768]{1,0:T(8,128)(2,1)}) %all-gather.17.cloned.1.call-update) | async-done | bytes 4718608 | tf_op jit(solution)/shard_map/all_gather | solution.py:338
  894.5 346.5 %while.77 = (s32[]{:T(128)}, f32[3072,3,64]{0,2,1:T(8,128)}, f32[3072,3,64]{0,2,1:T(8,128)}, bf16[6,512,3,64]{1,3,2,0:T(8,128)(2,1)}, s32[6]{0:T(128)S(1)}, /*in...) while((s32[]{:T(128)}, f32[3072,3,64]{0,2,1:T(8,128)}, ...), condition=%wide.region_30.31_spmd, body=%wide.region_24.30_spmd.sunk | while | flops 717455360 | bytes 28335536 | solution.py:215
  907.0 23.9 %while.81 = (s32[]{:T(128)}, f32[512,3,64]{0,2,1:T(8,128)S(1)}, f32[3072,3,64]{0,2,1:T(8,128)}, f32[3072,3,64]{0,2,1:T(8,128)}, s32[]{:T(128)}, /*index=5*/bf16[...) while((s32[]{:T(128)}, f32[512,3,64]{0,2,1:T(8,128)S(1)}, ...), condition=%wide.region_29.29_spmd, body=%wide.region_28.28_spmd.sunk | while | flops 511934464 | bytes 18704612 | solution.py:209
  936.5 15.2 while.80
  951.8 47.1 %while.81 = (s32[]{:T(128)}, f32[512,3,64]{0,2,1:T(8,128)S(1)}, f32[3072,3,64]{0,2,1:T(8,128)}, f32[3072,3,64]{0,2,1:T(8,128)}, s32[]{:T(128)}, /*index=5*/bf16[...) while((s32[]{:T(128)}, f32[512,3,64]{0,2,1:T(8,128)S(1)}, ...), condition=%wide.region_29.29_spmd, body=%wide.region_28.28_spmd.sunk | while | flops 511934464 | bytes 18704612 | solution.py:209
  1016.0 35.5 %while.81 = (s32[]{:T(128)}, f32[512,3,64]{0,2,1:T(8,128)S(1)}, f32[3072,3,64]{0,2,1:T(8,128)}, f32[3072,3,64]{0,2,1:T(8,128)}, s32[]{:T(128)}, /*index=5*/bf16[...) while((s32[]{:T(128)}, f32[512,3,64]{0,2,1:T(8,128)S(1)}, ...), condition=%wide.region_29.29_spmd, body=%wide.region_28.28_spmd.sunk | while | flops 511934464 | bytes 18704612 | solution.py:209
  1057.1 19.0 %while.80 = (s32[]{:T(128)}, f32[3,512]{1,0:T(4,128)S(1)}, s32[]{:T(128)}, bf16[3072,3,64]{0,2,1:T(8,128)(2,1)}, bf16[512,3,64]{0,2,1:T(8,128)(2,1)S(1)}, /*inde...) while((s32[]{:T(128)}, f32[3,512]{1,0:T(4,128)S(1)}, ...), condition=%wide.region_27.27_spmd, body=%wide.region_25.26_spmd.sunk | while | flops 205520896 | bytes 7641279 | solution.py:174
  1076.2 58.8 %while.81 = (s32[]{:T(128)}, f32[512,3,64]{0,2,1:T(8,128)S(1)}, f32[3072,3,64]{0,2,1:T(8,128)}, f32[3072,3,64]{0,2,1:T(8,128)}, s32[]{:T(128)}, /*index=5*/bf16[...) while((s32[]{:T(128)}, f32[512,3,64]{0,2,1:T(8,128)S(1)}, ...), condition=%wide.region_29.29_spmd, body=%wide.region_28.28_spmd.sunk | while | flops 511934464 | bytes 18704612 | solution.py:209
  1152.0 35.5 %while.81 = (s32[]{:T(128)}, f32[512,3,64]{0,2,1:T(8,128)S(1)}, f32[3072,3,64]{0,2,1:T(8,128)}, f32[3072,3,64]{0,2,1:T(8,128)}, s32[]{:T(128)}, /*index=5*/bf16[...) while((s32[]{:T(128)}, f32[512,3,64]{0,2,1:T(8,128)S(1)}, ...), condition=%wide.region_29.29_spmd, body=%wide.region_28.28_spmd.sunk | while | flops 511934464 | bytes 18704612 | solution.py:209
  1193.1 11.4 while.80
  1204.6 35.5 %while.81 = (s32[]{:T(128)}, f32[512,3,64]{0,2,1:T(8,128)S(1)}, f32[3072,3,64]{0,2,1:T(8,128)}, f32[3072,3,64]{0,2,1:T(8,128)}, s32[]{:T(128)}, /*index=5*/bf16[...) while((s32[]{:T(128)}, f32[512,3,64]{0,2,1:T(8,128)S(1)}, ...), condition=%wide.region_29.29_spmd, body=%wide.region_28.28_spmd.sunk | while | flops 511934464 | bytes 18704612 | solution.py:209
  1308.8 43.7 %all-reduce.9 = (f32[768]{0:T(1024)S(1)}, f32[768]{0:T(1024)S(1)}, f32[768]{0:T(1024)S(1)}, f32[3072]{0:T(1024)S(1)}, f32[768]{0:T(1024)S(1)}, /*index=5*/f32[76...) all-reduce(f32[768]{0:T(1024)S(1)} %dynamic_update_slice.27, ...), channel_id=12, replica_groups=mesh['dp'=8,'tensor'=4] {'dp','tensor'}, use_global_device_ids=true, to_apply=%region_39.40.clone | all-reduce | flops 9216 | bytes 73728
  1359.4 20.7 %reduce-scatter.25.cloned.1.call-done = bf16[768,768]{1,0:T(8,128)(2,1)} async-done(((bf16[3072,768]{1,0:T(8,128)(2,1)}), bf16[768,768]{1,0:T(8,128)(2,1)}) %reduce-scatter.25.cloned.1.call-update) | async-done | bytes 1179664 | tf_op jit(solution)/shard_map/reduce_scatter | solution.py:353
  1383.0 43.6 %reduce-scatter.29.cloned.1.call-done = f32[768,96]{0,1:T(8,128)} async-done(((f32[768,768]{0,1:T(8,128)}), f32[768,96]{0,1:T(8,128)}) %reduce-scatter.29.cloned.1.call-update) | async-done | bytes 294928 | tf_op jit(solution)/shard_map/reduce_scatter | solution.py:365
  1426.6 46.0 %reduce-scatter.27.cloned.1.call-done = f32[96,768]{1,0:T(8,128)} async-done(((f32[768,768]{1,0:T(8,128)}), f32[96,768]{1,0:T(8,128)}) %reduce-scatter.27.cloned.1.call-update) | async-done | bytes 294928 | tf_op jit(solution)/shard_map/reduce_scatter | solution.py:364
  1472.6 38.7 %reduce-scatter.31.cloned.1.call-done = f32[96,192]{1,0:T(8,128)} async-done(((f32[768,192]{1,0:T(8,128)}), f32[96,192]{1,0:T(8,128)}) %reduce-scatter.31.cloned.1.call-update) | async-done | bytes 73744
  1511.3 38.5 %reduce-scatter.35.cloned.1.call-done = f32[96,192]{1,0:T(8,128)} async-done(((f32[768,192]{1,0:T(8,128)}), f32[96,192]{1,0:T(8,128)}) %reduce-scatter.35.cloned.1.call-update) | async-done | bytes 73744
  1549.8 38.7 %reduce-scatter.33.cloned.1.call-done = f32[96,192]{1,0:T(8,128)} async-done(((f32[768,192]{1,0:T(8,128)}), f32[96,192]{1,0:T(8,128)}) %reduce-scatter.33.cloned.1.call-update) | async-done | bytes 73744
  (768 shorter events, 658.3 us)
Async XLA Ops:
  8.0 93.0 %all-gather.7.cloned.1.call-start = ((), (), s32[]{:S(2)}) async-start(), calls=%async_computation.10 | async-start | bytes 5898240 | tf_op jit(solution)/shard_map/all_gather | solution.py:285
  8.8 359.5 %reduce-scatter.19.cloned.1.call-start = ((), (), s32[]{:S(2)}) async-start(), calls=%async_computation.11 | async-start | bytes 5898240 | tf_op jit(solution)/shard_map/reduce_scatter | solution.py:296
  21.2 83.9 %copy-start.16 = (bf16[768,192]{1,0:T(8,128)(2,1)}, bf16[768,192]{1,0:T(8,128)(2,1)S(1)}, u32[]{:S(2)}) copy-start(bf16[768,192]{1,0:T(8,128)(2,1)S(1)} %all_gather.31) | copy-start | bytes 884740
  30.0 83.4 %copy-start.15 = (bf16[768,192]{1,0:T(8,128)(2,1)}, bf16[768,192]{1,0:T(8,128)(2,1)S(1)}, u32[]{:S(2)}) copy-start(bf16[768,192]{1,0:T(8,128)(2,1)S(1)} %all_gather.33) | copy-start | bytes 884740
  39.3 70.0 %copy-start.13 = (bf16[768,192]{1,0:T(8,128)(2,1)}, bf16[768,192]{1,0:T(8,128)(2,1)S(1)}, u32[]{:S(2)}) copy-start(bf16[768,192]{1,0:T(8,128)(2,1)S(1)} %all_gather.32) | copy-start | bytes 884740
  107.4 6.0 slice-start
  284.4 83.9 %copy-start.1 = (bf16[768,768]{1,0:T(8,128)(2,1)S(1)}, bf16[768,768]{1,0:T(8,128)(2,1)}, u32[]{:S(2)}) copy-start(bf16[768,768]{1,0:T(8,128)(2,1)} %param.31) | copy-start | bytes 3538948
  284.4 90.1 %all-gather.11.cloned.1.call-start = ((), (), s32[]{:S(2)}) async-start(), calls=%async_computation.13 | async-start | bytes 1327104 | tf_op jit(solution)/shard_map/all_gather | solution.py:306
  285.0 177.4 %all-gather.9.cloned.1.call-start = ((), (), s32[]{:S(2)}) async-start(), calls=%async_computation.12 | async-start | bytes 5898240 | tf_op jit(solution)/shard_map/all_gather | solution.py:309
  372.5 116.7 %all-gather.13.cloned.1.call-start = ((), (), s32[]{:S(2)}) async-start(), calls=%async_computation.14 | async-start | bytes 1327104 | tf_op jit(solution)/shard_map/all_gather | solution.py:307
  373.1 208.7 %reduce-scatter.21.cloned.1.call-start = ((), (), s32[]{:S(2)}) async-start(), calls=%async_computation.15 | async-start | bytes 5898240 | tf_op jit(solution)/shard_map/reduce_scatter | solution.py:312
  498.0 182.5 %all-gather.15.cloned.1.call-start = ((), (), s32[]{:S(2)}) async-start(), calls=%async_computation.16 | async-start | bytes 5898240 | tf_op jit(solution)/shard_map/all_gather | solution.py:324
  590.4 195.1 %reduce-scatter.23.cloned.1.call-start = ((), (), s32[]{:S(2)}) async-start(), calls=%async_computation.17 | async-start | bytes 5898240 | tf_op jit(solution)/shard_map/reduce_scatter | solution.py:330
  680.5 15.7 copy-start.32
  701.8 181.1 %all-gather.17.cloned.1.call-start = ((), (), s32[]{:S(2)}) async-start(), calls=%async_computation.18 | async-start | bytes 5898240 | tf_op jit(solution)/shard_map/all_gather | solution.py:338
  792.8 565.0 %reduce-scatter.37.cloned.1.call-start = ((), (), s32[]{:S(2)}) async-start(), calls=%async_computation.25 | async-start | bytes 884736
  1244.2 5.1 copy-start
  1249.3 6.1 slice-start.2
  1250.3 5.1 slice-start.3
  1250.3 5.1 copy-start.7
  1258.3 121.8 %reduce-scatter.25.cloned.1.call-start = ((), (), s32[]{:S(2)}) async-start(), calls=%async_computation.19 | async-start | bytes 5898240 | tf_op jit(solution)/shard_map/reduce_scatter | solution.py:353
  1268.8 157.9 %reduce-scatter.29.cloned.1.call-start = ((), (), s32[]{:S(2)}) async-start(), calls=%async_computation.21 | async-start | bytes 2654208 | tf_op jit(solution)/shard_map/reduce_scatter | solution.py:365
  1277.9 194.7 %reduce-scatter.27.cloned.1.call-start = ((), (), s32[]{:S(2)}) async-start(), calls=%async_computation.20 | async-start | bytes 2654208 | tf_op jit(solution)/shard_map/reduce_scatter | solution.py:364
  1287.5 223.8 %reduce-scatter.31.cloned.1.call-start = ((), (), s32[]{:S(2)}) async-start(), calls=%async_computation.22 | async-start | bytes 884736
  1294.1 255.8 %reduce-scatter.35.cloned.1.call-start = ((), (), s32[]{:S(2)}) async-start(), calls=%async_computation.24 | async-start | bytes 884736
  1298.7 7.6 copy-start.28
  1298.7 289.8 %reduce-scatter.33.cloned.1.call-start = ((), (), s32[]{:S(2)}) async-start(), calls=%async_computation.23 | async-start | bytes 884736
  1303.9 4.9 copy-start.24
  1303.9 4.9 copy-start.25
  1303.9 4.9 copy-start.26
  1303.9 4.9 copy-start.27
  1303.9 76.2 %copy-start.4 = (f32[768,768]{1,0:T(8,128)S(1)}, f32[768,768]{1,0:T(8,128)}, u32[]{:S(2)}) copy-start(f32[768,768]{1,0:T(8,128)} %get-tuple-element.689) | copy-start | bytes 7077892
  (26 other events, 67.0 us)
Sparse Core Ops, SparseCore 0:
  10.4 90.5 all-gather.6
  284.5 83.6 reduce-scatter.18
  590.5 89.8 all-gather.14
  792.9 89.9 all-gather.16
Sparse Core Ops, SparseCore 1:
  286.8 22.2 all-gather.10
  372.6 89.8 all-gather.8
  464.2 22.1 all-gather.12
  498.1 83.6 reduce-scatter.20
  701.8 83.6 reduce-scatter.22
  1258.4 33.2 reduce-scatter.36
  1293.8 86.2 reduce-scatter.24
  1383.9 42.6 reduce-scatter.28
  1430.4 42.2 reduce-scatter.26
  1476.4 34.9 reduce-scatter.30
  1514.9 34.9 reduce-scatter.34
  1553.6 34.9 reduce-scatter.32
where the time goes:
time: 1610 us; the launch traced here: 1600 us
  waiting for transfers between devices  791 us (49%)
  matrix products  402 us (25%)
  loops' own time  126 us (8%)
  local copies, waits for them, and re-layouts  103 us (6%)
  blocking collectives  81.4 us (5%)
  other arithmetic  74.2 us (5%)
  between operations  16.2 us (1%)
    unnamed x20, waiting for transfers between devices  118 us
    all_gather x1, waiting for transfers between devices, shards(): grad_ffn_all = lax.all_gather(grad_ffn, 'tensor', axis=0, tiled=True)  90 us
    all_gather x1, waiting for transfers between devices, shards(): grad_attn_all = lax.all_gather(grad_attn, 'tensor', axis=0, tiled=True)  89.8 us
    all_gather x1, waiting for transfers between devices, shards(): lax.all_gather(hidden.astype(jnp.bfloat16), 'tensor', axis=0, tiled=True)  87.9 us
    dot_general x40, matrix products, probs_at(): jnp.einsum('qhd,khd->hqk', grad_rows, value_part, preferred_element_type=...  86 us
    reduce_scatter x1, waiting for transfers between devices, shards(): lax.psum_scatter(contract_last(grad_pre, inner_full).astype(jnp.bfloat16)...  83.7 us
    reduce_scatter x1, waiting for transfers between devices, shards(): lax.psum_scatter(jnp.dot(context, out_full, preferred_element_type=jnp.fl...  82.4 us
    reduce_scatter x1, waiting for transfers between devices, shards(): lax.psum_scatter(jnp.dot(act, outer_full, preferred_element_type=jnp.floa...  79.5 us
  transfers between devices with their start and end apart: 16, of which 13 were waited for; matrix products, arithmetic and copies ran while one was open for 6% of the time, Pallas kernels for 0%

commit v1 on v0

v1 whole, which is shorter than its diff:
```python
import math

import jax
import jax.numpy as jnp
from jax import lax
from jax.experimental import pallas as pl
from jax.experimental.pallas import tpu as pltpu
from jax.sharding import PartitionSpec as P

HEAD_DIM = 64
LONGEST = 1024
BLOCK = 256

NEG = -1e30


def _fwd_kernel(lo_ref, hi_ref, q_ref, k_ref, v_ref, qs_ref, ks_ref, o_ref, lse_ref, m_sc, l_sc, acc_sc):
    i = pl.program_id(0)
    j = pl.program_id(1)
    kv = lo_ref[i] + j

    @pl.when(j == 0)
    def _():
        m_sc[...] = jnp.full_like(m_sc, NEG)
        l_sc[...] = jnp.zeros_like(l_sc)
        acc_sc[...] = jnp.zeros_like(acc_sc)

    @pl.when(kv <= hi_ref[i])
    def _():
        s = jnp.einsum("hqd,hkd->hqk", q_ref[...], k_ref[...], preferred_element_type=jnp.float32) * 0.125
        mask = (qs_ref[...] == ks_ref[...])[None]
        s = jnp.where(mask, s, NEG)
        m_old = m_sc[...]
        m_new = jnp.maximum(m_old, jnp.max(s, axis=-1, keepdims=True))
        alpha = jnp.exp(m_old - m_new)
        p = jnp.where(mask, jnp.exp(s - m_new), 0.0)
        l_sc[...] = alpha * l_sc[...] + jnp.sum(p, axis=-1, keepdims=True)
        acc_sc[...] = alpha * acc_sc[...] + jnp.einsum(
            "hqk,hkd->hqd", p.astype(jnp.bfloat16), v_ref[...], preferred_element_type=jnp.float32
        )
        m_sc[...] = m_new

    @pl.when(j == pl.num_programs(1) - 1)
    def _():
        o_ref[...] = acc_sc[...] / l_sc[...]
        lse_ref[...] = m_sc[...] + jnp.log(l_sc[...])


def _dq_kernel(lo_ref, hi_ref, q_ref, k_ref, v_ref, qs_ref, ks_ref, lse_ref, dl_ref, do_ref, dq_ref, acc_sc):
    i = pl.program_id(0)
    j = pl.program_id(1)
    kv = lo_ref[i] + j

    @pl.when(j == 0)
    def _():
        acc_sc[...] = jnp.zeros_like(acc_sc)

    @pl.when(kv <= hi_ref[i])
    def _():
        k = k_ref[...]
        s = jnp.einsum("hqd,hkd->hqk", q_ref[...], k, preferred_element_type=jnp.float32) * 0.125
        mask = (qs_ref[...] == ks_ref[...])[None]
        p = jnp.where(mask, jnp.exp(s - lse_ref[...]), 0.0)
        dp = jnp.einsum("hqd,hkd->hqk", do_ref[...], v_ref[...], preferred_element_type=jnp.float32)
        ds = (p * (dp - dl_ref[...])).astype(jnp.bfloat16)
        acc_sc[...] += jnp.einsum("hqk,hkd->hqd", ds, k, preferred_element_type=jnp.float32)

    @pl.when(j == pl.num_programs(1) - 1)
    def _():
        dq_ref[...] = acc_sc[...] * 0.125


def _dkv_kernel(lo_ref, hi_ref, q_ref, k_ref, v_ref, qs_ref, ks_ref, lse_ref, dl_ref, do_ref, dk_ref, dv_ref, dk_sc, dv_sc):
    j = pl.program_id(0)
    i = pl.program_id(1)
    qb = lo_ref[j] + i

    @pl.when(i == 0)
    def _():
        dk_sc[...] = jnp.zeros_like(dk_sc)
        dv_sc[...] = jnp.zeros_like(dv_sc)

    @pl.when(qb <= hi_ref[j])
    def _():
        q = q_ref[...]
        do = do_ref[...]
        s = jnp.einsum("hqd,hkd->hqk", q, k_ref[...], preferred_element_type=jnp.float32) * 0.125
        mask = (qs_ref[...] == ks_ref[...])[None]
        p = jnp.where(mask, jnp.exp(s - lse_ref[...]), 0.0)
        dp = jnp.einsum("hqd,hkd->hqk", do, v_ref[...], preferred_element_type=jnp.float32)
        ds = (p * (dp - dl_ref[...])).astype(jnp.bfloat16)
        dv_sc[...] += jnp.einsum("hqk,hqd->hkd", p.astype(jnp.bfloat16), do, preferred_element_type=jnp.float32)
        dk_sc[...] += jnp.einsum("hqk,hqd->hkd", ds, q, preferred_element_type=jnp.float32)

    @pl.when(i == pl.num_programs(1) - 1)
    def _():
        dk_ref[...] = dk_sc[...] * 0.125
        dv_ref[...] = dv_sc[...]


def _clamp(start, step, last):
    return jnp.minimum(start + step, jnp.maximum(last, 0))


def flash_forward(q, k, v, q_ids, k_ids, lo, hi, block_q, block_k, steps):
    heads, nq, hd = q.shape
    nk = k.shape[1]
    qs = q_ids.reshape(nq, 1)
    ks = k_ids.reshape(1, nk)

    def kv_map(i, j, lo_ref, hi_ref):
        return (0, _clamp(lo_ref[i], j, hi_ref[i]), 0)

    def ks_map(i, j, lo_ref, hi_ref):
        return (0, _clamp(lo_ref[i], j, hi_ref[i]))

    grid_spec = pltpu.PrefetchScalarGridSpec(
        num_scalar_prefetch=2,
        grid=(nq // block_q, steps),
        in_specs=[
            pl.BlockSpec((heads, block_q, hd), lambda i, j, a, b: (0, i, 0)),
            pl.BlockSpec((heads, block_k, hd), kv_map),
            pl.BlockSpec((heads, block_k, hd), kv_map),
            pl.BlockSpec((block_q, 1), lambda i, j, a, b: (i, 0)),
            pl.BlockSpec((1, block_k), ks_map),
        ],
        out_specs=[
            pl.BlockSpec((heads, block_q, hd), lambda i, j, a, b: (0, i, 0)),
            pl.BlockSpec((heads, block_q, 1), lambda i, j, a, b: (0, i, 0)),
        ],
        scratch_shapes=[
            pltpu.VMEM((heads, block_q, 1), jnp.float32),
            pltpu.VMEM((heads, block_q, 1), jnp.float32),
            pltpu.VMEM((heads, block_q, hd), jnp.float32),
        ],
    )
    return pl.pallas_call(
        _fwd_kernel,
        grid_spec=grid_spec,
        out_shape=[
            jax.ShapeDtypeStruct((heads, nq, hd), jnp.float32),
            jax.ShapeDtypeStruct((heads, nq, 1), jnp.float32),
        ],
        compiler_params=pltpu.CompilerParams(
            dimension_semantics=("arbitrary", "arbitrary"), vmem_limit_bytes=100 * 1024 * 1024 // 2
        ),
    )(lo, hi, q, k, v, qs, ks)


def flash_dq(q, k, v, q_ids, k_ids, lse, delta, do, lo, hi, block_q, block_k, steps):
    heads, nq, hd = q.shape
    nk = k.shape[1]
    qs = q_ids.reshape(nq, 1)
    ks = k_ids.reshape(1, nk)

    def kv_map(i, j, lo_ref, hi_ref):
        return (0, _clamp(lo_ref[i], j, hi_ref[i]), 0)

    def ks_map(i, j, lo_ref, hi_ref):
        return (0, _clamp(lo_ref[i], j, hi_ref[i]))

    row = lambda i, j, a, b: (0, i, 0)
    grid_spec = pltpu.PrefetchScalarGridSpec(
        num_scalar_prefetch=2,
        grid=(nq // block_q, steps),
        in_specs=[
            pl.BlockSpec((heads, block_q, hd), row),
            pl.BlockSpec((heads, block_k, hd), kv_map),
            pl.BlockSpec((heads, block_k, hd), kv_map),
            pl.BlockSpec((block_q, 1), lambda i, j, a, b: (i, 0)),
            pl.BlockSpec((1, block_k), ks_map),
            pl.BlockSpec((heads, block_q, 1), row),
            pl.BlockSpec((heads, block_q, 1), row),
            pl.BlockSpec((heads, block_q, hd), row),
        ],
        out_specs=pl.BlockSpec((heads, block_q, hd), row),
        scratch_shapes=[pltpu.VMEM((heads, block_q, hd), jnp.float32)],
    )
    return pl.pallas_call(
        _dq_kernel,
        grid_spec=grid_spec,
        out_shape=jax.ShapeDtypeStruct((heads, nq, hd), jnp.float32),
        compiler_params=pltpu.CompilerParams(
            dimension_semantics=("arbitrary", "arbitrary"), vmem_limit_bytes=100 * 1024 * 1024 // 2
        ),
    )(lo, hi, q, k, v, qs, ks, lse, delta, do)


def flash_dkv(q, k, v, q_ids, k_ids, lse, delta, do, qlo, qhi, block_q, block_k, steps):
    heads, nq, hd = q.shape
    nk = k.shape[1]
    qs = q_ids.reshape(nq, 1)
    ks = k_ids.reshape(1, nk)

    def q_map(j, i, lo_ref, hi_ref):
        return (0, _clamp(lo_ref[j], i, hi_ref[j]), 0)

    def qs_map(j, i, lo_ref, hi_ref):
        return (_clamp(lo_ref[j], i, hi_ref[j]), 0)

    col = lambda j, i, a, b: (0, j, 0)
    grid_spec = pltpu.PrefetchScalarGridSpec(
        num_scalar_prefetch=2,
        grid=(nk // block_k, steps),
        in_specs=[
            pl.BlockSpec((heads, block_q, hd), q_map),
            pl.BlockSpec((heads, block_k, hd), col),
            pl.BlockSpec((heads, block_k, hd), col),
            pl.BlockSpec((block_q, 1), qs_map),
            pl.BlockSpec((1, block_k), lambda j, i, a, b: (0, j)),
            pl.BlockSpec((heads, block_q, 1), q_map),
            pl.BlockSpec((heads, block_q, 1), q_map),
            pl.BlockSpec((heads, block_q, hd), q_map),
        ],
        out_specs=[pl.BlockSpec((heads, block_k, hd), col), pl.BlockSpec((heads, block_k, hd), col)],
        scratch_shapes=[pltpu.VMEM((heads, block_k, hd), jnp.float32), pltpu.VMEM((heads, block_k, hd), jnp.float32)],
    )
    return pl.pallas_call(
        _dkv_kernel,
        grid_spec=grid_spec,
        out_shape=[
            jax.ShapeDtypeStruct((heads, nk, hd), jnp.float32),
            jax.ShapeDtypeStruct((heads, nk, hd), jnp.float32),
        ],
        compiler_params=pltpu.CompilerParams(
            dimension_semantics=("arbitrary", "arbitrary"), vmem_limit_bytes=100 * 1024 * 1024 // 2
        ),
    )(qlo, qhi, q, k, v, qs, ks, lse, delta, do)


def block_ranges(q_ids, k_ids, q_start, q_end, block_q, block_k):
    nq = q_ids.shape[0]
    nk = k_ids.shape[0]
    nqb, nkb = nq // block_q, nk // block_k
    first = q_start.reshape(nqb, block_q)[:, 0]
    last = q_end.reshape(nqb, block_q)[:, block_q - 1]
    lo = jnp.clip(first // block_k, 0, nkb - 1).astype(jnp.int32)
    hi = jnp.clip((last - 1) // block_k, 0, nkb - 1).astype(jnp.int32)
    kb = jnp.arange(nkb, dtype=jnp.int32)
    qb = jnp.arange(nqb, dtype=jnp.int32)
    cover = (lo[:, None] <= kb[None, :]) & (kb[None, :] <= hi[:, None])
    qlo = jnp.min(jnp.where(cover, qb[:, None], nqb), axis=0).astype(jnp.int32)
    qhi = jnp.max(jnp.where(cover, qb[:, None], -1), axis=0).astype(jnp.int32)
    return lo, hi, qlo, qhi


def norm_forward(values, gain, shift):
    center = jnp.mean(values, axis=-1, keepdims=True)
    offsets = values - center
    spread = jnp.mean(offsets * offsets, axis=-1, keepdims=True)
    inverse = lax.rsqrt(spread + 1e-06)
    normed = offsets * inverse
    return (normed * gain + shift, normed, inverse)


def norm_backward(grad_y, normed, inverse, gain):
    grad_normed = grad_y * gain
    mean_one = jnp.mean(grad_normed, axis=-1, keepdims=True)
    mean_two = jnp.mean(grad_normed * normed, axis=-1, keepdims=True)
    return inverse * (grad_normed - mean_one - normed * mean_two)


def activate(values):
    return jax.nn.gelu(values, approximate=False)


def contract_last(left, right):
    return lax.dot_general(left, right, (((1,), (1,)), ((), ())), preferred_element_type=jnp.float32)


def contract_first(left, right):
    return lax.dot_general(left, right, (((0,), (0,)), ((), ())), preferred_element_type=jnp.float32)


def column_sum(values):
    return jnp.sum(values.astype(jnp.float32), axis=0)


def group_segments(lengths, dealing, group_index, group_rows, per_group):
    picked = lax.dynamic_slice_in_dim(dealing, group_index * per_group, per_group)
    match = picked[:, None] == jnp.arange(lengths.shape[0], dtype=jnp.int32)[None, :]
    chosen = jnp.sum(jnp.where(match, lengths[None, :], 0), axis=1)
    ends = jnp.cumsum(chosen)
    starts = ends - chosen
    places = jnp.arange(group_rows, dtype=jnp.int32)
    segment_ids = jnp.sum((places[:, None] >= ends[None, :]).astype(jnp.int32), axis=1)
    return (segment_ids, starts, ends)


def gather_weight(w, rows_over_dp):
    dp = lax.axis_size("dp")
    tens = lax.axis_size("tensor")
    r, c = w.shape
    full = lax.all_gather(w, ("dp", "tensor"), axis=0, tiled=False).reshape(dp, tens, r, c)
    if rows_over_dp:
        return full.transpose(0, 2, 1, 3).reshape(dp * r, tens * c)
    return full.transpose(1, 2, 0, 3).reshape(tens * r, dp * c)


def scatter_grad(g, rows_over_dp):
    dp = lax.axis_size("dp")
    tens = lax.axis_size("tensor")
    if rows_over_dp:
        r, c = g.shape[0] // dp, g.shape[1] // tens
        blocks = g.reshape(dp, r, tens, c).transpose(0, 2, 1, 3)
    else:
        r, c = g.shape[0] // tens, g.shape[1] // dp
        blocks = g.reshape(tens, r, dp, c).transpose(2, 0, 1, 3)
    blocks = blocks.reshape(dp * tens, r, c)
    return lax.psum_scatter(blocks, ("dp", "tensor"), scatter_dimension=0, tiled=True).reshape(r, c)


def scatter_vectors(vectors):
    parts = lax.axis_size("dp") * lax.axis_size("tensor")
    joined = jnp.concatenate([v.reshape(parts, -1) for v in vectors], axis=1)
    summed = lax.psum_scatter(joined, ("dp", "tensor"), scatter_dimension=0, tiled=True)[0]
    out, at = [], 0
    for v in vectors:
        n = v.shape[0] // parts
        out.append(summed[at:at + n])
        at += n
    return out


def halo_plan(rows):
    hops = -(-LONGEST // rows)
    takes = [rows] * (hops - 1) + [LONGEST - rows * (hops - 1)]
    return takes


def shift_rows(values, distance, count):
    if distance >= count:
        return jnp.zeros_like(values)
    if distance > 0:
        pairs = [(s, s + distance) for s in range(count - distance)]
    else:
        pairs = [(s - distance, s) for s in range(count + distance)]
    return lax.ppermute(values, "tensor", pairs)


def build_window(own, takes, count):
    rows = own.shape[0]
    left = [shift_rows(own[rows - take:], d + 1, count) for d, take in enumerate(takes)]
    right = [shift_rows(own[:take], -(d + 1), count) for d, take in enumerate(takes)]
    return jnp.concatenate(left[::-1] + [own] + right, axis=0)


def return_window(values, takes, count):
    rows = values.shape[0] - 2 * LONGEST
    total = values[LONGEST:LONGEST + rows]
    at = LONGEST
    for d, take in enumerate(takes):
        piece = values[at - take:at].astype(jnp.bfloat16)
        at -= take
        back = shift_rows(piece, -(d + 1), count).astype(jnp.float32)
        total = total + jnp.pad(back, ((rows - take, 0), (0, 0)))
    at = LONGEST + rows
    for d, take in enumerate(takes):
        piece = values[at:at + take].astype(jnp.bfloat16)
        at += take
        back = shift_rows(piece, d + 1, count).astype(jnp.float32)
        total = total + jnp.pad(back, ((0, rows - take), (0, 0)))
    return total


def to_heads(values):
    rows, width = values.shape
    return values.reshape(rows, width // HEAD_DIM, HEAD_DIM).transpose(1, 0, 2)


def from_heads(values):
    heads, rows, hd = values.shape
    return values.transpose(1, 0, 2).reshape(rows, heads * hd)


def shards(tokens, lengths, dealing, w_query, w_key, w_value, w_out, w_inner, w_outer, b_query, b_value, b_out, b_inner, b_outer, gain_attn, shift_attn, gain_ffn, shift_ffn, grad_out):
    count = lax.axis_size("tensor")
    tens_index = lax.axis_index("tensor")
    group_index = lax.axis_index("dp")
    rows = tokens.shape[0]
    group_rows = rows * count
    per_group = lengths.shape[0] // lax.axis_size("dp")
    takes = halo_plan(rows)
    window = rows + 2 * LONGEST
    seg, starts, ends = group_segments(lengths, dealing, group_index, group_rows, per_group)
    base = rows * tens_index - LONGEST
    places = base + jnp.arange(window, dtype=jnp.int32)
    valid = (places >= 0) & (places < group_rows)
    k_ids = jnp.where(valid, jnp.take(seg, jnp.clip(places, 0, group_rows - 1)), -1).astype(jnp.int32)
    q_ids = lax.dynamic_slice_in_dim(seg, rows * tens_index, rows)
    q_start = jnp.take(starts, q_ids) - base
    q_end = jnp.take(ends, q_ids) - base
    lo, hi, qlo, qhi = block_ranges(q_ids, k_ids, q_start, q_end, BLOCK, BLOCK)
    nkb = window // BLOCK
    kv_steps = min(nkb, (BLOCK + 2 * (LONGEST - 1)) // BLOCK + 2)
    q_steps = rows // BLOCK

    wq = gather_weight(w_query, True)
    wk = gather_weight(w_key, True)
    wv = gather_weight(w_value, True)
    wo = gather_weight(w_out, False)
    wi = gather_weight(w_inner, True)
    wf = gather_weight(w_outer, False)
    gain_one = gain_attn.astype(jnp.float32)
    gain_two = gain_ffn.astype(jnp.float32)

    x_own = tokens
    x_win = build_window(tokens, takes, count)
    query = (jnp.dot(x_own, wq, preferred_element_type=jnp.float32) + b_query.astype(jnp.float32)).astype(jnp.bfloat16)
    key_w = jnp.dot(x_win, wk, preferred_element_type=jnp.float32).astype(jnp.bfloat16)
    value_w = (jnp.dot(x_win, wv, preferred_element_type=jnp.float32) + b_value.astype(jnp.float32)).astype(jnp.bfloat16)
    q_h, k_h, v_h = to_heads(query), to_heads(key_w), to_heads(value_w)
    ctx_h, lse = flash_forward(q_h, k_h, v_h, q_ids, k_ids, lo, hi, BLOCK, BLOCK, kv_steps)
    context = from_heads(ctx_h).astype(jnp.bfloat16)
    attn = jnp.dot(context, wo, preferred_element_type=jnp.float32) + b_out.astype(jnp.float32)
    hidden, norm_one, inverse_one = norm_forward(tokens.astype(jnp.float32) + attn, gain_one, shift_attn.astype(jnp.float32))
    hidden_low = hidden.astype(jnp.bfloat16)
    pre_act = jnp.dot(hidden_low, wi, preferred_element_type=jnp.float32) + b_inner.astype(jnp.float32)
    act = activate(pre_act).astype(jnp.bfloat16)
    ffn = jnp.dot(act, wf, preferred_element_type=jnp.float32) + b_outer.astype(jnp.float32)
    output, norm_two, inverse_two = norm_forward(hidden + ffn, gain_two, shift_ffn.astype(jnp.float32))

    grad_y = grad_out.astype(jnp.float32)
    grad_resid_two = norm_backward(grad_y, norm_two, inverse_two, gain_two)
    grad_ffn = grad_resid_two.astype(jnp.bfloat16)
    grad_outer_w = contract_first(act, grad_ffn)
    grad_act = contract_last(grad_ffn, wf)
    unused, gelu_pull = jax.vjp(activate, pre_act)
    grad_pre = gelu_pull(grad_act)[0].astype(jnp.bfloat16)
    grad_inner_w = contract_first(hidden_low, grad_pre)
    grad_hidden = grad_resid_two + contract_last(grad_pre, wi)
    grad_resid_one = norm_backward(grad_hidden, norm_one, inverse_one, gain_one)
    grad_attn = grad_resid_one.astype(jnp.bfloat16)
    grad_out_w = contract_first(context, grad_attn)
    grad_context = contract_last(grad_attn, wo).astype(jnp.bfloat16)
    do_h = to_heads(grad_context)
    delta = jnp.sum(do_h.astype(jnp.float32) * ctx_h, axis=-1, keepdims=True)
    dq_h = flash_dq(q_h, k_h, v_h, q_ids, k_ids, lse, delta, do_h, lo, hi, BLOCK, BLOCK, kv_steps)
    dk_h, dv_h = flash_dkv(q_h, k_h, v_h, q_ids, k_ids, lse, delta, do_h, qlo, qhi, BLOCK, BLOCK, q_steps)
    grad_query = from_heads(dq_h).astype(jnp.bfloat16)
    grad_key = from_heads(dk_h).astype(jnp.bfloat16)
    grad_value = from_heads(dv_h).astype(jnp.bfloat16)
    grad_query_w = contract_first(x_own, grad_query)
    grad_key_w = contract_first(x_win, grad_key)
    grad_value_w = contract_first(x_win, grad_value)
    grad_win = contract_last(grad_key, wk) + contract_last(grad_value, wv)
    grad_tokens = grad_resid_one + contract_last(grad_query, wq) + return_window(grad_win, takes, count)

    summed = (
        scatter_grad(grad_query_w, True),
        scatter_grad(grad_key_w, True),
        scatter_grad(grad_value_w, True),
        scatter_grad(grad_out_w, False),
        scatter_grad(grad_inner_w, True),
        scatter_grad(grad_outer_w, False),
    )
    small = scatter_vectors([
        column_sum(grad_query),
        column_sum(grad_value),
        column_sum(grad_attn),
        column_sum(grad_pre),
        column_sum(grad_ffn),
        jnp.sum(grad_hidden * norm_one, axis=0),
        jnp.sum(grad_hidden, axis=0),
        jnp.sum(grad_y * norm_two, axis=0),
        jnp.sum(grad_y, axis=0),
    ])
    return (output.astype(jnp.bfloat16), grad_tokens) + summed + tuple(small)


def solution(mesh):
    rows = P(("dp", "tensor"), None)
    vec = P(("dp", "tensor"))
    return jax.shard_map(
        shards,
        mesh=mesh,
        in_specs=(rows, P(), P(), P("dp", "tensor"), P("dp", "tensor"), P("dp", "tensor"), P("tensor", "dp"), P("dp", "tensor"), P("tensor", "dp"), P(), P(), P(), P(), P(), P(), P(), P(), P(), rows),
        out_specs=(rows, rows, P("dp", "tensor"), P("dp", "tensor"), P("dp", "tensor"), P("tensor", "dp"), P("dp", "tensor"), P("tensor", "dp")) + (vec,) * 9,
        check_vma=False,
    )
```

time: 1610 us -> 1190 us (0.74)
  waiting for transfers between devices: 791 us -> 526 us
  matrix products: 402 us -> 147 us
  Pallas kernels: 0 us -> 141 us
  loops' own time: 126 us -> 0 us
  local copies, waits for them, and re-layouts: 103 us -> 203 us
  starting transfers between devices: 1.72 us -> 35.8 us
  other arithmetic: 74.2 us -> 46.6 us
  blocking collectives: 81.4 us -> 58.8 us
    dot_general x186 -> x6, matrix products: 324 us -> 55.4 us  [the longest x1 28.3 us: shards(): jnp.dot(hidden_low, wi, preferred_element_type=jnp.float32)]
    pallas_call x0 -> x3, Pallas kernels: none -> 141 us  [the longest x1 56 us: flash_dkv(): pl.pallas_call(_dkv_kernel, grid_spec=grid_spec, out_shape=[jax.ShapeDtyp...]
    all_gather x6, waiting for transfers between devices: 318 us -> 180 us  [gather_weight(): lax.all_gather(w, ('dp', 'tensor'), axis=0, tiled=False)]
    another operation x26 -> x0, loops' own time: 126 us -> none  [the longest x6 53.7 us: one_block(): lax.fori_loop(first_block, last_block + 1, grad_step, begin_state)]
    unnamed x20 -> x12, waiting for transfers between devices: 118 us -> 3.73 us
    reshape x3 -> x30, local copies, waits for them, and re-layouts: 4.6 us -> 91 us  [the longest x7 26.4 us: gather_weight(): lax.all_gather(w, ('dp', 'tensor'), axis=0, tiled=False)]
    dynamic_slice x117 -> x1, local copies, waits for them, and re-layouts: 53 us -> 0.07 us  [group_segments(): lax.dynamic_slice_in_dim(dealing, group_index * per_group, per_group)]
    all_gather x4 -> x0, blocking collectives: 37.7 us -> none  [the longest x1 9.99 us: shards(): lax.all_gather(w_out, 'dp', axis=1, tiled=True)]
  transfers between devices with their start and end apart: 16 -> 20, of which waited for: 13 -> 8; matrix products, arithmetic and copies ran while one was open for 6% -> 26% of each run, Pallas kernels for 0% -> 12%
where the time goes in v1:
time: 1190 us; the launch traced here: 1170 us
  waiting for transfers between devices  526 us (44%)
  local copies, waits for them, and re-layouts  203 us (17%)
  matrix products  147 us (12%)
  Pallas kernels  141 us (12%)
  blocking collectives  58.8 us (5%)
  other arithmetic  46.6 us (4%)
  starting transfers between devices  35.8 us (3%)
  between operations  15.5 us (1%)
    reduce_scatter x6, waiting for transfers between devices, scatter_grad(): lax.psum_scatter(blocks, ('dp', 'tensor'), scatter_dimension=0, tiled=True)  342 us
    all_gather x6, waiting for transfers between devices, gather_weight(): lax.all_gather(w, ('dp', 'tensor'), axis=0, tiled=False)  180 us
    unnamed x1, blocking collectives  58.8 us
    pallas_call x1, Pallas kernels, flash_dkv(): pl.pallas_call(_dkv_kernel, grid_spec=grid_spec, out_shape=[jax.ShapeDtyp...  56 us
    pallas_call x1, Pallas kernels, flash_forward(): pl.pallas_call(_fwd_kernel, grid_spec=grid_spec, out_shape=[jax.ShapeDtyp...  48.6 us
    dot_general x6, matrix products, contract_last(): lax.dot_general(left, right, (((1,), (1,)), ((), ())), preferred_element_...  46.6 us
    dot_general x6, matrix products, contract_first(): lax.dot_general(left, right, (((0,), (0,)), ((), ())), preferred_element_...  44.6 us
    pallas_call x1, Pallas kernels, flash_dq(): pl.pallas_call(_dq_kernel, grid_spec=grid_spec, out_shape=jax.ShapeDtypeS...  36.8 us
  transfers between devices with their start and end apart: 20, of which 8 were waited for; matrix products, arithmetic and copies ran while one was open for 26% of the time, Pallas kernels for 12%

profile of v1, /device:TPU:4, one launch (start us, length us, event | category | flops | bytes accessed | tf_op | source)
XLA Modules:
  0.0 1174.3 jit_solution(7819632162306692562)
XLA Ops:
  39.2 14.9 %gather_fusion = s32[2816]{0:T(1024)S(1)} fusion(s32[3072]{0:T(1024)S(1)} %convert_reduce_fusion.6, s32[3072]{0:T(1024)S(1)} %pad_clamp_fusion), kind=kCustom, calls=%fused_computation | custom fusion | bytes 33792 | tf_op jit(solution)/shard_map/jit(_take)/gather | solution.py:389
  64.3 9.7 all-gather.13.cloned.1.call-done
  78.2 53.3 %all-gather.15.cloned.1.call-done = bf16[3072,192]{1,0:T(8,128)(2,1)} async-done(((bf16[96,192]{1,0:T(8,128)(2,1)}), bf16[3072,192]{1,0:T(8,128)(2,1)}) %all-gather.15.cloned.1.call-update) | async-done | bytes 1179664 | tf_op jit(solution)/shard_map/all_gather | solution.py:294
  135.7 52.6 %all-gather.17.cloned.1.call-done = bf16[3072,192]{1,0:T(8,128)(2,1)} async-done(((bf16[96,192]{1,0:T(8,128)(2,1)}), bf16[3072,192]{1,0:T(8,128)(2,1)}) %all-gather.17.cloned.1.call-update) | async-done | bytes 1179664 | tf_op jit(solution)/shard_map/all_gather | solution.py:294
  192.5 52.4 %all-gather.19.cloned.1.call-done = bf16[6144,96]{1,0:T(8,128)(2,1)} async-done(((bf16[192,96]{1,0:T(8,128)(2,1)}), bf16[6144,96]{1,0:T(8,128)(2,1)}) %all-gather.19.cloned.1.call-update) | async-done | bytes 1179664 | tf_op jit(solution)/shard_map/all_gather | solution.py:294
  255.9 8.3 add_convert_fusion.1
  264.1 9.3 copy.148
  273.5 8.2 convolution_convert_fusion
  281.6 9.1 copy.146
  290.7 48.6 %shard_map.314 = (f32[12,768,64]{2,1,0:T(8,128)}, f32[12,768,1]{2,1,0:T(8,128)}) custom-call(s32[3]{0:T(128)S(1)} %get-tuple-element.178.lo_ref, s32[3]{0:T(128)S(1)} %get-tuple-element.177.hi_ref, bf16[12,768,64]{2,1,0:T(8,128)(2,1)S(1)} %bitcast.184, bf16[12,2816,64]{2,1,0:T(8,128)(2,1)} %bitcast.190, bf16[12,2816,64]{2,1,0:T(8,128)(2,1)} %bitcast.187, ...), custom_call_target="tpu_custom_call" | custom-call | tf_op jit(solution)/shard_map/pallas_call | solution.py:137
  362.4 12.4 %all-gather.23.cloned.1.call-done = bf16[24576,96]{0,1:T(8,128)(2,1)} async-done(((bf16[768,96]{0,1:T(8,128)(2,1)}), bf16[24576,96]{0,1:T(8,128)(2,1)}) %all-gather.23.cloned.1.call-update) | async-done | bytes 4718608 | tf_op jit(solution)/shard_map/all_gather | solution.py:294
  390.9 28.3 %multiply_convert_fusion = (bf16[768,3072]{1,0:T(8,128)(2,1)S(1)}, f32[768,3072]{1,0:T(8,128)}, f32[768,3072]{1,0:T(8,128)}) fusion(f32[3072]{0:T(1024)S(1)} %convert_element_type.162, bf16[768,3072]{1,0:T(8,128)(2,1)S(1)} %bitcast.213, f32[768,768]{0,1:T(8,128)S(1)} %copy-done.2, f32[768]{0:T(1024)S(1)} %convert_element_type.160, ...), kind=kOutput, calls=%fused_computation.6 | convolution fusion | flops 3782541312 | bytes 30695424 | tf_op jit(solution)/shard_map/dot_general | solution.py:418
  428.9 15.7 %convert_reduce_fusion.1 = (f32[3072]{0:T(1024)}, bf16[768,3072]{1,0:T(8,128)(2,1)}) fusion(f32[768,3072]{1,0:T(8,128)} %get-tuple-element.136, f32[768,3072]{1,0:T(8,128)} %get-tuple-element.171, f32[3072]{0:T(1024)S(1)} %convert_element_type.162, bf16[768,768]{0,1:T(8,128)(2,1)S(1)} %get-tuple-element.126, bf16[3072,768]{0,1:T(8,128)(2,1)} %bitcast.216), kind=kOutput, calls=%fused_computation.4 | convolution fusion | flops 3663983616 | bytes 29515776 | tf_op jit(solution)/shard_map/dot_general | solution.py:268
  472.9 36.8 %shard_map.315 = f32[12,768,64]{2,1,0:T(8,128)} custom-call(s32[3]{0:T(128)S(1)} %get-tuple-element.178.lo_ref, s32[3]{0:T(128)S(1)} %get-tuple-element.177.hi_ref, bf16[12,768,64]{2,1,0:T(8,128)(2,1)S(1)} %bitcast.185, bf16[12,2816,64]{2,1,0:T(8,128)(2,1)} %bitcast.191, bf16[12,2816,64]{2,1,0:T(8,128)(2,1)} %bitcast.188, s32[768,1]{1,0:T(8,128)S(1)} %reshape.460.qs_ref, ...), custom_call_target="tpu_custom_call" | custom-call | tf_op jit(solution)/shard_map/pallas_call | solution.py:179
  537.6 56.0 %shard_map.316 = (f32[12,2816,64]{2,1,0:T(8,128)}, f32[12,2816,64]{2,1,0:T(8,128)}) custom-call(s32[11]{0:T(128)S(1)} %get-tuple-element.124.lo_ref, s32[11]{0:T(128)S(1)} %get-tuple-element.123.hi_ref, bf16[12,768,64]{2,1,0:T(8,128)(2,1)S(1)} %bitcast.186, bf16[12,2816,64]{2,1,0:T(8,128)(2,1)} %bitcast.192, bf16[12,2816,64]{2,1,0:T(8,128)(2,1)} %bitcast.189, ...), custom_call_target="tpu_custom_call" | custom-call | tf_op jit(solution)/shard_map/pallas_call | solution.py:218
  593.6 9.5 convert_bitcast_fusion.1
  603.1 9.5 copy.162
  612.6 9.8 fusion.49
  622.5 9.6 convert_reduce_fusion
  632.2 9.5 copy.163
  641.7 9.9 fusion.50
  653.3 9.0 fusion.33
  662.4 12.5 %reshape.384 = f32[8,96,4,768]{3,2,1,0:T(4,128)} reshape(f32[768,3072]{1,0:T(8,128)} %fusion.33) | data formatting | bytes 18874368 | tf_op jit(solution)/shard_map/reshape | solution.py:305
  674.9 9.1 copy.169
  684.1 10.3 fusion.51
  694.4 12.8 %reshape.387 = f32[4,768,8,96]{1,0,3,2:T(4,128)} reshape(f32[3072,768]{0,1:T(8,128)} %fusion.51) | data formatting | bytes 18874368 | tf_op jit(solution)/shard_map/reshape | solution.py:308
  707.2 9.1 copy.171
  731.5 11.4 collective-permute-start.6
  754.5 58.8 %all-reduce.2 = f32[32,288]{1,0:T(8,128)S(1)} all-reduce(f32[32,288]{1,0:T(8,128)S(1)} %concatenate.7), channel_id=14, replica_groups=mesh['dp'=8,'tensor'=4] {'dp','tensor'}, use_global_device_ids=true, to_apply=%region_29.31.clone | all-reduce | flops 9216 | bytes 73728
  825.1 58.6 %reduce-scatter.11.cloned.1.call-done = f32[1,96,192]{2,1,0:T(8,128)} async-done(((f32[32,96,192]{2,1,0:T(8,128)}), f32[1,96,192]{2,1,0:T(8,128)}) %reduce-scatter.11.cloned.1.call-update) | async-done | bytes 73744 | tf_op jit(solution)/shard_map/reduce_scatter | solution.py:310
  883.7 141.7 %reduce-scatter.15.cloned.1.call-done = f32[1,96,768]{2,1,0:T(8,128)} async-done(((f32[32,96,768]{2,1,0:T(8,128)}), f32[1,96,768]{2,1,0:T(8,128)}) %reduce-scatter.15.cloned.1.call-update) | async-done | bytes 294928 | tf_op jit(solution)/shard_map/reduce_scatter | solution.py:310
  1025.4 141.5 %reduce-scatter.17.cloned.1.call-done = f32[1,768,96]{1,2,0:T(8,128)} async-done(((f32[32,768,96]{1,2,0:T(8,128)}), f32[1,768,96]{1,2,0:T(8,128)}) %reduce-scatter.17.cloned.1.call-update) | async-done | bytes 294928 | tf_op jit(solution)/shard_map/reduce_scatter | solution.py:310
  (210 shorter events, 210.3 us)
Async XLA Ops:
  7.2 22.5 %copy-start.18 = (bf16[768]{0:T(1024)(128)(2,1)S(1)}, bf16[768]{0:T(1024)(128)(2,1)}, u32[]{:S(2)}) copy-start(bf16[768]{0:T(1024)(128)(2,1)} %param.35) | copy-start | bytes 4612
  7.3 22.5 %copy-start.21 = (bf16[768]{0:T(1024)(128)(2,1)S(1)}, bf16[768]{0:T(1024)(128)(2,1)}, u32[]{:S(2)}) copy-start(bf16[768]{0:T(1024)(128)(2,1)} %param.30) | copy-start | bytes 4612
  7.3 22.5 %copy-start.22 = (bf16[768]{0:T(1024)(128)(2,1)S(1)}, bf16[768]{0:T(1024)(128)(2,1)}, u32[]{:S(2)}) copy-start(bf16[768]{0:T(1024)(128)(2,1)} %param.31) | copy-start | bytes 4612
  7.3 22.5 %copy-start.23 = (bf16[768]{0:T(1024)(128)(2,1)S(1)}, bf16[768]{0:T(1024)(128)(2,1)}, u32[]{:S(2)}) copy-start(bf16[768]{0:T(1024)(128)(2,1)} %param.32) | copy-start | bytes 4612
  7.3 22.5 %copy-start.24 = (bf16[768]{0:T(1024)(128)(2,1)S(1)}, bf16[768]{0:T(1024)(128)(2,1)}, u32[]{:S(2)}) copy-start(bf16[768]{0:T(1024)(128)(2,1)} %param.34) | copy-start | bytes 4612
  7.3 22.5 %copy-start.25 = (bf16[768]{0:T(1024)(128)(2,1)S(1)}, bf16[768]{0:T(1024)(128)(2,1)}, u32[]{:S(2)}) copy-start(bf16[768]{0:T(1024)(128)(2,1)} %param.38) | copy-start | bytes 4612
  7.3 30.4 %copy-start.17 = (bf16[3072]{0:T(1024)(128)(2,1)S(1)}, bf16[3072]{0:T(1024)(128)(2,1)}, u32[]{:S(2)}) copy-start(bf16[3072]{0:T(1024)(128)(2,1)} %param.33) | copy-start | bytes 18436
  7.3 66.7 %all-gather.13.cloned.1.call-start = ((), (), s32[]{:S(2)}) async-start(), calls=%async_computation.12 | async-start | bytes 1622016 | tf_op jit(solution)/shard_map/all_gather | solution.py:294
  8.0 123.4 %all-gather.15.cloned.1.call-start = ((), (), s32[]{:S(2)}) async-start(), calls=%async_computation.13 | async-start | bytes 1622016 | tf_op jit(solution)/shard_map/all_gather | solution.py:294
  8.8 179.5 %all-gather.17.cloned.1.call-start = ((), (), s32[]{:S(2)}) async-start(), calls=%async_computation.14 | async-start | bytes 1622016 | tf_op jit(solution)/shard_map/all_gather | solution.py:294
  9.5 235.4 %all-gather.19.cloned.1.call-start = ((), (), s32[]{:S(2)}) async-start(), calls=%async_computation.15 | async-start | bytes 1622016 | tf_op jit(solution)/shard_map/all_gather | solution.py:294
  10.1 342.6 %all-gather.21.cloned.1.call-start = ((), (), s32[]{:S(2)}) async-start(), calls=%async_computation.16 | async-start | bytes 4866048 | tf_op jit(solution)/shard_map/all_gather | solution.py:294
  10.7 364.1 %all-gather.23.cloned.1.call-start = ((), (), s32[]{:S(2)}) async-start(), calls=%async_computation.17 | async-start | bytes 4866048 | tf_op jit(solution)/shard_map/all_gather | solution.py:294
  11.3 813.8 %reduce-scatter.13.cloned.1.call-start = ((), (), s32[]{:S(2)}) async-start(), calls=%async_computation.9 | async-start | bytes 3244032 | tf_op jit(solution)/shard_map/reduce_scatter | solution.py:310
  11.3 49.8 %collective-permute-start.2 = (bf16[768,768]{1,0:T(8,128)(2,1)}, bf16[768,768]{1,0:T(8,128)(2,1)}, u32[]{:S(2)}, u32[]{:S(2)}) collective-permute-start(bf16[768,768]{1,0:T(8,128)(2,1)} %param.21), channel_id=1, source_target_pairs={{1,0},{2,1},{3,2},{5,4},{6,5},{7,6},{9,8},{10,9},{11,10},{13,12},{... | collective-permute-start | bytes 3538952 | tf_op jit(solution)/shard_map/ppermute | solution.py:338
  12.6 45.0 %collective-permute-start.1 = (bf16[768,768]{1,0:T(8,128)(2,1)}, bf16[768,768]{1,0:T(8,128)(2,1)}, u32[]{:S(2)}, u32[]{:S(2)}) collective-permute-start(bf16[768,768]{1,0:T(8,128)(2,1)} %param.21), channel_id=1, source_target_pairs={{0,1},{1,2},{2,3},{4,5},{5,6},{6,7},{8,9},{9,10},{10,11},{12,13},{... | collective-permute-start | bytes 3538952 | tf_op jit(solution)/shard_map/ppermute | solution.py:338
  20.3 43.2 %collective-permute-start.3 = (bf16[256,768]{1,0:T(8,128)(2,1)}, bf16[256,768]{1,0:T(8,128)(2,1)S(1)}, u32[]{:S(2)}, u32[]{:S(2)}) collective-permute-start(bf16[256,768]{1,0:T(8,128)(2,1)} %get-tuple-element.149), channel_id=1, source_target_pairs={{2,0},{3,1},{6,4},{7,5},{10,8},{11,9},{14,12},{15,13},{18,16},{19,... | collective-permute-start | bytes 1179656 | tf_op jit(solution)/shard_map/ppermute | solution.py:338
  21.6 34.2 %collective-permute-start = (bf16[256,768]{1,0:T(8,128)(2,1)}, bf16[256,768]{1,0:T(8,128)(2,1)}, u32[]{:S(2)}, u32[]{:S(2)}) collective-permute-start(bf16[256,768]{1,0:T(8,128)(2,1)} %get-tuple-element.150), channel_id=1, source_target_pairs={{0,2},{1,3},{4,6},{5,7},{8,10},{9,11},{12,14},{13,15},{16,18},{17,... | collective-permute-start | bytes 1179656 | tf_op jit(solution)/shard_map/ppermute | solution.py:338
  387.2 32.0 %copy-start.7 = (bf16[96,8,4,768]{3,1,2,0:T(8,128)(2,1)}, bf16[96,8,4,768]{3,1,2,0:T(8,128)(2,1)S(1)}, u32[]{:S(2)}) copy-start(bf16[96,8,4,768]{3,1,2,0:T(8,128)(2,1)S(1)} %copy.181) | copy-start | bytes 14155780
  457.6 367.5 %reduce-scatter.7.cloned.1.call-start = ((), (), s32[]{:S(2)}) async-start(), calls=%async_computation.6 | async-start | bytes 3244032 | tf_op jit(solution)/shard_map/reduce_scatter | solution.py:310
  530.2 294.9 %reduce-scatter.9.cloned.1.call-start = ((), (), s32[]{:S(2)}) async-start(), calls=%async_computation.7 | async-start | bytes 3244032 | tf_op jit(solution)/shard_map/reduce_scatter | solution.py:310
  622.5 261.2 %reduce-scatter.11.cloned.1.call-start = ((), (), s32[]{:S(2)}) async-start(), calls=%async_computation.8 | async-start | bytes 3244032 | tf_op jit(solution)/shard_map/reduce_scatter | solution.py:310
  651.6 373.8 %reduce-scatter.15.cloned.1.call-start = ((), (), s32[]{:S(2)}) async-start(), calls=%async_computation.10 | async-start | bytes 9732096 | tf_op jit(solution)/shard_map/reduce_scatter | solution.py:310
  684.0 482.9 %reduce-scatter.17.cloned.1.call-start = ((), (), s32[]{:S(2)}) async-start(), calls=%async_computation.11 | async-start | bytes 9732096 | tf_op jit(solution)/shard_map/reduce_scatter | solution.py:310
  728.6 22.6 %copy-start.15 = (f32[768]{0:T(1024)S(1)}, f32[768]{0:T(1024)}, u32[]{:S(2)}) copy-start(f32[768]{0:T(1024)} %get-tuple-element.113) | copy-start | bytes 9220
  728.6 22.7 %copy-start.14 = (f32[768]{0:T(1024)S(1)}, f32[768]{0:T(1024)}, u32[]{:S(2)}) copy-start(f32[768]{0:T(1024)} %get-tuple-element.118) | copy-start | bytes 9220
  728.6 22.8 %copy-start.16 = (f32[3072]{0:T(1024)S(1)}, f32[3072]{0:T(1024)}, u32[]{:S(2)}) copy-start(f32[3072]{0:T(1024)} %get-tuple-element.127) | copy-start | bytes 36868
  728.6 22.9 %copy-start.13 = (f32[768]{0:T(1024)S(1)}, f32[768]{0:T(1024)}, u32[]{:S(2)}) copy-start(f32[768]{0:T(1024)} %get-tuple-element.125) | copy-start | bytes 9220
  730.2 84.3 %collective-permute-start.4 = (bf16[768,768]{0,1:T(8,128)(2,1)}, bf16[768,768]{0,1:T(8,128)(2,1)}, u32[]{:S(2)}, u32[]{:S(2)}) collective-permute-start(bf16[768,768]{0,1:T(8,128)(2,1)} %get-tuple-element.146), channel_id=1, source_target_pairs={{1,0},{2,1},{3,2},{5,4},{6,5},{7,6},{9,8},{10,9},{11,10},{13,12},{... | collective-permute-start | bytes 3538952 | tf_op jit(solution)/shard_map/ppermute | solution.py:338
  731.5 83.0 %collective-permute-start.6 = (bf16[768,768]{0,1:T(8,128)(2,1)}, bf16[768,768]{0,1:T(8,128)(2,1)}, u32[]{:S(2)}, u32[]{:S(2)}) collective-permute-start(bf16[768,768]{0,1:T(8,128)(2,1)} %get-tuple-element.147), channel_id=1, source_target_pairs={{0,1},{1,2},{2,3},{4,5},{5,6},{6,7},{8,9},{9,10},{10,11},{12,13},{... | collective-permute-start | bytes 3538952 | tf_op jit(solution)/shard_map/ppermute | solution.py:338
  742.9 71.5 %collective-permute-start.5 = (bf16[256,768]{0,1:T(8,128)(2,1)S(1)}, bf16[256,768]{0,1:T(8,128)(2,1)}, u32[]{:S(2)}, u32[]{:S(2)}) collective-permute-start(bf16[256,768]{0,1:T(8,128)(2,1)S(1)} %get-tuple-element.144), channel_id=1, source_target_pairs={{2,0},{3,1},{6,4},{7,5},{10,8},{11,9},{14,12},{15,13},{18,16},{19,... | collective-permute-start | bytes 1179656 | tf_op jit(solution)/shard_map/ppermute | solution.py:338
  744.2 70.2 %collective-permute-start.7 = (bf16[256,768]{0,1:T(8,128)(2,1)S(1)}, bf16[256,768]{0,1:T(8,128)(2,1)}, u32[]{:S(2)}, u32[]{:S(2)}) collective-permute-start(bf16[256,768]{0,1:T(8,128)(2,1)S(1)} %get-tuple-element.145), channel_id=1, source_target_pairs={{0,2},{1,3},{4,6},{5,7},{8,10},{9,11},{12,14},{13,15},{16,18},{17,... | collective-permute-start | bytes 1179656 | tf_op jit(solution)/shard_map/ppermute | solution.py:338
  (21 other events, 181.4 us)
Sparse Core Ops, SparseCore 0:
  11.0 62.9 all-gather.12
  76.9 54.5 all-gather.14
  134.4 53.8 all-gather.16
  191.0 53.8 all-gather.18
  247.6 62.4 all-gather.20
  312.9 61.8 all-gather.22
  457.7 100.2 reduce-scatter.12
  564.1 101.3 reduce-scatter.6
  671.4 101.7 reduce-scatter.8
  779.1 104.5 reduce-scatter.10
  890.2 135.2 reduce-scatter.14
  1031.7 135.1 reduce-scatter.16

commit v2 on v1

--- a/solution.py
+++ b/solution.py
@@ -287,33 +287,72 @@
     return (segment_ids, starts, ends)
 
 
-def gather_weight(w, rows_over_dp):
+def _block_layout(w, rows_over_dp, dp, tens):
+    if rows_over_dp:
+        r, c = w.shape[0] // dp, w.shape[1] // tens
+        return w.reshape(dp, r, tens, c).transpose(0, 2, 1, 3).reshape(dp * tens, r * c)
+    r, c = w.shape[0] // tens, w.shape[1] // dp
+    return w.reshape(tens, r, dp, c).transpose(2, 0, 1, 3).reshape(dp * tens, r * c)
+
+
+def gather_weights(shards_and_kinds):
     dp = lax.axis_size("dp")
     tens = lax.axis_size("tensor")
-    r, c = w.shape
-    full = lax.all_gather(w, ("dp", "tensor"), axis=0, tiled=False).reshape(dp, tens, r, c)
-    if rows_over_dp:
-        return full.transpose(0, 2, 1, 3).reshape(dp * r, tens * c)
-    return full.transpose(1, 2, 0, 3).reshape(tens * r, dp * c)
-
-
-def scatter_grad(g, rows_over_dp):
+    flat = jnp.concatenate([w.reshape(-1) for w, _ in shards_and_kinds])
+    full = lax.all_gather(flat, ("dp", "tensor"), axis=0, tiled=False)
+    out, at = [], 0
+    for w, rows_over_dp in shards_and_kinds:
+        r, c = w.shape
+        part = full[:, at:at + r * c].reshape(dp, tens, r, c)
+        at += r * c
+        if rows_over_dp:
+            out.append(part.transpose(0, 2, 1, 3).reshape(dp * r, tens * c))
+        else:
+            out.append(part.transpose(1, 2, 0, 3).reshape(tens * r, dp * c))
+    return out
+
+
+def pack_grads(grads_and_kinds, extra=()):
     dp = lax.axis_size("dp")
     tens = lax.axis_size("tensor")
-    if rows_over_dp:
-        r, c = g.shape[0] // dp, g.shape[1] // tens
-        blocks = g.reshape(dp, r, tens, c).transpose(0, 2, 1, 3)
-    else:
-        r, c = g.shape[0] // tens, g.shape[1] // dp
-        blocks = g.reshape(tens, r, dp, c).transpose(2, 0, 1, 3)
-    blocks = blocks.reshape(dp * tens, r, c)
-    return lax.psum_scatter(blocks, ("dp", "tensor"), scatter_dimension=0, tiled=True).reshape(r, c)
+    parts = dp * tens
+    blocks = [_block_layout(g.astype(jnp.bfloat16), k, dp, tens) for g, k in grads_and_kinds]
+    blocks += [v.astype(jnp.bfloat16).reshape(parts, -1) for v in extra]
+    joined = jnp.concatenate(blocks, axis=1)
+    width = joined.shape[1]
+    padded = -(-width // 1024) * 1024
+    return jnp.pad(joined, ((0, 0), (0, padded - width))).reshape(parts, padded // 128, 128)
+
+
+def unpack_grads(joined, grads_and_kinds, extra=()):
+    dp = lax.axis_size("dp")
+    tens = lax.axis_size("tensor")
+    parts = dp * tens
+    summed = lax.psum_scatter(joined, ("dp", "tensor"), scatter_dimension=0, tiled=True)
+    summed = summed.reshape(-1).astype(jnp.float32)
+    out, at = [], 0
+    for g, k in grads_and_kinds:
+        if k:
+            r, c = g.shape[0] // dp, g.shape[1] // tens
+        else:
+            r, c = g.shape[0] // tens, g.shape[1] // dp
+        out.append(summed[at:at + r * c].reshape(r, c))
+        at += r * c
+    for v in extra:
+        n = v.shape[0] // parts
+        out.append(summed[at:at + n])
+        at += n
+    return out
 
 
 def scatter_vectors(vectors):
     parts = lax.axis_size("dp") * lax.axis_size("tensor")
     joined = jnp.concatenate([v.reshape(parts, -1) for v in vectors], axis=1)
-    summed = lax.psum_scatter(joined, ("dp", "tensor"), scatter_dimension=0, tiled=True)[0]
+    width = joined.shape[1]
+    padded = -(-width // 1024) * 1024
+    joined = jnp.pad(joined, ((0, 0), (0, padded - width))).reshape(parts, padded // 128, 128)
+    summed = lax.psum_scatter(joined, ("dp", "tensor"), scatter_dimension=0, tiled=True)
+    summed = summed.reshape(padded)[:width]
     out, at = [], 0
     for v in vectors:
         n = v.shape[0] // parts
@@ -395,12 +434,8 @@
     kv_steps = min(nkb, (BLOCK + 2 * (LONGEST - 1)) // BLOCK + 2)
     q_steps = rows // BLOCK
 
-    wq = gather_weight(w_query, True)
-    wk = gather_weight(w_key, True)
-    wv = gather_weight(w_value, True)
-    wo = gather_weight(w_out, False)
-    wi = gather_weight(w_inner, True)
-    wf = gather_weight(w_outer, False)
+    wq, wk, wv = gather_weights([(w_query, True), (w_key, True), (w_value, True)])
+    wo, wi, wf = gather_weights([(w_out, False), (w_inner, True), (w_outer, False)])
     gain_one = gain_attn.astype(jnp.float32)
     gain_two = gain_ffn.astype(jnp.float32)
 
@@ -433,6 +468,20 @@
     grad_attn = grad_resid_one.astype(jnp.bfloat16)
     grad_out_w = contract_first(context, grad_attn)
     grad_context = contract_last(grad_attn, wo).astype(jnp.bfloat16)
+    late = [
+        column_sum(grad_attn),
+        column_sum(grad_pre),
+        column_sum(grad_ffn),
+        jnp.sum(grad_hidden * norm_one, axis=0),
+        jnp.sum(grad_hidden, axis=0),
+        jnp.sum(grad_y * norm_two, axis=0),
+        jnp.sum(grad_y, axis=0),
+    ]
+    early_kinds = [(grad_out_w, False), (grad_inner_w, True), (grad_outer_w, False)]
+    early = pack_grads(early_kinds)
+    grad_context, early, late = lax.optimization_barrier((grad_context, early, late))
+    late = scatter_vectors(late)
+    g_out, g_inner, g_outer = unpack_grads(early, early_kinds)
     do_h = to_heads(grad_context)
     delta = jnp.sum(do_h.astype(jnp.float32) * ctx_h, axis=-1, keepdims=True)
     dq_h = flash_dq(q_h, k_h, v_h, q_ids, k_ids, lse, delta, do_h, lo, hi, BLOCK, BLOCK, kv_steps)
@@ -446,25 +495,11 @@
     grad_win = contract_last(grad_key, wk) + contract_last(grad_value, wv)
     grad_tokens = grad_resid_one + contract_last(grad_query, wq) + return_window(grad_win, takes, count)
 
-    summed = (
-        scatter_grad(grad_query_w, True),
-        scatter_grad(grad_key_w, True),
-        scatter_grad(grad_value_w, True),
-        scatter_grad(grad_out_w, False),
-        scatter_grad(grad_inner_w, True),
-        scatter_grad(grad_outer_w, False),
-    )
-    small = scatter_vectors([
-        column_sum(grad_query),
-        column_sum(grad_value),
-        column_sum(grad_attn),
-        column_sum(grad_pre),
-        column_sum(grad_ffn),
-        jnp.sum(grad_hidden * norm_one, axis=0),
-        jnp.sum(grad_hidden, axis=0),
-        jnp.sum(grad_y * norm_two, axis=0),
-        jnp.sum(grad_y, axis=0),
-    ])
+    late_kinds = [(grad_query_w, True), (grad_key_w, True), (grad_value_w, True)]
+    extra = (column_sum(grad_query), column_sum(grad_value))
+    g_query, g_key, g_value, g_bq, g_bv = unpack_grads(pack_grads(late_kinds, extra), late_kinds, extra)
+    summed = (g_query, g_key, g_value, g_out, g_inner, g_outer)
+    small = [g_bq, g_bv] + late
     return (output.astype(jnp.bfloat16), grad_tokens) + summed + tuple(small)
 
 

time: 1190 us -> 1010 us (0.85)
  waiting for transfers between devices: 526 us -> 287 us
  local copies, waits for them, and re-layouts: 203 us -> 322 us
  blocking collectives: 58.8 us -> 0 us
  starting transfers between devices: 35.8 us -> 73 us
  matrix products: 147 us -> 124 us
  Pallas kernels: 141 us -> 122 us
    reduce_scatter x6 -> x1, waiting for transfers between devices: 342 us -> 145 us  [unpack_grads(): lax.psum_scatter(joined, ('dp', 'tensor'), scatter_dimension=0, tiled=True)]
    all_gather x6 -> x2, waiting for transfers between devices: 180 us -> 0.01 us  [gather_weights(): full = lax.all_gather(flat, ('dp', 'tensor'), axis=0, tiled=False)]
    unnamed x12 -> x7, waiting for transfers between devices: 3.73 us -> 98.1 us
    unnamed x1 -> x0, blocking collectives: 58.8 us -> none
    reshape x14 -> x39, local copies, waits for them, and re-layouts: 64.7 us -> 122 us  [the longest x11 37.6 us: _block_layout(): w.reshape(dp, r, tens, c).transpose(0, 2, 1, 3).reshape(dp * tens, r * c)]
    ppermute x8, waiting for transfers between devices: 0.02 us -> 43.3 us  [shift_rows(): return lax.ppermute(values, 'tensor', pairs)]
    ppermute x8, starting transfers between devices: 35.4 us -> 72.8 us  [shift_rows(): return lax.ppermute(values, 'tensor', pairs)]
    all_gather x0 -> x2, local copies, waits for them, and re-layouts: none -> 24.6 us  [gather_weights(): full = lax.all_gather(flat, ('dp', 'tensor'), axis=0, tiled=False)]
  transfers between devices with their start and end apart: 20 -> 13, of which waited for: 8 -> 5; matrix products, arithmetic and copies ran while one was open for 26% -> 26% of each run, Pallas kernels for 12% -> 12%
where the time goes in v2:
time: 1010 us; the launch traced here: 999 us
  local copies, waits for them, and re-layouts  322 us (32%)
  waiting for transfers between devices  287 us (28%)
  matrix products  124 us (12%)
  Pallas kernels  122 us (12%)
  starting transfers between devices  73 us (7%)
  other arithmetic  57 us (6%)
  between operations  15.1 us (1%)
    reduce_scatter x1, waiting for transfers between devices, unpack_grads(): lax.psum_scatter(joined, ('dp', 'tensor'), scatter_dimension=0, tiled=True)  145 us
    unnamed x7, waiting for transfers between devices  98.1 us
    ppermute x8, starting transfers between devices, shift_rows(): return lax.ppermute(values, 'tensor', pairs)  72.8 us
    pallas_call x1, Pallas kernels, flash_dkv(): pl.pallas_call(_dkv_kernel, grid_spec=grid_spec, out_shape=[jax.ShapeDtyp...  54.6 us
    unnamed x93, local copies, waits for them, and re-layouts  44.6 us
    ppermute x8, waiting for transfers between devices, shift_rows(): return lax.ppermute(values, 'tensor', pairs)  43.3 us
    dot_general x6, matrix products, contract_last(): lax.dot_general(left, right, (((1,), (1,)), ((), ())), preferred_element_...  39.9 us
    reshape x11, local copies, waits for them, and re-layouts, _block_layout(): w.reshape(dp, r, tens, c).transpose(0, 2, 1, 3).reshape(dp * tens, r * c)  37.6 us
  transfers between devices with their start and end apart: 13, of which 5 were waited for; matrix products, arithmetic and copies ran while one was open for 26% of the time, Pallas kernels for 12%

profile of v2, /device:TPU:4, one launch (start us, length us, event | category | flops | bytes accessed | tf_op | source)
XLA Modules:
  0.0 999.0 jit_solution(14189878261272840201)
XLA Ops:
  42.1 14.9 %gather_fusion = s32[2816]{0:T(1024)S(1)} fusion(s32[3072]{0:T(1024)S(1)} %convert_reduce_fusion.4, s32[3072]{0:T(1024)S(1)} %pad_clamp_fusion), kind=kCustom, calls=%fused_computation | custom fusion | bytes 33792 | tf_op jit(solution)/shard_map/jit(_take)/gather | solution.py:428
  58.7 6.7 collective-permute-done
  118.8 8.1 add_convert_fusion.1
  126.9 9.2 copy.162
  136.1 8.1 convolution_convert_fusion.2
  144.2 9.1 copy.160
  153.3 37.2 %shard_map.314 = (f32[12,768,64]{2,1,0:T(8,128)}, f32[12,768,1]{2,1,0:T(8,128)}) custom-call(s32[3]{0:T(128)S(1)} %get-tuple-element.204.lo_ref, s32[3]{0:T(128)S(1)} %get-tuple-element.203.hi_ref, bf16[12,768,64]{2,1,0:T(8,128)(2,1)S(1)} %bitcast.148, bf16[12,2816,64]{2,1,0:T(8,128)(2,1)} %bitcast.154, bf16[12,2816,64]{2,1,0:T(8,128)(2,1)} %bitcast.151, ...), custom_call_target="tpu_custom_call" | custom-call | tf_op jit(solution)/shard_map/pallas_call | solution.py:137
  198.5 19.6 %reshape.479 = bf16[32,165888]{1,0:T(8,128)(2,1)} reshape(bf16[5308416]{0:T(1024)(128)(2,1)} %all-gather.7.cloned.1.call-done) | data formatting | bytes 21233664 | tf_op jit(solution)/shard_map/all_gather | solution.py:302
  246.0 8.8 reshape.414
  254.8 10.2 %copy.168 = bf16[4,768,8,96]{1,0,3,2:T(4,128)(2,1)} copy(bf16[4,768,8,96]{3,1,0,2:T(8,128)(2,1)} %bitcast.160) | data formatting | bytes 9437184 | tf_op jit(solution)/shard_map/transpose | solution.py:311
  270.9 28.5 %multiply_convert_fusion = (bf16[768,3072]{1,0:T(8,128)(2,1)S(1)}, f32[768,3072]{1,0:T(8,128)}, f32[768,3072]{1,0:T(8,128)}) fusion(f32[3072]{0:T(1024)S(1)} %convert_element_type.201, bf16[768,3072]{1,0:T(8,128)(2,1)S(1)} %bitcast.186, f32[768,768]{0,1:T(8,128)S(1)} %get-tuple-element.196, f32[768]{0:T(1024)S(1)} %convert_element_type.199, ...), kind=kOutput, calls=%fused_computation.6 | convolution fusion | flops 3782541312 | bytes 30695424 | tf_op jit(solution)/shard_map/dot_general | solution.py:453
  313.7 13.4 %convert_reduce_fusion = (f32[3072]{0:T(1024)S(1)}, bf16[768,3072]{1,0:T(8,128)(2,1)}) fusion(f32[768,3072]{1,0:T(8,128)} %get-tuple-element.154, f32[768,3072]{1,0:T(8,128)} %get-tuple-element.197, f32[3072]{0:T(1024)S(1)} %convert_element_type.201, bf16[768,768]{0,1:T(8,128)(2,1)} %copy-done.11, bf16[3072,768]{0,1:T(8,128)(2,1)S(1)} %bitcast.189), kind=kOutput, calls=%fused_computation.4 | convolution fusion | flops 3663983616 | bytes 29515776 | tf_op jit(solution)/shard_map/dot_general | solution.py:268
  327.1 7.6 multiply_reduce_fusion.1
  345.9 6.7 copy.174
  352.5 9.8 reshape.420
  362.3 10.1 %reshape.418 = bf16[8,96,4,768]{3,2,1,0:T(4,128)(2,1)} reshape(bf16[768,3072]{1,0:T(8,128)(2,1)} %convolution_convert_fusion.1) | data formatting | bytes 9437184 | tf_op jit(solution)/shard_map/reshape | solution.py:293
  391.6 10.1 %copy.175 = bf16[8,4,768,96]{3,2,1,0:T(8,128)(2,1)} copy(bf16[8,4,768,96]{2,1,3,0:T(4,128)(2,1)} %bitcast.168) | data formatting | bytes 9437184 | tf_op jit(solution)/shard_map/transpose | solution.py:295
  401.7 11.6 %reshape.421 = bf16[32,73728]{1,0:T(8,128)(2,1)} reshape(bf16[8,4,768,96]{3,2,1,0:T(8,128)(2,1)} %copy.175) | data formatting | bytes 9437184 | tf_op jit(solution)/shard_map/reshape | solution.py:295
  413.3 8.8 maximum_bitcast_fusion
  442.2 29.9 %shard_map.315 = f32[12,768,64]{2,1,0:T(8,128)} custom-call(s32[3]{0:T(128)S(1)} %get-tuple-element.204.lo_ref, s32[3]{0:T(128)S(1)} %get-tuple-element.203.hi_ref, bf16[12,768,64]{2,1,0:T(8,128)(2,1)S(1)} %bitcast.149, bf16[12,2816,64]{2,1,0:T(8,128)(2,1)} %bitcast.155, bf16[12,2816,64]{2,1,0:T(8,128)(2,1)} %bitcast.152, s32[768,1]{1,0:T(8,128)S(1)} %reshape.492.qs_ref, ...), custom_call_target="tpu_custom_call" | custom-call | tf_op jit(solution)/shard_map/pallas_call | solution.py:179
  497.3 54.6 %shard_map.316 = (f32[12,2816,64]{2,1,0:T(8,128)}, f32[12,2816,64]{2,1,0:T(8,128)}) custom-call(s32[11]{0:T(128)S(1)} %get-tuple-element.142.lo_ref, s32[11]{0:T(128)S(1)} %get-tuple-element.141.hi_ref, bf16[12,768,64]{2,1,0:T(8,128)(2,1)S(1)} %bitcast.150, bf16[12,2816,64]{2,1,0:T(8,128)(2,1)} %bitcast.156, bf16[12,2816,64]{2,1,0:T(8,128)(2,1)} %bitcast.153, ...), custom_call_target="tpu_custom_call" | custom-call | tf_op jit(solution)/shard_map/pallas_call | solution.py:218
  551.9 9.2 convert_bitcast_fusion.1
  561.0 9.8 copy.184
  570.8 7.1 convolution_convert_fusion.4
  582.1 9.5 fusion.38
  592.3 9.5 copy.185
  601.8 7.1 convolution_convert_fusion.3
  639.9 16.7 %collective-permute-start.6 = (bf16[768,768]{0,1:T(8,128)(2,1)}, bf16[768,768]{0,1:T(8,128)(2,1)}, u32[]{:S(2)}, u32[]{:S(2)}) collective-permute-start(bf16[768,768]{0,1:T(8,128)(2,1)} %get-tuple-element.167), channel_id=1, source_target_pairs={{0,1},{1,2},{2,3},{4,5},{5,6},{6,7},{8,9},{9,10},{10,11},{12,13},{... | collective-permute-start | bytes 3538952 | tf_op jit(solution)/shard_map/ppermute | solution.py:377
  658.8 39.1 %collective-permute-start.7 = (bf16[256,768]{0,1:T(8,128)(2,1)}, bf16[256,768]{0,1:T(8,128)(2,1)}, u32[]{:S(2)}, u32[]{:S(2)}) collective-permute-start(bf16[256,768]{0,1:T(8,128)(2,1)} %get-tuple-element.165), channel_id=1, source_target_pairs={{0,2},{1,3},{4,6},{5,7},{8,10},{9,11},{12,14},{13,15},{16,18},{17,... | collective-permute-start | bytes 1179656 | tf_op jit(solution)/shard_map/ppermute | solution.py:377
  701.2 30.6 %collective-permute-done.5 = bf16[256,768]{0,1:T(8,128)(2,1)} collective-permute-done((bf16[256,768]{0,1:T(8,128)(2,1)}, bf16[256,768]{0,1:T(8,128)(2,1)}, u32[]{:S(2)}, u32[]{:S(2)}) %collective-permute-start.5) | collective-permute-done | bytes 393248 | tf_op jit(solution)/shard_map/ppermute | solution.py:377
  739.7 97.5 %reduce-scatter.8.cloned.1.call-done = bf16[1,440,128]{2,1,0:T(8,128)(2,1)} async-done(((bf16[32,440,128]{2,1,0:T(8,128)(2,1)}), bf16[1,440,128]{2,1,0:T(8,128)(2,1)}) %reduce-scatter.8.cloned.1.call-update) | async-done | bytes 112656
  841.7 145.2 %reduce-scatter.6.cloned.1.call-done = bf16[1,1296,128]{2,1,0:T(8,128)(2,1)} async-done(((bf16[32,1296,128]{2,1,0:T(8,128)(2,1)}), bf16[1,1296,128]{2,1,0:T(8,128)(2,1)}) %reduce-scatter.6.cloned.1.call-update) | async-done | bytes 331792 | tf_op jit(solution)/shard_map/reduce_scatter | solution.py:331
  (249 shorter events, 279.8 us)
Async XLA Ops:
  7.2 7.9 copy-start.2
  7.2 23.2 %copy-start.28 = (s32[40]{0:T(128)S(1)}, s32[40]{0:T(128)}, u32[]{:S(2)}) copy-start(s32[40]{0:T(128)} %param.23) | copy-start | bytes 484
  7.2 23.3 %copy-start.29 = (s32[40]{0:T(128)S(1)}, s32[40]{0:T(128)}, u32[]{:S(2)}) copy-start(s32[40]{0:T(128)} %param.22) | copy-start | bytes 484
  7.2 72.7 %all-gather.5.cloned.1.call-start = ((), (), s32[]{:S(2)}) async-start(), calls=%async_computation.3 | async-start | bytes 3649536 | tf_op jit(solution)/shard_map/all_gather | solution.py:302
  10.8 187.7 %all-gather.7.cloned.1.call-start = ((), (), s32[]{:S(2)}) async-start(), calls=%async_computation.4 | async-start | bytes 10948608 | tf_op jit(solution)/shard_map/all_gather | solution.py:302
  14.9 25.3 %copy-start.20 = (bf16[768]{0:T(1024)(128)(2,1)S(1)}, bf16[768]{0:T(1024)(128)(2,1)}, u32[]{:S(2)}) copy-start(bf16[768]{0:T(1024)(128)(2,1)} %param.35) | copy-start | bytes 4612
  14.9 25.3 %copy-start.21 = (bf16[768]{0:T(1024)(128)(2,1)S(1)}, bf16[768]{0:T(1024)(128)(2,1)}, u32[]{:S(2)}) copy-start(bf16[768]{0:T(1024)(128)(2,1)} %param.36) | copy-start | bytes 4612
  14.9 25.3 %copy-start.22 = (bf16[768]{0:T(1024)(128)(2,1)S(1)}, bf16[768]{0:T(1024)(128)(2,1)}, u32[]{:S(2)}) copy-start(bf16[768]{0:T(1024)(128)(2,1)} %param.37) | copy-start | bytes 4612
  14.9 25.9 %copy-start.23 = (bf16[768]{0:T(1024)(128)(2,1)S(1)}, bf16[768]{0:T(1024)(128)(2,1)}, u32[]{:S(2)}) copy-start(bf16[768]{0:T(1024)(128)(2,1)} %param.30) | copy-start | bytes 4612
  14.9 25.9 %copy-start.24 = (bf16[768]{0:T(1024)(128)(2,1)S(1)}, bf16[768]{0:T(1024)(128)(2,1)}, u32[]{:S(2)}) copy-start(bf16[768]{0:T(1024)(128)(2,1)} %param.31) | copy-start | bytes 4612
  15.0 25.9 %copy-start.25 = (bf16[768]{0:T(1024)(128)(2,1)S(1)}, bf16[768]{0:T(1024)(128)(2,1)}, u32[]{:S(2)}) copy-start(bf16[768]{0:T(1024)(128)(2,1)} %param.32) | copy-start | bytes 4612
  15.0 25.9 %copy-start.26 = (bf16[768]{0:T(1024)(128)(2,1)S(1)}, bf16[768]{0:T(1024)(128)(2,1)}, u32[]{:S(2)}) copy-start(bf16[768]{0:T(1024)(128)(2,1)} %param.34) | copy-start | bytes 4612
  15.0 25.9 %copy-start.27 = (bf16[768]{0:T(1024)(128)(2,1)S(1)}, bf16[768]{0:T(1024)(128)(2,1)}, u32[]{:S(2)}) copy-start(bf16[768]{0:T(1024)(128)(2,1)} %param.38) | copy-start | bytes 4612
  15.0 26.5 %copy-start.19 = (bf16[3072]{0:T(1024)(128)(2,1)S(1)}, bf16[3072]{0:T(1024)(128)(2,1)}, u32[]{:S(2)}) copy-start(bf16[3072]{0:T(1024)(128)(2,1)} %param.33) | copy-start | bytes 18436
  15.0 684.3 %all-reduce.8.cloned.1.call-start = ((), (), s32[]{:S(2)}) async-start(), calls=%async_computation.5 | async-start | bytes 262144
  15.1 55.6 %collective-permute-start.2 = (bf16[768,768]{1,0:T(8,128)(2,1)S(1)}, bf16[768,768]{1,0:T(8,128)(2,1)}, u32[]{:S(2)}, u32[]{:S(2)}) collective-permute-start(bf16[768,768]{1,0:T(8,128)(2,1)S(1)} %copy-done.2), channel_id=1, source_target_pairs={{1,0},{2,1},{3,2},{5,4},{6,5},{7,6},{9,8},{10,9},{11,10},{13,12},{... | collective-permute-start | bytes 3538952 | tf_op jit(solution)/shard_map/ppermute | solution.py:377
  16.4 50.8 %collective-permute-start.1 = (bf16[768,768]{1,0:T(8,128)(2,1)S(1)}, bf16[768,768]{1,0:T(8,128)(2,1)}, u32[]{:S(2)}, u32[]{:S(2)}) collective-permute-start(bf16[768,768]{1,0:T(8,128)(2,1)S(1)} %copy-done.2), channel_id=1, source_target_pairs={{0,1},{1,2},{2,3},{4,5},{5,6},{6,7},{8,9},{9,10},{10,11},{12,13},{... | collective-permute-start | bytes 3538952 | tf_op jit(solution)/shard_map/ppermute | solution.py:377
  22.9 56.2 %collective-permute-start.3 = (bf16[256,768]{1,0:T(8,128)(2,1)}, bf16[256,768]{1,0:T(8,128)(2,1)S(1)}, u32[]{:S(2)}, u32[]{:S(2)}) collective-permute-start(bf16[256,768]{1,0:T(8,128)(2,1)} %get-tuple-element.172), channel_id=1, source_target_pairs={{2,0},{3,1},{6,4},{7,5},{10,8},{11,9},{14,12},{15,13},{18,16},{19,... | collective-permute-start | bytes 1179656 | tf_op jit(solution)/shard_map/ppermute | solution.py:377
  24.2 41.2 %collective-permute-start = (bf16[256,768]{1,0:T(8,128)(2,1)}, bf16[256,768]{1,0:T(8,128)(2,1)}, u32[]{:S(2)}, u32[]{:S(2)}) collective-permute-start(bf16[256,768]{1,0:T(8,128)(2,1)} %get-tuple-element.173), channel_id=1, source_target_pairs={{0,2},{1,3},{4,6},{5,7},{8,10},{9,11},{12,14},{13,15},{16,18},{17,... | collective-permute-start | bytes 1179656 | tf_op jit(solution)/shard_map/ppermute | solution.py:377
  42.1 15.1 %copy-start.12 = (bf16[768,768]{1,0:T(8,128)(2,1)S(1)}, bf16[768,768]{1,0:T(8,128)(2,1)}, u32[]{:S(2)}) copy-start(bf16[768,768]{1,0:T(8,128)(2,1)} %param.39) | copy-start | bytes 3538948
  327.1 7.6 copy-start.30
  431.0 406.2 %reduce-scatter.8.cloned.1.call-start = ((), (), s32[]{:S(2)}) async-start(), calls=%async_computation.6 | async-start | bytes 3717120
  611.2 6.8 copy-start.3
  623.7 363.2 %reduce-scatter.6.cloned.1.call-start = ((), (), s32[]{:S(2)}) async-start(), calls=%async_computation.2 | async-start | bytes 10948608 | tf_op jit(solution)/shard_map/reduce_scatter | solution.py:331
  623.8 7.2 slice-start
  625.0 6.0 copy-start.6
  636.8 61.1 %copy-start.7 = (bf16[768,768]{0,1:T(8,128)(2,1)S(1)}, bf16[768,768]{0,1:T(8,128)(2,1)}, u32[]{:S(2)}) copy-start(bf16[768,768]{0,1:T(8,128)(2,1)} %get-tuple-element.171) | copy-start | bytes 3538948
  638.4 94.4 %copy-start.4 = (bf16[768,12,64]{0,2,1:T(8,128)(2,1)S(1)}, bf16[768,12,64]{0,2,1:T(8,128)(2,1)}, u32[]{:S(2)}) copy-start(bf16[768,12,64]{0,2,1:T(8,128)(2,1)} %copy.180) | copy-start | bytes 3538948
  638.4 93.3 %collective-permute-start.4 = (bf16[768,768]{0,1:T(8,128)(2,1)}, bf16[768,768]{0,1:T(8,128)(2,1)S(1)}, u32[]{:S(2)}, u32[]{:S(2)}) collective-permute-start(bf16[768,768]{0,1:T(8,128)(2,1)} %get-tuple-element.166), channel_id=1, source_target_pairs={{1,0},{2,1},{3,2},{5,4},{6,5},{7,6},{9,8},{10,9},{11,10},{13,12},{... | collective-permute-start | bytes 3538952 | tf_op jit(solution)/shard_map/ppermute | solution.py:377
  639.9 91.9 %collective-permute-start.6 = (bf16[768,768]{0,1:T(8,128)(2,1)}, bf16[768,768]{0,1:T(8,128)(2,1)}, u32[]{:S(2)}, u32[]{:S(2)}) collective-permute-start(bf16[768,768]{0,1:T(8,128)(2,1)} %get-tuple-element.167), channel_id=1, source_target_pairs={{0,1},{1,2},{2,3},{4,5},{5,6},{6,7},{8,9},{9,10},{10,11},{12,13},{... | collective-permute-start | bytes 3538952 | tf_op jit(solution)/shard_map/ppermute | solution.py:377
  657.6 74.2 %collective-permute-start.5 = (bf16[256,768]{0,1:T(8,128)(2,1)}, bf16[256,768]{0,1:T(8,128)(2,1)}, u32[]{:S(2)}, u32[]{:S(2)}) collective-permute-start(bf16[256,768]{0,1:T(8,128)(2,1)} %get-tuple-element.164), channel_id=1, source_target_pairs={{2,0},{3,1},{6,4},{7,5},{10,8},{11,9},{14,12},{15,13},{18,16},{19,... | collective-permute-start | bytes 1179656 | tf_op jit(solution)/shard_map/ppermute | solution.py:377
  658.8 72.9 %collective-permute-start.7 = (bf16[256,768]{0,1:T(8,128)(2,1)}, bf16[256,768]{0,1:T(8,128)(2,1)}, u32[]{:S(2)}, u32[]{:S(2)}) collective-permute-start(bf16[256,768]{0,1:T(8,128)(2,1)} %get-tuple-element.165), channel_id=1, source_target_pairs={{0,2},{1,3},{4,6},{5,7},{8,10},{9,11},{12,14},{13,15},{16,18},{17,... | collective-permute-start | bytes 1179656 | tf_op jit(solution)/shard_map/ppermute | solution.py:377
  (16 other events, 41.9 us)
Sparse Core Ops, SparseCore 0:
  11.4 67.0 all-gather.4
  81.3 87.4 all-gather.6
  431.1 155.1 all-reduce.7
  623.8 213.3 reduce-scatter.7
  843.1 143.7 reduce-scatter.5

commit v3 on v2

--- a/solution.py
+++ b/solution.py
@@ -425,7 +425,7 @@
     base = rows * tens_index - LONGEST
     places = base + jnp.arange(window, dtype=jnp.int32)
     valid = (places >= 0) & (places < group_rows)
-    k_ids = jnp.where(valid, jnp.take(seg, jnp.clip(places, 0, group_rows - 1)), -1).astype(jnp.int32)
+    k_ids = jnp.where(valid, jnp.sum((places[:, None] >= ends[None, :]).astype(jnp.int32), axis=1), -1).astype(jnp.int32)
     q_ids = lax.dynamic_slice_in_dim(seg, rows * tens_index, rows)
     q_start = jnp.take(starts, q_ids) - base
     q_end = jnp.take(ends, q_ids) - base
@@ -478,14 +478,16 @@
         jnp.sum(grad_y, axis=0),
     ]
     early_kinds = [(grad_out_w, False), (grad_inner_w, True), (grad_outer_w, False)]
-    early = pack_grads(early_kinds)
-    grad_context, early, late = lax.optimization_barrier((grad_context, early, late))
-    late = scatter_vectors(late)
-    g_out, g_inner, g_outer = unpack_grads(early, early_kinds)
+    early = pack_grads(early_kinds, late)
+    grad_context, early = lax.optimization_barrier((grad_context, early))
+    early_sums = unpack_grads(early, early_kinds, late)
     do_h = to_heads(grad_context)
     delta = jnp.sum(do_h.astype(jnp.float32) * ctx_h, axis=-1, keepdims=True)
     dq_h = flash_dq(q_h, k_h, v_h, q_ids, k_ids, lse, delta, do_h, lo, hi, BLOCK, BLOCK, kv_steps)
     dk_h, dv_h = flash_dkv(q_h, k_h, v_h, q_ids, k_ids, lse, delta, do_h, qlo, qhi, BLOCK, BLOCK, q_steps)
+    early_sums, dq_h, dk_h, dv_h = lax.optimization_barrier((early_sums, dq_h, dk_h, dv_h))
+    g_out, g_inner, g_outer = early_sums[:3]
+    late = early_sums[3:]
     grad_query = from_heads(dq_h).astype(jnp.bfloat16)
     grad_key = from_heads(dk_h).astype(jnp.bfloat16)
     grad_value = from_heads(dv_h).astype(jnp.bfloat16)

time: 1010 us -> 1010 us (level)
  starting transfers between devices: 73 us -> 23.3 us
  waiting for transfers between devices: 287 us -> 321 us
  local copies, waits for them, and re-layouts: 322 us -> 336 us
    reduce_scatter x1 -> x0, waiting for transfers between devices: 145 us -> none  [unpack_grads(): lax.psum_scatter(joined, ('dp', 'tensor'), scatter_dimension=0, tiled=True)]
    unnamed x7 -> x6, waiting for transfers between devices: 98.1 us -> 225 us
    ppermute x8, waiting for transfers between devices: 43.3 us -> 94.4 us  [shift_rows(): return lax.ppermute(values, 'tensor', pairs)]
    ppermute x8, starting transfers between devices: 72.8 us -> 23.2 us  [shift_rows(): return lax.ppermute(values, 'tensor', pairs)]
    unnamed x93 -> x111, local copies, waits for them, and re-layouts: 44.6 us -> 72.8 us
    gather x1 -> x0, local copies, waits for them, and re-layouts: 14.9 us -> none  [shards(): jnp.take(seg, jnp.clip(places, 0, group_rows - 1))]
  transfers between devices with their start and end apart: 13 -> 12, of which waited for: 5 -> 7; matrix products, arithmetic and copies ran while one was open for 26% -> 16% of each run, Pallas kernels for 12% -> 12%
where the time goes in v3:
time: 1010 us; the launch traced here: 996 us
  local copies, waits for them, and re-layouts  336 us (33%)
  waiting for transfers between devices  321 us (32%)
  matrix products  130 us (13%)
  Pallas kernels  122 us (12%)
  other arithmetic  48.9 us (5%)
  starting transfers between devices  23.3 us (2%)
  between operations  15 us (1%)
    unnamed x6, waiting for transfers between devices  225 us
    ppermute x8, waiting for transfers between devices, shift_rows(): return lax.ppermute(values, 'tensor', pairs)  94.4 us
    unnamed x111, local copies, waits for them, and re-layouts  72.8 us
    pallas_call x1, Pallas kernels, flash_dkv(): pl.pallas_call(_dkv_kernel, grid_spec=grid_spec, out_shape=[jax.ShapeDtyp...  54.6 us
    reshape x11, local copies, waits for them, and re-layouts, _block_layout(): w.reshape(dp, r, tens, c).transpose(0, 2, 1, 3).reshape(dp * tens, r * c)  42.4 us
    dot_general x6, matrix products, contract_last(): lax.dot_general(left, right, (((1,), (1,)), ((), ())), preferred_element_...  40.5 us
    pallas_call x1, Pallas kernels, flash_forward(): pl.pallas_call(_fwd_kernel, grid_spec=grid_spec, out_shape=[jax.ShapeDtyp...  37.2 us
    dot_general x6, matrix products, contract_first(): lax.dot_general(left, right, (((0,), (0,)), ((), ())), preferred_element_...  33.3 us
  transfers between devices with their start and end apart: 12, of which 7 were waited for; matrix products, arithmetic and copies ran while one was open for 16% of the time, Pallas kernels for 12%

profile of v3, /device:TPU:4, one launch (start us, length us, event | category | flops | bytes accessed | tf_op | source)
XLA Modules:
  0.0 995.7 jit_solution(6888828650442316148)
XLA Ops:
  44.8 18.5 %collective-permute-done = bf16[256,768]{1,0:T(8,128)(2,1)} collective-permute-done((bf16[256,768]{1,0:T(8,128)(2,1)}, bf16[256,768]{1,0:T(8,128)(2,1)}, u32[]{:S(2)}, u32[]{:S(2)}) %collective-permute-start) | collective-permute-done | bytes 393248 | tf_op jit(solution)/shard_map/ppermute | solution.py:377
  71.0 11.6 %collective-permute-done.3 = bf16[256,768]{1,0:T(8,128)(2,1)S(1)} collective-permute-done((bf16[256,768]{1,0:T(8,128)(2,1)}, bf16[256,768]{1,0:T(8,128)(2,1)S(1)}, u32[]{:S(2)}, u32[]{:S(2)}) %collective-permute-start.3) | collective-permute-done | bytes 393248 | tf_op jit(solution)/shard_map/ppermute | solution.py:377
  116.9 8.1 convolution_convert_fusion.2
  125.0 9.1 copy.160
  145.1 8.1 add_convert_fusion.1
  153.2 9.1 copy.162
  162.4 37.2 %shard_map.314 = (f32[12,768,64]{2,1,0:T(8,128)}, f32[12,768,1]{2,1,0:T(8,128)}) custom-call(s32[3]{0:T(128)S(1)} %get-tuple-element.217.lo_ref, s32[3]{0:T(128)S(1)} %get-tuple-element.216.hi_ref, bf16[12,768,64]{2,1,0:T(8,128)(2,1)S(1)} %bitcast.145, bf16[12,2816,64]{2,1,0:T(8,128)(2,1)} %bitcast.148, bf16[12,2816,64]{2,1,0:T(8,128)(2,1)} %bitcast.151, ...), custom_call_target="tpu_custom_call" | custom-call | tf_op jit(solution)/shard_map/pallas_call | solution.py:137
  207.5 10.4 %reshape.419 = bf16[32,165888]{1,0:T(8,128)(2,1)} reshape(bf16[5308416]{0:T(1024)(128)(2,1)} %all-gather.7.cloned.1.call-done) | data formatting | bytes 21233664 | tf_op jit(solution)/shard_map/all_gather | solution.py:302
  217.9 6.5 fusion.43
  250.7 8.8 reshape.365
  259.5 10.2 %copy.168 = bf16[4,768,8,96]{1,0,3,2:T(4,128)(2,1)} copy(bf16[4,768,8,96]{3,1,0,2:T(8,128)(2,1)} %bitcast.157) | data formatting | bytes 9437184 | tf_op jit(solution)/shard_map/transpose | solution.py:311
  273.3 30.1 %multiply_convert_fusion = (bf16[768,3072]{1,0:T(8,128)(2,1)S(1)}, f32[768,3072]{1,0:T(8,128)}, f32[768,3072]{1,0:T(8,128)}) fusion(f32[3072]{0:T(1024)S(1)} %convert_element_type.222, bf16[768,3072]{1,0:T(8,128)(2,1)} %bitcast.181, f32[768,768]{0,1:T(8,128)S(1)} %copy-done.3, f32[768]{0:T(1024)S(1)} %convert_element_type.220, ...), kind=kOutput, calls=%fused_computation.4 | convolution fusion | flops 3782541312 | bytes 30695424 | tf_op jit(solution)/shard_map/dot_general | solution.py:453
  311.0 13.4 %fusion.41 = (bf16[3072]{0:T(1024)(128)(2,1)S(1)}, bf16[768,3072]{1,0:T(8,128)(2,1)}) fusion(f32[768,3072]{1,0:T(8,128)} %get-tuple-element.165, f32[768,3072]{1,0:T(8,128)} %get-tuple-element.210, f32[3072]{0:T(1024)S(1)} %convert_element_type.222, bf16[768,768]{0,1:T(8,128)(2,1)S(1)} %get-tuple-element.159, bf16[3072,768]{0,1:T(8,128)(2,1)S(1)} %bitcast.186), kind=kOutput, calls=%fused_computation.151 | convolution fusion | flops 3661624320 | bytes 29509632 | tf_op jit(solution)/shard_map/dot_general | solution.py:268
  324.5 7.4 multiply_reduce_fusion.1
  363.0 9.8 reshape.369
  380.9 6.6 copy.174
  387.6 9.7 reshape.371
  397.3 10.1 %copy.175 = bf16[8,4,768,96]{3,2,1,0:T(8,128)(2,1)} copy(bf16[8,4,768,96]{2,1,3,0:T(4,128)(2,1)} %bitcast.168) | data formatting | bytes 9437184 | tf_op jit(solution)/shard_map/transpose | solution.py:295
  407.4 11.6 %reshape.372 = bf16[32,73728]{1,0:T(8,128)(2,1)} reshape(bf16[8,4,768,96]{3,2,1,0:T(8,128)(2,1)} %copy.175) | data formatting | bytes 9437184 | tf_op jit(solution)/shard_map/reshape | solution.py:295
  436.9 6.5 pad_bitcast_fusion
  462.7 29.9 %shard_map.315 = f32[12,768,64]{2,1,0:T(8,128)} custom-call(s32[3]{0:T(128)S(1)} %get-tuple-element.217.lo_ref, s32[3]{0:T(128)S(1)} %get-tuple-element.216.hi_ref, bf16[12,768,64]{2,1,0:T(8,128)(2,1)S(1)} %bitcast.146, bf16[12,2816,64]{2,1,0:T(8,128)(2,1)} %bitcast.149, bf16[12,2816,64]{2,1,0:T(8,128)(2,1)} %bitcast.152, s32[768,1]{1,0:T(8,128)S(1)} %reshape.432.qs_ref, ...), custom_call_target="tpu_custom_call" | custom-call | tf_op jit(solution)/shard_map/pallas_call | solution.py:179
  492.6 54.6 %shard_map.316 = (f32[12,2816,64]{2,1,0:T(8,128)}, f32[12,2816,64]{2,1,0:T(8,128)}) custom-call(s32[11]{0:T(128)S(1)} %get-tuple-element.153.lo_ref, s32[11]{0:T(128)S(1)} %get-tuple-element.152.hi_ref, bf16[12,768,64]{2,1,0:T(8,128)(2,1)S(1)} %bitcast.147, bf16[12,2816,64]{2,1,0:T(8,128)(2,1)} %bitcast.150, bf16[12,2816,64]{2,1,0:T(8,128)(2,1)} %bitcast.153, ...), custom_call_target="tpu_custom_call" | custom-call | tf_op jit(solution)/shard_map/pallas_call | solution.py:218
  547.3 158.2 %reduce-scatter.9.cloned.1.call-done = bf16[1,1304,128]{2,1,0:T(8,128)(2,1)} async-done(((bf16[32,1304,128]{2,1,0:T(8,128)(2,1)}), bf16[1,1304,128]{2,1,0:T(8,128)(2,1)}) %reduce-scatter.9.cloned.1.call-update) | async-done | bytes 333840
  711.9 9.2 convert_bitcast_fusion.1
  721.1 9.5 copy.184
  730.5 10.1 %fusion.37 = (bf16[12,64]{1,0:T(8,128)(2,1)}, bf16[2816,12,64]{2,0,1:T(8,128)(2,1)}) fusion(f32[12,2816,64]{2,1,0:T(8,128)} %get-tuple-element.45), kind=kLoop, calls=%fused_computation.148 | loop fusion | flops 4324608 | bytes 12977664 | tf_op jit(solution)/shard_map/reduce_sum | solution.py:276
  740.6 9.5 copy.185
  767.0 8.1 convolution_convert_fusion.4
  786.2 8.1 convolution_convert_fusion.3
  844.2 44.9 %collective-permute-done.7 = bf16[256,768]{0,1:T(8,128)(2,1)} collective-permute-done((bf16[256,768]{0,1:T(8,128)(2,1)}, bf16[256,768]{0,1:T(8,128)(2,1)}, u32[]{:S(2)}, u32[]{:S(2)}) %collective-permute-start.7) | collective-permute-done | bytes 393248 | tf_op jit(solution)/shard_map/ppermute | solution.py:377
  889.1 19.5 %collective-permute-done.5 = bf16[256,768]{0,1:T(8,128)(2,1)} collective-permute-done((bf16[256,768]{0,1:T(8,128)(2,1)}, bf16[256,768]{0,1:T(8,128)(2,1)}, u32[]{:S(2)}, u32[]{:S(2)}) %collective-permute-start.5) | collective-permute-done | bytes 393248 | tf_op jit(solution)/shard_map/ppermute | solution.py:377
  917.3 66.9 %reduce-scatter.11.cloned.1.call-done = bf16[1,440,128]{2,1,0:T(8,128)(2,1)} async-done(((bf16[32,440,128]{2,1,0:T(8,128)(2,1)}), bf16[1,440,128]{2,1,0:T(8,128)(2,1)}) %reduce-scatter.11.cloned.1.call-update) | async-done | bytes 112656
  (264 shorter events, 309.2 us)
Async XLA Ops:
  7.2 32.3 %copy-start.6 = (bf16[768,768]{1,0:T(8,128)(2,1)S(1)}, bf16[768,768]{1,0:T(8,128)(2,1)}, u32[]{:S(2)}) copy-start(bf16[768,768]{1,0:T(8,128)(2,1)} %param.21) | copy-start | bytes 3538948
  7.2 22.4 %copy-start.29 = (s32[40]{0:T(128)S(1)}, s32[40]{0:T(128)}, u32[]{:S(2)}) copy-start(s32[40]{0:T(128)} %param.23) | copy-start | bytes 484
  7.2 22.5 %copy-start.30 = (s32[40]{0:T(128)S(1)}, s32[40]{0:T(128)}, u32[]{:S(2)}) copy-start(s32[40]{0:T(128)} %param.22) | copy-start | bytes 484
  7.2 33.7 %copy-start.11 = (bf16[768,768]{1,0:T(8,128)(2,1)S(1)}, bf16[768,768]{1,0:T(8,128)(2,1)}, u32[]{:S(2)}) copy-start(bf16[768,768]{1,0:T(8,128)(2,1)} %param.39) | copy-start | bytes 3538948
  7.2 77.4 %all-gather.5.cloned.1.call-start = ((), (), s32[]{:S(2)}) async-start(), calls=%async_computation.2 | async-start | bytes 3649536 | tf_op jit(solution)/shard_map/all_gather | solution.py:302
  10.9 196.7 %all-gather.7.cloned.1.call-start = ((), (), s32[]{:S(2)}) async-start(), calls=%async_computation.3 | async-start | bytes 10948608 | tf_op jit(solution)/shard_map/all_gather | solution.py:302
  15.0 27.3 %copy-start.19 = (bf16[768]{0:T(1024)(128)(2,1)S(1)}, bf16[768]{0:T(1024)(128)(2,1)}, u32[]{:S(2)}) copy-start(bf16[768]{0:T(1024)(128)(2,1)} %param.34) | copy-start | bytes 4612
  15.0 27.4 %copy-start.18 = (bf16[3072]{0:T(1024)(128)(2,1)S(1)}, bf16[3072]{0:T(1024)(128)(2,1)}, u32[]{:S(2)}) copy-start(bf16[3072]{0:T(1024)(128)(2,1)} %param.33) | copy-start | bytes 18436
  15.0 27.4 %copy-start.20 = (bf16[768]{0:T(1024)(128)(2,1)S(1)}, bf16[768]{0:T(1024)(128)(2,1)}, u32[]{:S(2)}) copy-start(bf16[768]{0:T(1024)(128)(2,1)} %param.32) | copy-start | bytes 4612
  15.0 27.4 %copy-start.21 = (bf16[768]{0:T(1024)(128)(2,1)S(1)}, bf16[768]{0:T(1024)(128)(2,1)}, u32[]{:S(2)}) copy-start(bf16[768]{0:T(1024)(128)(2,1)} %param.30) | copy-start | bytes 4612
  15.0 27.4 %copy-start.22 = (bf16[768]{0:T(1024)(128)(2,1)S(1)}, bf16[768]{0:T(1024)(128)(2,1)}, u32[]{:S(2)}) copy-start(bf16[768]{0:T(1024)(128)(2,1)} %param.31) | copy-start | bytes 4612
  15.1 27.5 %copy-start.23 = (bf16[768]{0:T(1024)(128)(2,1)S(1)}, bf16[768]{0:T(1024)(128)(2,1)}, u32[]{:S(2)}) copy-start(bf16[768]{0:T(1024)(128)(2,1)} %param.36) | copy-start | bytes 4612
  15.1 27.6 %copy-start.24 = (bf16[768]{0:T(1024)(128)(2,1)S(1)}, bf16[768]{0:T(1024)(128)(2,1)}, u32[]{:S(2)}) copy-start(bf16[768]{0:T(1024)(128)(2,1)} %param.35) | copy-start | bytes 4612
  15.1 27.6 %copy-start.25 = (bf16[768]{0:T(1024)(128)(2,1)S(1)}, bf16[768]{0:T(1024)(128)(2,1)}, u32[]{:S(2)}) copy-start(bf16[768]{0:T(1024)(128)(2,1)} %param.37) | copy-start | bytes 4612
  15.1 28.2 %copy-start.26 = (bf16[768]{0:T(1024)(128)(2,1)S(1)}, bf16[768]{0:T(1024)(128)(2,1)}, u32[]{:S(2)}) copy-start(bf16[768]{0:T(1024)(128)(2,1)} %param.38) | copy-start | bytes 4612
  15.1 690.4 %reduce-scatter.9.cloned.1.call-start = ((), (), s32[]{:S(2)}) async-start(), calls=%async_computation.4 | async-start | bytes 11016192
  15.2 49.9 %collective-permute-start.1 = (bf16[768,768]{1,0:T(8,128)(2,1)}, bf16[768,768]{1,0:T(8,128)(2,1)}, u32[]{:S(2)}, u32[]{:S(2)}) collective-permute-start(bf16[768,768]{1,0:T(8,128)(2,1)} %param.21), channel_id=1, source_target_pairs={{0,1},{1,2},{2,3},{4,5},{5,6},{6,7},{8,9},{9,10},{10,11},{12,13},{... | collective-permute-start | bytes 3538952 | tf_op jit(solution)/shard_map/ppermute | solution.py:377
  19.7 48.9 %collective-permute-start.2 = (bf16[768,768]{1,0:T(8,128)(2,1)}, bf16[768,768]{1,0:T(8,128)(2,1)}, u32[]{:S(2)}, u32[]{:S(2)}) collective-permute-start(bf16[768,768]{1,0:T(8,128)(2,1)} %param.21), channel_id=1, source_target_pairs={{1,0},{2,1},{3,2},{5,4},{6,5},{7,6},{9,8},{10,9},{11,10},{13,12},{... | collective-permute-start | bytes 3538952 | tf_op jit(solution)/shard_map/ppermute | solution.py:377
  23.1 40.2 %collective-permute-start = (bf16[256,768]{1,0:T(8,128)(2,1)}, bf16[256,768]{1,0:T(8,128)(2,1)}, u32[]{:S(2)}, u32[]{:S(2)}) collective-permute-start(bf16[256,768]{1,0:T(8,128)(2,1)} %get-tuple-element.184), channel_id=1, source_target_pairs={{0,2},{1,3},{4,6},{5,7},{8,10},{9,11},{12,14},{13,15},{16,18},{17,... | collective-permute-start | bytes 1179656 | tf_op jit(solution)/shard_map/ppermute | solution.py:377
  28.3 54.3 %collective-permute-start.3 = (bf16[256,768]{1,0:T(8,128)(2,1)}, bf16[256,768]{1,0:T(8,128)(2,1)S(1)}, u32[]{:S(2)}, u32[]{:S(2)}) collective-permute-start(bf16[256,768]{1,0:T(8,128)(2,1)} %get-tuple-element.183), channel_id=1, source_target_pairs={{2,0},{3,1},{6,4},{7,5},{10,8},{11,9},{14,12},{15,13},{18,16},{19,... | collective-permute-start | bytes 1179656 | tf_op jit(solution)/shard_map/ppermute | solution.py:377
  310.0 14.4 %slice-start.2 = ((s8[4718592]{0:T(1024)(128)(4,1)}), s8[4194304]{0:T(1024)(128)(4,1)S(1)}, s32[]{:S(2)}) async-start(s8[4718592]{0:T(1024)(128)(4,1)} %bitcast.182), calls=%async_computation.8 | async-start | bytes 8388608
  311.0 13.4 %slice-start.3 = ((s8[4718592]{0:T(1024)(128)(4,1)}), s8[524288]{0:T(1024)(128)(4,1)S(1)}, s32[]{:S(2)}) async-start(s8[4718592]{0:T(1024)(128)(4,1)} %bitcast.182), calls=%async_computation.9 | async-start | bytes 1048576
  335.4 8.0 slice-start.6
  424.6 10.9 %copy-start.16 = (bf16[32,24]{1,0:T(8,128)(2,1)S(1)}, bf16[32,24]{1,0:T(8,128)(2,1)}, u32[]{:S(2)}) copy-start(bf16[32,24]{1,0:T(8,128)(2,1)} %reshape.376) | copy-start | bytes 4612
  448.4 535.8 %reduce-scatter.11.cloned.1.call-start = ((), (), s32[]{:S(2)}) async-start(), calls=%async_computation.5 | async-start | bytes 3717120
  813.5 7.2 slice-start
  826.6 81.9 %copy-start.5 = (f32[768,768]{0,1:T(8,128)S(1)}, f32[768,768]{0,1:T(8,128)}, u32[]{:S(2)}) copy-start(f32[768,768]{0,1:T(8,128)} %copy-done.4) | copy-start | bytes 7077892
  826.6 81.9 %copy-start.8 = (bf16[768,12,64]{0,2,1:T(8,128)(2,1)S(1)}, bf16[768,12,64]{0,2,1:T(8,128)(2,1)}, u32[]{:S(2)}) copy-start(bf16[768,12,64]{0,2,1:T(8,128)(2,1)} %copy.182) | copy-start | bytes 3538948
  828.2 80.3 %collective-permute-start.6 = (bf16[768,768]{0,1:T(8,128)(2,1)}, bf16[768,768]{0,1:T(8,128)(2,1)}, u32[]{:S(2)}, u32[]{:S(2)}) collective-permute-start(bf16[768,768]{0,1:T(8,128)(2,1)} %get-tuple-element.178), channel_id=1, source_target_pairs={{0,1},{1,2},{2,3},{4,5},{5,6},{6,7},{8,9},{9,10},{10,11},{12,13},{... | collective-permute-start | bytes 3538952 | tf_op jit(solution)/shard_map/ppermute | solution.py:377
  830.7 77.9 %collective-permute-start.4 = (bf16[768,768]{0,1:T(8,128)(2,1)}, bf16[768,768]{0,1:T(8,128)(2,1)}, u32[]{:S(2)}, u32[]{:S(2)}) collective-permute-start(bf16[768,768]{0,1:T(8,128)(2,1)} %get-tuple-element.177), channel_id=1, source_target_pairs={{1,0},{2,1},{3,2},{5,4},{6,5},{7,6},{9,8},{10,9},{11,10},{13,12},{... | collective-permute-start | bytes 3538952 | tf_op jit(solution)/shard_map/ppermute | solution.py:377
  832.9 56.2 %collective-permute-start.7 = (bf16[256,768]{0,1:T(8,128)(2,1)}, bf16[256,768]{0,1:T(8,128)(2,1)}, u32[]{:S(2)}, u32[]{:S(2)}) collective-permute-start(bf16[256,768]{0,1:T(8,128)(2,1)} %get-tuple-element.176), channel_id=1, source_target_pairs={{0,2},{1,3},{4,6},{5,7},{8,10},{9,11},{12,14},{13,15},{16,18},{17,... | collective-permute-start | bytes 1179656 | tf_op jit(solution)/shard_map/ppermute | solution.py:377
  838.7 69.9 %collective-permute-start.5 = (bf16[256,768]{0,1:T(8,128)(2,1)}, bf16[256,768]{0,1:T(8,128)(2,1)}, u32[]{:S(2)}, u32[]{:S(2)}) collective-permute-start(bf16[256,768]{0,1:T(8,128)(2,1)} %get-tuple-element.175), channel_id=1, source_target_pairs={{2,0},{3,1},{6,4},{7,5},{10,8},{11,9},{14,12},{15,13},{18,16},{19,... | collective-permute-start | bytes 1179656 | tf_op jit(solution)/shard_map/ppermute | solution.py:377
  (20 other events, 70.4 us)
Sparse Core Ops, SparseCore 0:
  11.4 73.2 all-gather.4
  87.5 85.0 all-gather.6
  448.6 256.8 reduce-scatter.8
  813.6 170.5 reduce-scatter.10

commit v4 on v1

--- a/solution.py
+++ b/solution.py
@@ -287,38 +287,76 @@
     return (segment_ids, starts, ends)
 
 
-def gather_weight(w, rows_over_dp):
+def cyclic_pieces(piece):
+    count = lax.axis_size("tensor")
+    me = lax.axis_index("tensor")
+    got = [piece]
+    for k in range(1, count):
+        got.append(lax.ppermute(piece, "tensor", [(s, (s + k) % count) for s in range(count)]))
+    order = (me - jnp.arange(count, dtype=jnp.int32)) % count
+    return jnp.take(jnp.stack(got), order, axis=0)
+
+
+def gather_weights(blocks):
+    count = lax.axis_size("tensor")
+    widths = [b.shape[1] for b in blocks]
+    piece = jnp.concatenate(blocks, axis=1)
+    parts = cyclic_pieces(piece)
+    cols, at = [], 0
+    for w in widths:
+        cols.extend(parts[t, :, at:at + w] for t in range(count))
+        at += w
+    strip = jnp.concatenate(cols, axis=1)
+    full = lax.all_gather(strip, "dp", axis=0, tiled=True)
+    out, at = [], 0
+    for w in widths:
+        out.append(full[:, at:at + w * count])
+        at += w * count
+    return out
+
+
+def vector_rows(v, rows):
     dp = lax.axis_size("dp")
-    tens = lax.axis_size("tensor")
-    r, c = w.shape
-    full = lax.all_gather(w, ("dp", "tensor"), axis=0, tiled=False).reshape(dp, tens, r, c)
-    if rows_over_dp:
-        return full.transpose(0, 2, 1, 3).reshape(dp * r, tens * c)
-    return full.transpose(1, 2, 0, 3).reshape(tens * r, dp * c)
-
-
-def scatter_grad(g, rows_over_dp):
-    dp = lax.axis_size("dp")
-    tens = lax.axis_size("tensor")
-    if rows_over_dp:
-        r, c = g.shape[0] // dp, g.shape[1] // tens
-        blocks = g.reshape(dp, r, tens, c).transpose(0, 2, 1, 3)
-    else:
-        r, c = g.shape[0] // tens, g.shape[1] // dp
-        blocks = g.reshape(tens, r, dp, c).transpose(2, 0, 1, 3)
-    blocks = blocks.reshape(dp * tens, r, c)
-    return lax.psum_scatter(blocks, ("dp", "tensor"), scatter_dimension=0, tiled=True).reshape(r, c)
-
-
-def scatter_vectors(vectors):
-    parts = lax.axis_size("dp") * lax.axis_size("tensor")
-    joined = jnp.concatenate([v.reshape(parts, -1) for v in vectors], axis=1)
-    summed = lax.psum_scatter(joined, ("dp", "tensor"), scatter_dimension=0, tiled=True)[0]
+    slab = rows // dp
+    spread = v.reshape(dp, 1, -1)
+    return jnp.pad(spread, ((0, 0), (0, slab - 1), (0, 0))).reshape(rows, -1)
+
+
+def pack_grads(grads, vectors):
+    count = lax.axis_size("tensor")
+    me = lax.axis_index("tensor")
+    rows = grads[0].shape[0]
+    mats = [g.astype(jnp.bfloat16) for g in grads] + [vector_rows(v.astype(jnp.bfloat16), rows) for v in vectors]
+    widths = [m.shape[1] // count for m in mats]
+    cat = jnp.concatenate(mats, axis=1)
+    return widths, cat
+
+
+def reduce_dp(cat):
+    return lax.psum_scatter(cat, "dp", scatter_dimension=0, tiled=True)
+
+
+def reduce_tensor(strip, widths, n_grads):
+    count = lax.axis_size("tensor")
+    me = lax.axis_index("tensor")
+    strip = strip.astype(jnp.float32)
+    per_t = []
+    for t in range(count):
+        at, cols = 0, []
+        for w in widths:
+            cols.append(strip[:, at + t * w:at + (t + 1) * w])
+            at += w * count
+        per_t.append(jnp.concatenate(cols, axis=1))
+    stacked = jnp.stack(per_t)
+    total = jnp.take(stacked, me, axis=0)
+    for k in range(1, count):
+        send = jnp.take(stacked, (me + k) % count, axis=0)
+        total = total + lax.ppermute(send, "tensor", [(s, (s + k) % count) for s in range(count)])
     out, at = [], 0
-    for v in vectors:
-        n = v.shape[0] // parts
-        out.append(summed[at:at + n])
-        at += n
+    for i, w in enumerate(widths):
+        block = total[:, at:at + w]
+        at += w
+        out.append(block if i < n_grads else block[0])
     return out
 
 
@@ -386,7 +424,7 @@
     base = rows * tens_index - LONGEST
     places = base + jnp.arange(window, dtype=jnp.int32)
     valid = (places >= 0) & (places < group_rows)
-    k_ids = jnp.where(valid, jnp.take(seg, jnp.clip(places, 0, group_rows - 1)), -1).astype(jnp.int32)
+    k_ids = jnp.where(valid, jnp.sum((places[:, None] >= ends[None, :]).astype(jnp.int32), axis=1), -1).astype(jnp.int32)
     q_ids = lax.dynamic_slice_in_dim(seg, rows * tens_index, rows)
     q_start = jnp.take(starts, q_ids) - base
     q_end = jnp.take(ends, q_ids) - base
@@ -395,12 +433,8 @@
     kv_steps = min(nkb, (BLOCK + 2 * (LONGEST - 1)) // BLOCK + 2)
     q_steps = rows // BLOCK
 
-    wq = gather_weight(w_query, True)
-    wk = gather_weight(w_key, True)
-    wv = gather_weight(w_value, True)
-    wo = gather_weight(w_out, False)
-    wi = gather_weight(w_inner, True)
-    wf = gather_weight(w_outer, False)
+    wq, wk, wv = gather_weights([w_query, w_key, w_value])
+    wo_t, wi, wf_t = gather_weights([w_out.T, w_inner, w_outer.T])
     gain_one = gain_attn.astype(jnp.float32)
     gain_two = gain_ffn.astype(jnp.float32)
 
@@ -412,31 +446,47 @@
     q_h, k_h, v_h = to_heads(query), to_heads(key_w), to_heads(value_w)
     ctx_h, lse = flash_forward(q_h, k_h, v_h, q_ids, k_ids, lo, hi, BLOCK, BLOCK, kv_steps)
     context = from_heads(ctx_h).astype(jnp.bfloat16)
-    attn = jnp.dot(context, wo, preferred_element_type=jnp.float32) + b_out.astype(jnp.float32)
+    attn = contract_last(context, wo_t) + b_out.astype(jnp.float32)
     hidden, norm_one, inverse_one = norm_forward(tokens.astype(jnp.float32) + attn, gain_one, shift_attn.astype(jnp.float32))
     hidden_low = hidden.astype(jnp.bfloat16)
     pre_act = jnp.dot(hidden_low, wi, preferred_element_type=jnp.float32) + b_inner.astype(jnp.float32)
     act = activate(pre_act).astype(jnp.bfloat16)
-    ffn = jnp.dot(act, wf, preferred_element_type=jnp.float32) + b_outer.astype(jnp.float32)
+    ffn = contract_last(act, wf_t) + b_outer.astype(jnp.float32)
     output, norm_two, inverse_two = norm_forward(hidden + ffn, gain_two, shift_ffn.astype(jnp.float32))
 
     grad_y = grad_out.astype(jnp.float32)
     grad_resid_two = norm_backward(grad_y, norm_two, inverse_two, gain_two)
     grad_ffn = grad_resid_two.astype(jnp.bfloat16)
-    grad_outer_w = contract_first(act, grad_ffn)
-    grad_act = contract_last(grad_ffn, wf)
+    grad_outer_t = contract_first(grad_ffn, act)
+    grad_act = jnp.dot(grad_ffn, wf_t, preferred_element_type=jnp.float32)
     unused, gelu_pull = jax.vjp(activate, pre_act)
     grad_pre = gelu_pull(grad_act)[0].astype(jnp.bfloat16)
     grad_inner_w = contract_first(hidden_low, grad_pre)
     grad_hidden = grad_resid_two + contract_last(grad_pre, wi)
     grad_resid_one = norm_backward(grad_hidden, norm_one, inverse_one, gain_one)
     grad_attn = grad_resid_one.astype(jnp.bfloat16)
-    grad_out_w = contract_first(context, grad_attn)
-    grad_context = contract_last(grad_attn, wo).astype(jnp.bfloat16)
+    grad_out_t = contract_first(grad_attn, context)
+    grad_context = jnp.dot(grad_attn, wo_t, preferred_element_type=jnp.float32).astype(jnp.bfloat16)
+    late = [
+        column_sum(grad_attn),
+        column_sum(grad_pre),
+        column_sum(grad_ffn),
+        jnp.sum(grad_hidden * norm_one, axis=0),
+        jnp.sum(grad_hidden, axis=0),
+        jnp.sum(grad_y * norm_two, axis=0),
+        jnp.sum(grad_y, axis=0),
+    ]
+    early_widths, early_cat = pack_grads([grad_out_t, grad_inner_w, grad_outer_t], late)
+    grad_context, early_cat = lax.optimization_barrier((grad_context, early_cat))
+    early_strip = reduce_dp(early_cat)
     do_h = to_heads(grad_context)
     delta = jnp.sum(do_h.astype(jnp.float32) * ctx_h, axis=-1, keepdims=True)
     dq_h = flash_dq(q_h, k_h, v_h, q_ids, k_ids, lse, delta, do_h, lo, hi, BLOCK, BLOCK, kv_steps)
     dk_h, dv_h = flash_dkv(q_h, k_h, v_h, q_ids, k_ids, lse, delta, do_h, qlo, qhi, BLOCK, BLOCK, q_steps)
+    early_strip, dq_h, dk_h, dv_h = lax.optimization_barrier((early_strip, dq_h, dk_h, dv_h))
+    early_sums = reduce_tensor(early_strip, early_widths, 3)
+    g_out_t, g_inner, g_outer_t = early_sums[:3]
+    late = early_sums[3:]
     grad_query = from_heads(dq_h).astype(jnp.bfloat16)
     grad_key = from_heads(dk_h).astype(jnp.bfloat16)
     grad_value = from_heads(dv_h).astype(jnp.bfloat16)
@@ -446,25 +496,12 @@
     grad_win = contract_last(grad_key, wk) + contract_last(grad_value, wv)
     grad_tokens = grad_resid_one + contract_last(grad_query, wq) + return_window(grad_win, takes, count)
 
-    summed = (
-        scatter_grad(grad_query_w, True),
-        scatter_grad(grad_key_w, True),
-        scatter_grad(grad_value_w, True),
-        scatter_grad(grad_out_w, False),
-        scatter_grad(grad_inner_w, True),
-        scatter_grad(grad_outer_w, False),
+    late_widths, late_cat = pack_grads(
+        [grad_query_w, grad_key_w, grad_value_w], [column_sum(grad_query), column_sum(grad_value)]
     )
-    small = scatter_vectors([
-        column_sum(grad_query),
-        column_sum(grad_value),
-        column_sum(grad_attn),
-        column_sum(grad_pre),
-        column_sum(grad_ffn),
-        jnp.sum(grad_hidden * norm_one, axis=0),
-        jnp.sum(grad_hidden, axis=0),
-        jnp.sum(grad_y * norm_two, axis=0),
-        jnp.sum(grad_y, axis=0),
-    ])
+    g_query, g_key, g_value, g_bq, g_bv = reduce_tensor(reduce_dp(late_cat), late_widths, 3)
+    summed = (g_query, g_key, g_value, g_out_t.T, g_inner, g_outer_t.T)
+    small = [g_bq, g_bv] + late
     return (output.astype(jnp.bfloat16), grad_tokens) + summed + tuple(small)
 
 

time: 1190 us -> 689 us (0.58)
  waiting for transfers between devices: 526 us -> 122 us
  local copies, waits for them, and re-layouts: 203 us -> 140 us
  blocking collectives: 58.8 us -> 0 us
  starting transfers between devices: 35.8 us -> 82.2 us
  Pallas kernels: 141 us -> 125 us
  matrix products: 147 us -> 132 us
  other arithmetic: 46.6 us -> 60.1 us
    reduce_scatter x6 -> x1, waiting for transfers between devices: 342 us -> 10.7 us  [reduce_dp(): return lax.psum_scatter(cat, 'dp', scatter_dimension=0, tiled=True)]
    all_gather x6 -> x2, waiting for transfers between devices: 180 us -> 0.01 us  [gather_weights(): full = lax.all_gather(strip, 'dp', axis=0, tiled=True)]
    ppermute x0 -> x12, waiting for transfers between devices: none -> 77.7 us  [the longest x6 41.5 us: reduce_tensor(): lax.ppermute(send, 'tensor', [(s, (s + k) % count) for s in range(count)])]
    reshape x23 -> x8, local copies, waits for them, and re-layouts: 65.4 us -> 0.77 us  [the longest x6 0.44 us: vector_rows(): spread = v.reshape(dp, 1, -1)]
    unnamed x1 -> x0, blocking collectives: 58.8 us -> none
    ppermute x0 -> x12, starting transfers between devices: none -> 54.6 us  [the longest x6 45.3 us: reduce_tensor(): lax.ppermute(send, 'tensor', [(s, (s + k) % count) for s in range(count)])]
    ppermute x8, waiting for transfers between devices: 0.02 us -> 33.3 us  [shift_rows(): return lax.ppermute(values, 'tensor', pairs)]
    concatenate x1 -> x10, local copies, waits for them, and re-layouts: 0.12 us -> 28.6 us  [the longest x2 19.1 us: pack_grads(): cat = jnp.concatenate(mats, axis=1)]
  transfers between devices with their start and end apart: 20 -> 24, of which waited for: 8 -> 11; matrix products, arithmetic and copies ran while one was open for 26% -> 20% of each run, Pallas kernels for 12% -> 19%
where the time goes in v4:
time: 689 us; the launch traced here: 676 us
  local copies, waits for them, and re-layouts  140 us (20%)
  matrix products  132 us (19%)
  Pallas kernels  125 us (18%)
  waiting for transfers between devices  122 us (18%)
  starting transfers between devices  82.2 us (12%)
  other arithmetic  60.1 us (9%)
  between operations  15.1 us (2%)
    pallas_call x1, Pallas kernels, flash_dkv(): pl.pallas_call(_dkv_kernel, grid_spec=grid_spec, out_shape=[jax.ShapeDtyp...  56.1 us
    ppermute x6, starting transfers between devices, reduce_tensor(): lax.ppermute(send, 'tensor', [(s, (s + k) % count) for s in range(count)])  45.3 us
    ppermute x6, waiting for transfers between devices, reduce_tensor(): lax.ppermute(send, 'tensor', [(s, (s + k) % count) for s in range(count)])  41.5 us
    pallas_call x1, Pallas kernels, flash_forward(): pl.pallas_call(_fwd_kernel, grid_spec=grid_spec, out_shape=[jax.ShapeDtyp...  37.7 us
    ppermute x6, waiting for transfers between devices, cyclic_pieces(): lax.ppermute(piece, 'tensor', [(s, (s + k) % count) for s in range(count)])  36.2 us
    dot_general x6, matrix products, contract_first(): lax.dot_general(left, right, (((0,), (0,)), ((), ())), preferred_element_...  34.4 us
    unnamed x110, local copies, waits for them, and re-layouts  33.3 us
    ppermute x8, waiting for transfers between devices, shift_rows(): return lax.ppermute(values, 'tensor', pairs)  33.3 us
  transfers between devices with their start and end apart: 24, of which 11 were waited for; matrix products, arithmetic and copies ran while one was open for 20% of the time, Pallas kernels for 19%

profile of v4, /device:TPU:4, one launch (start us, length us, event | category | flops | bytes accessed | tf_op | source)
XLA Modules:
  0.0 675.7 jit_solution(2639962334195645998)
XLA Ops:
  15.5 6.9 %collective-permute-done.1 = bf16[96,576]{1,0:T(8,128)(2,1)S(1)} collective-permute-done((bf16[96,576]{1,0:T(8,128)(2,1)S(1)}, bf16[96,576]{1,0:T(8,128)(2,1)S(1)}, u32[]{:S(2)}, u32[]{:S(2)}) %collective-permute-start.1) | collective-permute-done | bytes 110624 | tf_op jit(solution)/shard_map/ppermute | solution.py:295
  35.1 22.0 %collective-permute-done.8 = bf16[96,1728]{1,0:T(8,128)(2,1)S(1)} collective-permute-done((bf16[96,1728]{1,0:T(8,128)(2,1)S(1)}, bf16[96,1728]{1,0:T(8,128)(2,1)S(1)}, u32[]{:S(2)}, u32[]{:S(2)}) %collective-permute-start.8) | collective-permute-done | bytes 331808 | tf_op jit(solution)/shard_map/ppermute | solution.py:295
  86.3 9.4 %collective-permute-done.3 = bf16[256,768]{1,0:T(8,128)(2,1)} collective-permute-done((bf16[256,768]{1,0:T(8,128)(2,1)}, bf16[256,768]{1,0:T(8,128)(2,1)}, u32[]{:S(2)}, u32[]{:S(2)}) %collective-permute-start.3) | collective-permute-done | bytes 393248 | tf_op jit(solution)/shard_map/ppermute | solution.py:376
  103.3 6.7 collective-permute-done.6
  117.3 8.2 %convolution_convert_fusion.2 = bf16[2816,768]{0,1:T(8,128)(2,1)} fusion(bf16[2816,768]{1,0:T(8,128)(2,1)} %constant_dynamic-update-slice_fusion, bf16[768,2304]{1,0:T(8,128)(2,1)} %all-gather.3.cloned.1.call-done), kind=kOutput, calls=%fused_computation.24 | convolution fusion | flops 3324051456 | bytes 9830400 | tf_op jit(solution)/shard_map/dot_general | solution.py:444
  125.5 9.1 %copy.167 = bf16[2816,12,64]{2,0,1:T(8,128)(2,1)} copy(bf16[2816,12,64]{0,2,1:T(8,128)(2,1)} %bitcast.209) | data formatting | bytes 8650752 | tf_op jit(solution)/shard_map/reshape | solution.py:406
  134.7 8.2 %add_convert_fusion.1 = bf16[2816,768]{0,1:T(8,128)(2,1)} fusion(bf16[2816,768]{1,0:T(8,128)(2,1)} %constant_dynamic-update-slice_fusion, f32[768]{0:T(1024)S(1)} %convert_element_type.225, bf16[768,2304]{1,0:T(8,128)(2,1)} %all-gather.3.cloned.1.call-done), kind=kOutput, calls=%fused_computation.20 | convolution fusion | flops 3326214144 | bytes 9833472 | tf_op jit(solution)/shard_map/dot_general | solution.py:445
  142.9 9.1 %copy.168 = bf16[2816,12,64]{2,0,1:T(8,128)(2,1)} copy(bf16[2816,12,64]{0,2,1:T(8,128)(2,1)} %bitcast.208) | data formatting | bytes 8650752 | tf_op jit(solution)/shard_map/reshape | solution.py:406
  152.0 37.7 %shard_map.314 = (f32[12,768,64]{2,1,0:T(8,128)}, f32[12,768,1]{2,1,0:T(8,128)}) custom-call(s32[3]{0:T(128)S(1)} %fusion.68.lo_ref, s32[3]{0:T(128)S(1)} %fusion.67.hi_ref, bf16[12,768,64]{2,1,0:T(8,128)(2,1)S(1)} %bitcast.184, bf16[12,2816,64]{2,1,0:T(8,128)(2,1)} %bitcast.187, bf16[12,2816,64]{2,1,0:T(8,128)(2,1)} %bitcast.190, ...), custom_call_target="tpu_custom_call" | custom-call | tf_op jit(solution)/shard_map/pallas_call | solution.py:137
  202.8 27.9 %multiply_convert_fusion = (bf16[768,3072]{1,0:T(8,128)(2,1)S(1)}, f32[768,3072]{1,0:T(8,128)}, f32[768,3072]{1,0:T(8,128)}) fusion(f32[3072]{0:T(1024)S(1)} %convert_element_type.235, bf16[768,6912]{1,0:T(8,128)(2,1)S(1)} %copy-done.31, f32[768,768]{0,1:T(8,128)S(1)} %get-tuple-element.294, f32[768]{0:T(1024)S(1)} %convert_element_type.233, ...), kind=kOutput, calls=%fused_computation.5 | convolution fusion | flops 3782541312 | bytes 30699520 | tf_op jit(solution)/shard_map/dot_general | solution.py:452
  244.9 14.5 %fusion.89 = (bf16[3072]{0:T(1024)(128)(2,1)S(1)}, bf16[768,3072]{1,0:T(8,128)(2,1)}) fusion(f32[768,3072]{1,0:T(8,128)} %get-tuple-element.167, bf16[768,768]{0,1:T(8,128)(2,1)S(1)} %get-tuple-element.163, bf16[768,6912]{1,0:T(8,128)(2,1)} %all-gather.5.cloned.1.call-done, f32[768,3072]{1,0:T(8,128)} %get-tuple-element.295, ...), kind=kOutput, calls=%fused_computation.259 | convolution fusion | flops 3661624320 | bytes 29509632 | tf_op jit(solution)/shard_map/dot_general | solution.py:461
  259.4 8.3 %convolution_convert_fusion.1 = bf16[768,3072]{1,0:T(8,128)(2,1)} fusion(bf16[768,3072]{1,0:T(8,128)(2,1)} %get-tuple-element.300, f32[768,768]{0,1:T(8,128)S(1)} %get-tuple-element.294, f32[768]{0:T(1024)S(1)} %convert_element_type.233, f32[768]{0:T(1024)S(1)} %convert_element_type.232, f32[768]{0:T(1024)S(1)} %add_rsqrt_fusion.1, ...), kind=kOutput, calls=%fused_computation.23 | convolution fusion | flops 3629187072 | bytes 11808768 | tf_op jit(solution)/shard_map/dot_general | solution.py:272
  267.7 7.5 %multiply_reduce_fusion.1 = (bf16[768]{0:T(1024)(128)(2,1)S(1)}, f32[768]{0:T(1024)S(1)}, f32[768]{0:T(1024)S(1)}, bf16[768]{0:T(1024)(128)(2,1)S(1)}, f32[768,768]{0,1:T(8,128)S(1)}) fusion(f32[768,768]{0,1:T(8,128)S(1)} %get-tuple-element.294, f32[768]{0:T(1024)S(1)} %add_rsqrt_fusion.1, f32[768]{0:T(1024)S(1)} %broadcast_multiply_fusion.5, ...), kind=kOutput, calls=%fused_computation.51 | convolution fusion | flops 3634492416 | bytes 17728512 | tf_op jit(solution)/shard_map/dot_general | solution.py:268
  286.1 18.5 %concatenate.50 = bf16[768,7872]{1,0:T(8,128)(2,1)} concatenate(bf16[768,768]{1,0:T(8,128)(2,1)} %copy.182, bf16[768,3072]{1,0:T(8,128)(2,1)} %convolution_convert_fusion.1, bf16[768,3072]{1,0:T(8,128)(2,1)} %convolution_convert_fusion, bf16[768,96]{1,0:T(8,128)(2,1)} %bitcast.220, bf16[768,384]{1,0:T(8,128)(2,1)S(1)} %bitcast.214, bf16[768,96]{1,0:T(8,128)(2,1)} %bitcast.221, ...), dimensions={1} | concatenate | bytes 24182784 | tf_op jit(solution)/shard_map/concatenate | solution.py:331
  322.9 31.3 %shard_map.315 = f32[12,768,64]{2,1,0:T(8,128)} custom-call(s32[3]{0:T(128)S(1)} %fusion.68.lo_ref, s32[3]{0:T(128)S(1)} %fusion.67.hi_ref, bf16[12,768,64]{2,1,0:T(8,128)(2,1)S(1)} %bitcast.185, bf16[12,2816,64]{2,1,0:T(8,128)(2,1)} %bitcast.188, bf16[12,2816,64]{2,1,0:T(8,128)(2,1)} %bitcast.191, s32[768,1]{1,0:T(8,128)S(1)} %reshape.545.qs_ref, ...), custom_call_target="tpu_custom_call" | custom-call | tf_op jit(solution)/shard_map/pallas_call | solution.py:179
  354.2 56.1 %shard_map.316 = (f32[12,2816,64]{2,1,0:T(8,128)}, f32[12,2816,64]{2,1,0:T(8,128)}) custom-call(s32[11]{0:T(128)S(1)} %get-tuple-element.161.lo_ref, s32[11]{0:T(128)S(1)} %get-tuple-element.160.hi_ref, bf16[12,768,64]{2,1,0:T(8,128)(2,1)S(1)} %bitcast.186, bf16[12,2816,64]{2,1,0:T(8,128)(2,1)} %bitcast.189, bf16[12,2816,64]{2,1,0:T(8,128)(2,1)} %bitcast.192, ...), custom_call_target="tpu_custom_call" | custom-call | tf_op jit(solution)/shard_map/pallas_call | solution.py:218
  410.3 10.7 %reduce-scatter.5.cloned.1.call-done = bf16[96,7872]{1,0:T(8,128)(2,1)} async-done(((bf16[768,7872]{1,0:T(8,128)(2,1)}), bf16[96,7872]{1,0:T(8,128)(2,1)}) %reduce-scatter.5.cloned.1.call-update) | async-done | bytes 1511440 | tf_op jit(solution)/shard_map/reduce_scatter | solution.py:336
  425.1 9.2 %convert_bitcast_fusion.1 = bf16[2816,12,64]{2,0,1:T(8,128)(2,1)} fusion(f32[12,2816,64]{2,1,0:T(8,128)} %get-tuple-element.38), kind=kLoop, calls=%fused_computation.27 | loop fusion | flops 2162688 | bytes 12976128 | tf_op jit(solution)/shard_map/convert_element_type | solution.py:492
  434.2 7.1 %convert_reduce_fusion = bf16[12,64]{1,0:T(8,128)(2,1)S(1)} fusion(f32[12,2816,64]{2,1,0:T(8,128)} %get-tuple-element.38), kind=kLoop, calls=%fused_computation.26 | loop fusion | flops 4324608 | bytes 8652288 | tf_op jit(solution)/shard_map/reduce_sum | solution.py:276
  441.3 9.3 %convert_bitcast_fusion = bf16[2816,12,64]{2,0,1:T(8,128)(2,1)} fusion(f32[12,2816,64]{2,1,0:T(8,128)} %get-tuple-element.37), kind=kLoop, calls=%fused_computation.19 | loop fusion | flops 2162688 | bytes 12976128 | tf_op jit(solution)/shard_map/convert_element_type | solution.py:491
  450.6 9.5 %copy.191 = bf16[2816,12,64]{0,2,1:T(8,128)(2,1)} copy(bf16[2816,12,64]{2,0,1:T(8,128)(2,1)} %convert_bitcast_fusion) | data formatting | bytes 8650752 | tf_op jit(solution)/shard_map/convert_element_type | solution.py:491
  460.1 9.6 %copy.192 = bf16[2816,12,64]{0,2,1:T(8,128)(2,1)} copy(bf16[2816,12,64]{2,0,1:T(8,128)(2,1)} %convert_bitcast_fusion.1) | data formatting | bytes 8650752 | tf_op jit(solution)/shard_map/convert_element_type | solution.py:492
  476.4 8.2 %fusion.34 = bf16[768,2496]{0,1:T(8,128)(2,1)} fusion(bf16[768,2496]{0,1:T(8,128)(2,1)} %fusion.36, bf16[2816,768]{0,1:T(8,128)(2,1)} %bitcast.204, bf16[2816,768]{1,0:T(8,128)(2,1)} %constant_dynamic-update-slice_fusion), kind=kOutput, calls=%fused_computation.70 | convolution fusion | flops 3322478592 | bytes 9830400 | tf_op jit(solution)/shard_map/dot_general | solution.py:272
  484.6 6.8 fusion.33
  515.0 16.8 %collective-permute-start.19 = (f32[96,1968]{1,0:T(8,128)}, f32[96,1968]{1,0:T(8,128)}, u32[]{:S(2)}, u32[]{:S(2)}) collective-permute-start(f32[96,1968]{1,0:T(8,128)} %get-tuple-element.180), channel_id=1, source_target_pairs={{0,3},{1,0},{2,1},{3,2},{4,7},{5,4},{6,5},{7,6},{8,11},{9,8},{10,9... | collective-permute-start | bytes 2267144 | tf_op jit(solution)/shard_map/ppermute | solution.py:354
  531.7 12.6 %collective-permute-start.18 = (f32[96,1968]{1,0:T(8,128)}, f32[96,1968]{1,0:T(8,128)}, u32[]{:S(2)}, u32[]{:S(2)}) collective-permute-start(f32[96,1968]{1,0:T(8,128)} %get-tuple-element.181), channel_id=1, source_target_pairs={{0,2},{1,3},{2,0},{3,1},{4,6},{5,7},{6,4},{7,5},{8,10},{9,11},{10,... | collective-permute-start | bytes 2267144 | tf_op jit(solution)/shard_map/ppermute | solution.py:354
  549.5 7.5 %fusion.90 = (bf16[2816,768]{0,1:T(8,128)(2,1)S(1)}, f32[2816,768]{0,1:T(8,128)}) fusion(f32[2816,768]{0,1:T(8,128)S(1)} %fusion.39, bf16[2816,768]{0,1:T(8,128)(2,1)S(1)} %bitcast.200, bf16[768,2304]{1,0:T(8,128)(2,1)} %all-gather.3.cloned.1.call-done), kind=kOutput, calls=%fused_computation.260 | convolution fusion | flops 3326214144 | bytes 27131904 | tf_op jit(solution)/shard_map/dot_general | solution.py:268
  563.3 11.2 %collective-permute-done.19 = f32[96,1968]{1,0:T(8,128)} collective-permute-done((f32[96,1968]{1,0:T(8,128)}, f32[96,1968]{1,0:T(8,128)}, u32[]{:S(2)}, u32[]{:S(2)}) %collective-permute-start.19) | collective-permute-done | bytes 755744 | tf_op jit(solution)/shard_map/ppermute | solution.py:354
  574.5 11.4 %collective-permute-start.13 = (bf16[256,768]{0,1:T(8,128)(2,1)}, bf16[256,768]{0,1:T(8,128)(2,1)}, u32[]{:S(2)}, u32[]{:S(2)}) collective-permute-start(bf16[256,768]{0,1:T(8,128)(2,1)} %get-tuple-element.176), channel_id=1, source_target_pairs={{0,2},{1,3},{4,6},{5,7},{8,10},{9,11},{12,14},{13,15},{16,18},{17,... | collective-permute-start | bytes 1179656 | tf_op jit(solution)/shard_map/ppermute | solution.py:376
  585.8 23.7 %collective-permute-done.18 = f32[96,1968]{1,0:T(8,128)} collective-permute-done((f32[96,1968]{1,0:T(8,128)}, f32[96,1968]{1,0:T(8,128)}, u32[]{:S(2)}, u32[]{:S(2)}) %collective-permute-start.18) | collective-permute-done | bytes 755744 | tf_op jit(solution)/shard_map/ppermute | solution.py:354
  622.6 17.2 %collective-permute-done.11 = bf16[256,768]{0,1:T(8,128)(2,1)} collective-permute-done((bf16[256,768]{0,1:T(8,128)(2,1)}, bf16[256,768]{0,1:T(8,128)(2,1)}, u32[]{:S(2)}, u32[]{:S(2)}) %collective-permute-start.11) | collective-permute-done | bytes 393248 | tf_op jit(solution)/shard_map/ppermute | solution.py:376
  639.9 11.5 %collective-permute-start.14 = (f32[96,624]{0,1:T(8,128)}, f32[96,624]{0,1:T(8,128)}, u32[]{:S(2)}, u32[]{:S(2)}) collective-permute-start(f32[96,624]{0,1:T(8,128)} %get-tuple-element.235), channel_id=1, source_target_pairs={{0,1},{1,2},{2,3},{3,0},{4,5},{5,6},{6,7},{7,4},{8,9},{9,10},{10,1... | collective-permute-start | bytes 718856 | tf_op jit(solution)/shard_map/ppermute | solution.py:354
  (281 shorter events, 197.1 us)
Async XLA Ops:
  7.2 103.7 %all-gather.3.cloned.1.call-start = ((), (), s32[]{:S(2)}) async-start(), calls=%async_computation.2 | async-start | bytes 3981312 | tf_op jit(solution)/shard_map/all_gather | solution.py:310
  8.2 7.4 %collective-permute-start.2 = (bf16[96,576]{1,0:T(8,128)(2,1)S(1)}, bf16[96,576]{1,0:T(8,128)(2,1)S(1)}, u32[]{:S(2)}, u32[]{:S(2)}) collective-permute-start(bf16[96,576]{1,0:T(8,128)(2,1)S(1)} %pad_maximum_fusion.4), channel_id=1, source_target_pairs={{0,3},{1,0},{2,1},{3,2},{4,7},{5,4},{6,5},{7,6},{8,11},{9,8},{10,9... | collective-permute-start | bytes 331784 | tf_op jit(solution)/shard_map/ppermute | solution.py:295
  11.8 10.6 %collective-permute-start.1 = (bf16[96,576]{1,0:T(8,128)(2,1)S(1)}, bf16[96,576]{1,0:T(8,128)(2,1)S(1)}, u32[]{:S(2)}, u32[]{:S(2)}) collective-permute-start(bf16[96,576]{1,0:T(8,128)(2,1)S(1)} %pad_maximum_fusion.4), channel_id=1, source_target_pairs={{0,2},{1,3},{2,0},{3,1},{4,6},{5,7},{6,4},{7,5},{8,10},{9,11},{10,... | collective-permute-start | bytes 331784 | tf_op jit(solution)/shard_map/ppermute | solution.py:295
  11.8 10.6 %collective-permute-start = (bf16[96,576]{1,0:T(8,128)(2,1)S(1)}, bf16[96,576]{1,0:T(8,128)(2,1)S(1)}, u32[]{:S(2)}, u32[]{:S(2)}) collective-permute-start(bf16[96,576]{1,0:T(8,128)(2,1)S(1)} %pad_maximum_fusion.4), channel_id=1, source_target_pairs={{0,1},{1,2},{2,3},{3,0},{4,5},{5,6},{6,7},{7,4},{8,9},{9,10},{10,1... | collective-permute-start | bytes 331784 | tf_op jit(solution)/shard_map/ppermute | solution.py:295
  24.5 173.2 %all-gather.5.cloned.1.call-start = ((), (), s32[]{:S(2)}) async-start(), calls=%async_computation.3 | async-start | bytes 11943936 | tf_op jit(solution)/shard_map/all_gather | solution.py:310
  24.9 10.2 %collective-permute-start.9 = (bf16[96,1728]{1,0:T(8,128)(2,1)S(1)}, bf16[96,1728]{1,0:T(8,128)(2,1)S(1)}, u32[]{:S(2)}, u32[]{:S(2)}) collective-permute-start(bf16[96,1728]{1,0:T(8,128)(2,1)S(1)} %concatenate.48), channel_id=1, source_target_pairs={{0,3},{1,0},{2,1},{3,2},{4,7},{5,4},{6,5},{7,6},{8,11},{9,8},{10,9... | collective-permute-start | bytes 995336 | tf_op jit(solution)/shard_map/ppermute | solution.py:295
  26.6 30.5 %collective-permute-start.8 = (bf16[96,1728]{1,0:T(8,128)(2,1)S(1)}, bf16[96,1728]{1,0:T(8,128)(2,1)S(1)}, u32[]{:S(2)}, u32[]{:S(2)}) collective-permute-start(bf16[96,1728]{1,0:T(8,128)(2,1)S(1)} %concatenate.48), channel_id=1, source_target_pairs={{0,2},{1,3},{2,0},{3,1},{4,6},{5,7},{6,4},{7,5},{8,10},{9,11},{10,... | collective-permute-start | bytes 995336 | tf_op jit(solution)/shard_map/ppermute | solution.py:295
  27.6 29.6 %collective-permute-start.7 = (bf16[96,1728]{1,0:T(8,128)(2,1)S(1)}, bf16[96,1728]{1,0:T(8,128)(2,1)S(1)}, u32[]{:S(2)}, u32[]{:S(2)}) collective-permute-start(bf16[96,1728]{1,0:T(8,128)(2,1)S(1)} %concatenate.48), channel_id=1, source_target_pairs={{0,1},{1,2},{2,3},{3,0},{4,5},{5,6},{6,7},{7,4},{8,9},{9,10},{10,1... | collective-permute-start | bytes 995336 | tf_op jit(solution)/shard_map/ppermute | solution.py:295
  58.7 14.0 %copy-start.33 = (s32[40]{0:T(128)S(1)}, s32[40]{0:T(128)}, u32[]{:S(2)}) copy-start(s32[40]{0:T(128)} %param.26) | copy-start | bytes 484
  60.6 22.9 %copy-start.9 = (bf16[768,768]{1,0:T(8,128)(2,1)S(1)}, bf16[768,768]{1,0:T(8,128)(2,1)}, u32[]{:S(2)}) copy-start(bf16[768,768]{1,0:T(8,128)(2,1)} %param.43) | copy-start | bytes 3538948
  60.6 360.4 %reduce-scatter.5.cloned.1.call-start = ((), (), s32[]{:S(2)}) async-start(), calls=%async_computation.4 | async-start | bytes 13713408 | tf_op jit(solution)/shard_map/reduce_scatter | solution.py:336
  60.7 36.8 %collective-permute-start.4 = (bf16[768,768]{1,0:T(8,128)(2,1)S(1)}, bf16[768,768]{1,0:T(8,128)(2,1)}, u32[]{:S(2)}, u32[]{:S(2)}) collective-permute-start(bf16[768,768]{1,0:T(8,128)(2,1)S(1)} %copy-done.5), channel_id=1, source_target_pairs={{0,1},{1,2},{2,3},{4,5},{5,6},{6,7},{8,9},{9,10},{10,11},{12,13},{... | collective-permute-start | bytes 3538952 | tf_op jit(solution)/shard_map/ppermute | solution.py:376
  63.1 37.8 %collective-permute-start.5 = (bf16[768,768]{1,0:T(8,128)(2,1)S(1)}, bf16[768,768]{1,0:T(8,128)(2,1)}, u32[]{:S(2)}, u32[]{:S(2)}) collective-permute-start(bf16[768,768]{1,0:T(8,128)(2,1)S(1)} %copy-done.5), channel_id=1, source_target_pairs={{1,0},{2,1},{3,2},{5,4},{6,5},{7,6},{9,8},{10,9},{11,10},{13,12},{... | collective-permute-start | bytes 3538952 | tf_op jit(solution)/shard_map/ppermute | solution.py:376
  65.4 30.3 %collective-permute-start.3 = (bf16[256,768]{1,0:T(8,128)(2,1)}, bf16[256,768]{1,0:T(8,128)(2,1)}, u32[]{:S(2)}, u32[]{:S(2)}) collective-permute-start(bf16[256,768]{1,0:T(8,128)(2,1)} %get-tuple-element.259), channel_id=1, source_target_pairs={{0,2},{1,3},{4,6},{5,7},{8,10},{9,11},{12,14},{13,15},{16,18},{17,... | collective-permute-start | bytes 1179656 | tf_op jit(solution)/shard_map/ppermute | solution.py:376
  71.2 38.9 %collective-permute-start.6 = (bf16[256,768]{1,0:T(8,128)(2,1)}, bf16[256,768]{1,0:T(8,128)(2,1)S(1)}, u32[]{:S(2)}, u32[]{:S(2)}) collective-permute-start(bf16[256,768]{1,0:T(8,128)(2,1)} %get-tuple-element.258), channel_id=1, source_target_pairs={{2,0},{3,1},{6,4},{7,5},{10,8},{11,9},{14,12},{15,13},{18,16},{19,... | collective-permute-start | bytes 1179656 | tf_op jit(solution)/shard_map/ppermute | solution.py:376
  308.8 306.8 %reduce-scatter.7.cloned.1.call-start = ((), (), s32[]{:S(2)}) async-start(), calls=%async_computation.5 | async-start | bytes 4423680
  509.6 34.9 %slice-start.4 = ((s8[4325376]{0:T(1024)(128)(4,1)}), s8[131072]{0:T(1024)(128)(4,1)S(1)}, s32[]{:S(2)}) async-start(s8[4325376]{0:T(1024)(128)(4,1)} %bitcast.205), calls=%async_computation.10 | async-start | bytes 262144
  511.8 32.7 %slice-start.5 = ((s8[4325376]{0:T(1024)(128)(4,1)}), s8[4194304]{0:T(1024)(128)(4,1)S(1)}, s32[]{:S(2)}) async-start(s8[4325376]{0:T(1024)(128)(4,1)} %bitcast.205), calls=%async_computation.11 | async-start | bytes 8388608
  513.4 36.0 %slice-start.2 = ((s8[4325376]{0:T(1024)(128)(4,1)}), s8[4194304]{0:T(1024)(128)(4,1)S(1)}, s32[]{:S(2)}) async-start(s8[4325376]{0:T(1024)(128)(4,1)} %bitcast.198), calls=%async_computation.8 | async-start | bytes 8388608
  515.0 59.5 %collective-permute-start.19 = (f32[96,1968]{1,0:T(8,128)}, f32[96,1968]{1,0:T(8,128)}, u32[]{:S(2)}, u32[]{:S(2)}) collective-permute-start(f32[96,1968]{1,0:T(8,128)} %get-tuple-element.180), channel_id=1, source_target_pairs={{0,3},{1,0},{2,1},{3,2},{4,7},{5,4},{6,5},{7,6},{8,11},{9,8},{10,9... | collective-permute-start | bytes 2267144 | tf_op jit(solution)/shard_map/ppermute | solution.py:354
  531.7 77.8 %collective-permute-start.18 = (f32[96,1968]{1,0:T(8,128)}, f32[96,1968]{1,0:T(8,128)}, u32[]{:S(2)}, u32[]{:S(2)}) collective-permute-start(f32[96,1968]{1,0:T(8,128)} %get-tuple-element.181), channel_id=1, source_target_pairs={{0,2},{1,3},{2,0},{3,1},{4,6},{5,7},{6,4},{7,5},{8,10},{9,11},{10,... | collective-permute-start | bytes 2267144 | tf_op jit(solution)/shard_map/ppermute | solution.py:354
  544.3 66.6 %collective-permute-start.17 = (f32[96,1968]{1,0:T(8,128)}, f32[96,1968]{1,0:T(8,128)}, u32[]{:S(2)}, u32[]{:S(2)}) collective-permute-start(f32[96,1968]{1,0:T(8,128)} %get-tuple-element.179), channel_id=1, source_target_pairs={{0,1},{1,2},{2,3},{3,0},{4,5},{5,6},{6,7},{7,4},{8,9},{9,10},{10,1... | collective-permute-start | bytes 2267144 | tf_op jit(solution)/shard_map/ppermute | solution.py:354
  558.5 92.8 %collective-permute-start.12 = (bf16[768,768]{0,1:T(8,128)(2,1)}, bf16[768,768]{0,1:T(8,128)(2,1)S(1)}, u32[]{:S(2)}, u32[]{:S(2)}) collective-permute-start(bf16[768,768]{0,1:T(8,128)(2,1)} %get-tuple-element.178), channel_id=1, source_target_pairs={{0,1},{1,2},{2,3},{4,5},{5,6},{6,7},{8,9},{9,10},{10,11},{12,13},{... | collective-permute-start | bytes 3538952 | tf_op jit(solution)/shard_map/ppermute | solution.py:376
  561.0 90.3 %collective-permute-start.10 = (bf16[768,768]{0,1:T(8,128)(2,1)}, bf16[768,768]{0,1:T(8,128)(2,1)S(1)}, u32[]{:S(2)}, u32[]{:S(2)}) collective-permute-start(bf16[768,768]{0,1:T(8,128)(2,1)} %get-tuple-element.177), channel_id=1, source_target_pairs={{1,0},{2,1},{3,2},{5,4},{6,5},{7,6},{9,8},{10,9},{11,10},{13,12},{... | collective-permute-start | bytes 3538952 | tf_op jit(solution)/shard_map/ppermute | solution.py:376
  574.5 43.9 %collective-permute-start.13 = (bf16[256,768]{0,1:T(8,128)(2,1)}, bf16[256,768]{0,1:T(8,128)(2,1)}, u32[]{:S(2)}, u32[]{:S(2)}) collective-permute-start(bf16[256,768]{0,1:T(8,128)(2,1)} %get-tuple-element.176), channel_id=1, source_target_pairs={{0,2},{1,3},{4,6},{5,7},{8,10},{9,11},{12,14},{13,15},{16,18},{17,... | collective-permute-start | bytes 1179656 | tf_op jit(solution)/shard_map/ppermute | solution.py:376
  609.6 30.3 %collective-permute-start.11 = (bf16[256,768]{0,1:T(8,128)(2,1)}, bf16[256,768]{0,1:T(8,128)(2,1)}, u32[]{:S(2)}, u32[]{:S(2)}) collective-permute-start(bf16[256,768]{0,1:T(8,128)(2,1)} %get-tuple-element.175), channel_id=1, source_target_pairs={{2,0},{3,1},{6,4},{7,5},{10,8},{11,9},{14,12},{15,13},{18,16},{19,... | collective-permute-start | bytes 1179656 | tf_op jit(solution)/shard_map/ppermute | solution.py:376
  617.2 35.1 %copy-start.4 = (f32[768,768]{0,1:T(8,128)S(1)}, f32[768,768]{0,1:T(8,128)}, u32[]{:S(2)}) copy-start(f32[768,768]{0,1:T(8,128)} %copy-done.3) | copy-start | bytes 7077892
  617.2 35.1 %copy-start.8 = (bf16[768,12,64]{0,2,1:T(8,128)(2,1)S(1)}, bf16[768,12,64]{0,2,1:T(8,128)(2,1)}, u32[]{:S(2)}) copy-start(bf16[768,12,64]{0,2,1:T(8,128)(2,1)} %copy.189) | copy-start | bytes 3538948
  617.4 34.0 %copy-start.7 = (f32[4,96,624]{1,2,0:T(8,128)}, f32[4,96,624]{1,2,0:T(8,128)S(1)}, u32[]{:S(2)}) copy-start(f32[4,96,624]{1,2,0:T(8,128)S(1)} %pad_maximum_fusion.2) | copy-start | bytes 2875396
  618.4 39.8 %collective-permute-start.16 = (f32[96,624]{0,1:T(8,128)}, f32[96,624]{0,1:T(8,128)}, u32[]{:S(2)}, u32[]{:S(2)}) collective-permute-start(f32[96,624]{0,1:T(8,128)} %get-tuple-element.236), channel_id=1, source_target_pairs={{0,3},{1,0},{2,1},{3,2},{4,7},{5,4},{6,5},{7,6},{8,11},{9,8},{10,9... | collective-permute-start | bytes 718856 | tf_op jit(solution)/shard_map/ppermute | solution.py:354
  618.4 39.8 %collective-permute-start.15 = (f32[96,624]{0,1:T(8,128)}, f32[96,624]{0,1:T(8,128)}, u32[]{:S(2)}, u32[]{:S(2)}) collective-permute-start(f32[96,624]{0,1:T(8,128)} %get-tuple-element.237), channel_id=1, source_target_pairs={{0,2},{1,3},{2,0},{3,1},{4,6},{5,7},{6,4},{7,5},{8,10},{9,11},{10,... | collective-permute-start | bytes 718856 | tf_op jit(solution)/shard_map/ppermute | solution.py:354
  639.9 24.9 %collective-permute-start.14 = (f32[96,624]{0,1:T(8,128)}, f32[96,624]{0,1:T(8,128)}, u32[]{:S(2)}, u32[]{:S(2)}) collective-permute-start(f32[96,624]{0,1:T(8,128)} %get-tuple-element.235), channel_id=1, source_target_pairs={{0,1},{1,2},{2,3},{3,0},{4,5},{5,6},{6,7},{7,4},{8,9},{9,10},{10,1... | collective-permute-start | bytes 718856 | tf_op jit(solution)/shard_map/ppermute | solution.py:354
  (36 other events, 128.6 us)
Sparse Core Ops, SparseCore 0:
  24.6 33.8 all-gather.2
  60.7 62.9 all-gather.4
  308.9 112.0 reduce-scatter.4
  499.0 86.9 reduce-scatter.6

commit v5 on v4

--- a/solution.py
+++ b/solution.py
@@ -12,12 +12,35 @@
 BLOCK = 256
 
 NEG = -1e30
-
-
-def _fwd_kernel(lo_ref, hi_ref, q_ref, k_ref, v_ref, qs_ref, ks_ref, o_ref, lse_ref, m_sc, l_sc, acc_sc):
+LANES = 128
+
+
+def _lanes(rows):
+    return lax.broadcasted_iota(jnp.int32, (rows, LANES), 1) < LANES // 2
+
+
+def _pick(first, second, lanes):
+    return jnp.where(lanes, first, second)
+
+
+def _nt(a, b):
+    return lax.dot_general(a, b, (((1,), (1,)), ((), ())), preferred_element_type=jnp.float32)
+
+
+def _tn(a, b):
+    return lax.dot_general(a, b, (((0,), (0,)), ((), ())), preferred_element_type=jnp.float32)
+
+
+def _nn(a, b):
+    return lax.dot_general(a, b, (((1,), (0,)), ((), ())), preferred_element_type=jnp.float32)
+
+
+def _attn_fwd(lo_ref, hi_ref, q_ref, k_ref, v_ref, qs_ref, ks_ref, o_ref, lse_ref, m_sc, l_sc, acc_sc):
     i = pl.program_id(0)
     j = pl.program_id(1)
     kv = lo_ref[i] + j
+    pairs = q_ref.shape[1] // LANES
+    bq = q_ref.shape[0]
 
     @pl.when(j == 0)
     def _():
@@ -27,29 +50,53 @@
 
     @pl.when(kv <= hi_ref[i])
     def _():
-        s = jnp.einsum("hqd,hkd->hqk", q_ref[...], k_ref[...], preferred_element_type=jnp.float32) * 0.125
-        mask = (qs_ref[...] == ks_ref[...])[None]
-        s = jnp.where(mask, s, NEG)
-        m_old = m_sc[...]
-        m_new = jnp.maximum(m_old, jnp.max(s, axis=-1, keepdims=True))
-        alpha = jnp.exp(m_old - m_new)
-        p = jnp.where(mask, jnp.exp(s - m_new), 0.0)
-        l_sc[...] = alpha * l_sc[...] + jnp.sum(p, axis=-1, keepdims=True)
-        acc_sc[...] = alpha * acc_sc[...] + jnp.einsum(
-            "hqk,hkd->hqd", p.astype(jnp.bfloat16), v_ref[...], preferred_element_type=jnp.float32
-        )
-        m_sc[...] = m_new
+        mask = qs_ref[...] == ks_ref[...]
+        lanes = _lanes(bq)
+
+        def pair(p, carry):
+            cols = pl.ds(pl.multiple_of(p * LANES, LANES), LANES)
+            q2 = q_ref[:, cols]
+            k2 = k_ref[:, cols]
+            v2 = v_ref[:, cols]
+            zero = jnp.zeros_like(q2)
+            alphas, pvs = [], []
+            for h in range(2):
+                hq = _pick(q2, zero, lanes) if h == 0 else _pick(zero, q2, lanes)
+                s = jnp.where(mask, _nt(hq, k2) * 0.125, NEG)
+                m_old = m_sc[2 * p + h]
+                m_new = jnp.maximum(m_old, jnp.max(s, axis=-1, keepdims=True))
+                alpha = jnp.exp(m_old - m_new)
+                e = jnp.where(mask, jnp.exp(s - m_new), 0.0)
+                l_sc[2 * p + h] = alpha * l_sc[2 * p + h] + jnp.sum(e, axis=-1, keepdims=True)
+                m_sc[2 * p + h] = m_new
+                alphas.append(alpha)
+                pvs.append(_nn(e.astype(jnp.bfloat16), v2))
+            acc_sc[:, cols] = _pick(alphas[0], alphas[1], lanes) * acc_sc[:, cols] + _pick(pvs[0], pvs[1], lanes)
+            return carry
+
+        lax.fori_loop(0, pairs, pair, 0)
 
     @pl.when(j == pl.num_programs(1) - 1)
     def _():
-        o_ref[...] = acc_sc[...] / l_sc[...]
-        lse_ref[...] = m_sc[...] + jnp.log(l_sc[...])
-
-
-def _dq_kernel(lo_ref, hi_ref, q_ref, k_ref, v_ref, qs_ref, ks_ref, lse_ref, dl_ref, do_ref, dq_ref, acc_sc):
+        lanes = _lanes(bq)
+
+        def pair(p, carry):
+            cols = pl.ds(pl.multiple_of(p * LANES, LANES), LANES)
+            l0, l1 = l_sc[2 * p], l_sc[2 * p + 1]
+            o_ref[:, cols] = acc_sc[:, cols] / _pick(l0, l1, lanes)
+            lse_ref[2 * p] = m_sc[2 * p] + jnp.log(l0)
+            lse_ref[2 * p + 1] = m_sc[2 * p + 1] + jnp.log(l1)
+            return carry
+
+        lax.fori_loop(0, pairs, pair, 0)
+
+
+def _attn_dq(lo_ref, hi_ref, q_ref, k_ref, v_ref, qs_ref, ks_ref, lse_ref, dl_ref, do_ref, dq_ref, acc_sc):
     i = pl.program_id(0)
     j = pl.program_id(1)
     kv = lo_ref[i] + j
+    pairs = q_ref.shape[1] // LANES
+    bq = q_ref.shape[0]
 
     @pl.when(j == 0)
     def _():
@@ -57,23 +104,41 @@
 
     @pl.when(kv <= hi_ref[i])
     def _():
-        k = k_ref[...]
-        s = jnp.einsum("hqd,hkd->hqk", q_ref[...], k, preferred_element_type=jnp.float32) * 0.125
-        mask = (qs_ref[...] == ks_ref[...])[None]
-        p = jnp.where(mask, jnp.exp(s - lse_ref[...]), 0.0)
-        dp = jnp.einsum("hqd,hkd->hqk", do_ref[...], v_ref[...], preferred_element_type=jnp.float32)
-        ds = (p * (dp - dl_ref[...])).astype(jnp.bfloat16)
-        acc_sc[...] += jnp.einsum("hqk,hkd->hqd", ds, k, preferred_element_type=jnp.float32)
+        mask = qs_ref[...] == ks_ref[...]
+        lanes = _lanes(bq)
+
+        def pair(p, carry):
+            cols = pl.ds(pl.multiple_of(p * LANES, LANES), LANES)
+            q2 = q_ref[:, cols]
+            k2 = k_ref[:, cols]
+            v2 = v_ref[:, cols]
+            do2 = do_ref[:, cols]
+            zero = jnp.zeros_like(q2)
+            parts = []
+            for h in range(2):
+                sel = (lambda a: _pick(a, zero, lanes)) if h == 0 else (lambda a: _pick(zero, a, lanes))
+                s = _nt(sel(q2), k2) * 0.125
+                e = jnp.where(mask, jnp.exp(s - lse_ref[2 * p + h]), 0.0)
+                dp = _nt(sel(do2), v2)
+                ds = (e * (dp - dl_ref[2 * p + h])).astype(jnp.bfloat16)
+                parts.append(_nn(ds, k2))
+            acc_sc[:, cols] += _pick(parts[0], parts[1], lanes)
+            return carry
+
+        lax.fori_loop(0, pairs, pair, 0)
 
     @pl.when(j == pl.num_programs(1) - 1)
     def _():
         dq_ref[...] = acc_sc[...] * 0.125
 
 
-def _dkv_kernel(lo_ref, hi_ref, q_ref, k_ref, v_ref, qs_ref, ks_ref, lse_ref, dl_ref, do_ref, dk_ref, dv_ref, dk_sc, dv_sc):
+def _attn_dkv(lo_ref, hi_ref, q_ref, k_ref, v_ref, qs_ref, ks_ref, lse_ref, dl_ref, do_ref, dk_ref, dv_ref, dk_sc, dv_sc):
     j = pl.program_id(0)
     i = pl.program_id(1)
     qb = lo_ref[j] + i
+    pairs = q_ref.shape[1] // LANES
+    bq = q_ref.shape[0]
+    bk = k_ref.shape[0]
 
     @pl.when(i == 0)
     def _():
@@ -82,15 +147,31 @@
 
     @pl.when(qb <= hi_ref[j])
     def _():
-        q = q_ref[...]
-        do = do_ref[...]
-        s = jnp.einsum("hqd,hkd->hqk", q, k_ref[...], preferred_element_type=jnp.float32) * 0.125
-        mask = (qs_ref[...] == ks_ref[...])[None]
-        p = jnp.where(mask, jnp.exp(s - lse_ref[...]), 0.0)
-        dp = jnp.einsum("hqd,hkd->hqk", do, v_ref[...], preferred_element_type=jnp.float32)
-        ds = (p * (dp - dl_ref[...])).astype(jnp.bfloat16)
-        dv_sc[...] += jnp.einsum("hqk,hqd->hkd", p.astype(jnp.bfloat16), do, preferred_element_type=jnp.float32)
-        dk_sc[...] += jnp.einsum("hqk,hqd->hkd", ds, q, preferred_element_type=jnp.float32)
+        mask = qs_ref[...] == ks_ref[...]
+        lanes_q = _lanes(bq)
+        lanes_k = _lanes(bk)
+
+        def pair(p, carry):
+            cols = pl.ds(pl.multiple_of(p * LANES, LANES), LANES)
+            q2 = q_ref[:, cols]
+            k2 = k_ref[:, cols]
+            v2 = v_ref[:, cols]
+            do2 = do_ref[:, cols]
+            zero = jnp.zeros_like(q2)
+            dks, dvs = [], []
+            for h in range(2):
+                sel = (lambda a: _pick(a, zero, lanes_q)) if h == 0 else (lambda a: _pick(zero, a, lanes_q))
+                s = _nt(sel(q2), k2) * 0.125
+                e = jnp.where(mask, jnp.exp(s - lse_ref[2 * p + h]), 0.0)
+                dp = _nt(sel(do2), v2)
+                ds = (e * (dp - dl_ref[2 * p + h])).astype(jnp.bfloat16)
+                dvs.append(_tn(e.astype(jnp.bfloat16), do2))
+                dks.append(_tn(ds, q2))
+            dv_sc[:, cols] += _pick(dvs[0], dvs[1], lanes_k)
+            dk_sc[:, cols] += _pick(dks[0], dks[1], lanes_k)
+            return carry
+
+        lax.fori_loop(0, pairs, pair, 0)
 
     @pl.when(i == pl.num_programs(1) - 1)
     def _():
@@ -102,130 +183,106 @@
     return jnp.minimum(start + step, jnp.maximum(last, 0))
 
 
+def _params():
+    return pltpu.CompilerParams(dimension_semantics=("arbitrary", "arbitrary"), vmem_limit_bytes=48 * 1024 * 1024)
+
+
 def flash_forward(q, k, v, q_ids, k_ids, lo, hi, block_q, block_k, steps):
-    heads, nq, hd = q.shape
-    nk = k.shape[1]
-    qs = q_ids.reshape(nq, 1)
-    ks = k_ids.reshape(1, nk)
-
-    def kv_map(i, j, lo_ref, hi_ref):
-        return (0, _clamp(lo_ref[i], j, hi_ref[i]), 0)
-
-    def ks_map(i, j, lo_ref, hi_ref):
-        return (0, _clamp(lo_ref[i], j, hi_ref[i]))
-
+    nq, width = q.shape
+    nk = k.shape[0]
+    heads = width // 64
+    kv_map = lambda i, j, a, b: (_clamp(a[i], j, b[i]), 0)
+    ks_map = lambda i, j, a, b: (0, _clamp(a[i], j, b[i]))
+    row = lambda i, j, a, b: (i, 0)
     grid_spec = pltpu.PrefetchScalarGridSpec(
         num_scalar_prefetch=2,
         grid=(nq // block_q, steps),
         in_specs=[
-            pl.BlockSpec((heads, block_q, hd), lambda i, j, a, b: (0, i, 0)),
-            pl.BlockSpec((heads, block_k, hd), kv_map),
-            pl.BlockSpec((heads, block_k, hd), kv_map),
-            pl.BlockSpec((block_q, 1), lambda i, j, a, b: (i, 0)),
+            pl.BlockSpec((block_q, width), row),
+            pl.BlockSpec((block_k, width), kv_map),
+            pl.BlockSpec((block_k, width), kv_map),
+            pl.BlockSpec((block_q, 1), row),
             pl.BlockSpec((1, block_k), ks_map),
         ],
         out_specs=[
-            pl.BlockSpec((heads, block_q, hd), lambda i, j, a, b: (0, i, 0)),
+            pl.BlockSpec((block_q, width), row),
             pl.BlockSpec((heads, block_q, 1), lambda i, j, a, b: (0, i, 0)),
         ],
         scratch_shapes=[
             pltpu.VMEM((heads, block_q, 1), jnp.float32),
             pltpu.VMEM((heads, block_q, 1), jnp.float32),
-            pltpu.VMEM((heads, block_q, hd), jnp.float32),
+            pltpu.VMEM((block_q, width), jnp.float32),
         ],
     )
     return pl.pallas_call(
-        _fwd_kernel,
+        _attn_fwd,
         grid_spec=grid_spec,
-        out_shape=[
-            jax.ShapeDtypeStruct((heads, nq, hd), jnp.float32),
-            jax.ShapeDtypeStruct((heads, nq, 1), jnp.float32),
-        ],
-        compiler_params=pltpu.CompilerParams(
-            dimension_semantics=("arbitrary", "arbitrary"), vmem_limit_bytes=100 * 1024 * 1024 // 2
-        ),
-    )(lo, hi, q, k, v, qs, ks)
+        out_shape=[jax.ShapeDtypeStruct((nq, width), jnp.float32), jax.ShapeDtypeStruct((heads, nq, 1), jnp.float32)],
+        compiler_params=_params(),
+    )(lo, hi, q, k, v, q_ids.reshape(nq, 1), k_ids.reshape(1, nk))
 
 
 def flash_dq(q, k, v, q_ids, k_ids, lse, delta, do, lo, hi, block_q, block_k, steps):
-    heads, nq, hd = q.shape
-    nk = k.shape[1]
-    qs = q_ids.reshape(nq, 1)
-    ks = k_ids.reshape(1, nk)
-
-    def kv_map(i, j, lo_ref, hi_ref):
-        return (0, _clamp(lo_ref[i], j, hi_ref[i]), 0)
-
-    def ks_map(i, j, lo_ref, hi_ref):
-        return (0, _clamp(lo_ref[i], j, hi_ref[i]))
-
-    row = lambda i, j, a, b: (0, i, 0)
+    nq, width = q.shape
+    nk = k.shape[0]
+    heads = width // 64
+    kv_map = lambda i, j, a, b: (_clamp(a[i], j, b[i]), 0)
+    ks_map = lambda i, j, a, b: (0, _clamp(a[i], j, b[i]))
+    row = lambda i, j, a, b: (i, 0)
+    hrow = lambda i, j, a, b: (0, i, 0)
     grid_spec = pltpu.PrefetchScalarGridSpec(
         num_scalar_prefetch=2,
         grid=(nq // block_q, steps),
         in_specs=[
-            pl.BlockSpec((heads, block_q, hd), row),
-            pl.BlockSpec((heads, block_k, hd), kv_map),
-            pl.BlockSpec((heads, block_k, hd), kv_map),
-            pl.BlockSpec((block_q, 1), lambda i, j, a, b: (i, 0)),
+            pl.BlockSpec((block_q, width), row),
+            pl.BlockSpec((block_k, width), kv_map),
+            pl.BlockSpec((block_k, width), kv_map),
+            pl.BlockSpec((block_q, 1), row),
             pl.BlockSpec((1, block_k), ks_map),
-            pl.BlockSpec((heads, block_q, 1), row),
-            pl.BlockSpec((heads, block_q, 1), row),
-            pl.BlockSpec((heads, block_q, hd), row),
+            pl.BlockSpec((heads, block_q, 1), hrow),
+            pl.BlockSpec((heads, block_q, 1), hrow),
+            pl.BlockSpec((block_q, width), row),
         ],
-        out_specs=pl.BlockSpec((heads, block_q, hd), row),
-        scratch_shapes=[pltpu.VMEM((heads, block_q, hd), jnp.float32)],
+        out_specs=pl.BlockSpec((block_q, width), row),
+        scratch_shapes=[pltpu.VMEM((block_q, width), jnp.float32)],
     )
     return pl.pallas_call(
-        _dq_kernel,
+        _attn_dq,
         grid_spec=grid_spec,
-        out_shape=jax.ShapeDtypeStruct((heads, nq, hd), jnp.float32),
-        compiler_params=pltpu.CompilerParams(
-            dimension_semantics=("arbitrary", "arbitrary"), vmem_limit_bytes=100 * 1024 * 1024 // 2
-        ),
-    )(lo, hi, q, k, v, qs, ks, lse, delta, do)
+        out_shape=jax.ShapeDtypeStruct((nq, width), jnp.float32),
+        compiler_params=_params(),
+    )(lo, hi, q, k, v, q_ids.reshape(nq, 1), k_ids.reshape(1, nk), lse, delta, do)
 
 
 def flash_dkv(q, k, v, q_ids, k_ids, lse, delta, do, qlo, qhi, block_q, block_k, steps):
-    heads, nq, hd = q.shape
-    nk = k.shape[1]
-    qs = q_ids.reshape(nq, 1)
-    ks = k_ids.reshape(1, nk)
-
-    def q_map(j, i, lo_ref, hi_ref):
-        return (0, _clamp(lo_ref[j], i, hi_ref[j]), 0)
-
-    def qs_map(j, i, lo_ref, hi_ref):
-        return (_clamp(lo_ref[j], i, hi_ref[j]), 0)
-
-    col = lambda j, i, a, b: (0, j, 0)
+    nq, width = q.shape
+    nk = k.shape[0]
+    heads = width // 64
+    q_map = lambda j, i, a, b: (_clamp(a[j], i, b[j]), 0)
+    h_map = lambda j, i, a, b: (0, _clamp(a[j], i, b[j]), 0)
+    col = lambda j, i, a, b: (j, 0)
     grid_spec = pltpu.PrefetchScalarGridSpec(
         num_scalar_prefetch=2,
         grid=(nk // block_k, steps),
         in_specs=[
-            pl.BlockSpec((heads, block_q, hd), q_map),
-            pl.BlockSpec((heads, block_k, hd), col),
-            pl.BlockSpec((heads, block_k, hd), col),
-            pl.BlockSpec((block_q, 1), qs_map),
+            pl.BlockSpec((block_q, width), q_map),
+            pl.BlockSpec((block_k, width), col),
+            pl.BlockSpec((block_k, width), col),
+            pl.BlockSpec((block_q, 1), q_map),
             pl.BlockSpec((1, block_k), lambda j, i, a, b: (0, j)),
-            pl.BlockSpec((heads, block_q, 1), q_map),
-            pl.BlockSpec((heads, block_q, 1), q_map),
-            pl.BlockSpec((heads, block_q, hd), q_map),
+            pl.BlockSpec((heads, block_q, 1), h_map),
+            pl.BlockSpec((heads, block_q, 1), h_map),
+            pl.BlockSpec((block_q, width), q_map),
         ],
-        out_specs=[pl.BlockSpec((heads, block_k, hd), col), pl.BlockSpec((heads, block_k, hd), col)],
-        scratch_shapes=[pltpu.VMEM((heads, block_k, hd), jnp.float32), pltpu.VMEM((heads, block_k, hd), jnp.float32)],
+        out_specs=[pl.BlockSpec((block_k, width), col), pl.BlockSpec((block_k, width), col)],
+        scratch_shapes=[pltpu.VMEM((block_k, width), jnp.float32), pltpu.VMEM((block_k, width), jnp.float32)],
     )
     return pl.pallas_call(
-        _dkv_kernel,
+        _attn_dkv,
         grid_spec=grid_spec,
-        out_shape=[
-            jax.ShapeDtypeStruct((heads, nk, hd), jnp.float32),
-            jax.ShapeDtypeStruct((heads, nk, hd), jnp.float32),
-        ],
-        compiler_params=pltpu.CompilerParams(
-            dimension_semantics=("arbitrary", "arbitrary"), vmem_limit_bytes=100 * 1024 * 1024 // 2
-        ),
-    )(qlo, qhi, q, k, v, qs, ks, lse, delta, do)
+        out_shape=[jax.ShapeDtypeStruct((nk, width), jnp.float32), jax.ShapeDtypeStruct((nk, width), jnp.float32)],
+        compiler_params=_params(),
+    )(qlo, qhi, q, k, v, q_ids.reshape(nq, 1), k_ids.reshape(1, nk), lse, delta, do)
 
 
 def block_ranges(q_ids, k_ids, q_start, q_end, block_q, block_k):
@@ -443,9 +500,8 @@
     query = (jnp.dot(x_own, wq, preferred_element_type=jnp.float32) + b_query.astype(jnp.float32)).astype(jnp.bfloat16)
     key_w = jnp.dot(x_win, wk, preferred_element_type=jnp.float32).astype(jnp.bfloat16)
     value_w = (jnp.dot(x_win, wv, preferred_element_type=jnp.float32) + b_value.astype(jnp.float32)).astype(jnp.bfloat16)
-    q_h, k_h, v_h = to_heads(query), to_heads(key_w), to_heads(value_w)
-    ctx_h, lse = flash_forward(q_h, k_h, v_h, q_ids, k_ids, lo, hi, BLOCK, BLOCK, kv_steps)
-    context = from_heads(ctx_h).astype(jnp.bfloat16)
+    ctx32, lse = flash_forward(query, key_w, value_w, q_ids, k_ids, lo, hi, BLOCK, BLOCK, kv_steps)
+    context = ctx32.astype(jnp.bfloat16)
     attn = contract_last(context, wo_t) + b_out.astype(jnp.float32)
     hidden, norm_one, inverse_one = norm_forward(tokens.astype(jnp.float32) + attn, gain_one, shift_attn.astype(jnp.float32))
     hidden_low = hidden.astype(jnp.bfloat16)
@@ -479,17 +535,18 @@
     early_widths, early_cat = pack_grads([grad_out_t, grad_inner_w, grad_outer_t], late)
     grad_context, early_cat = lax.optimization_barrier((grad_context, early_cat))
     early_strip = reduce_dp(early_cat)
-    do_h = to_heads(grad_context)
-    delta = jnp.sum(do_h.astype(jnp.float32) * ctx_h, axis=-1, keepdims=True)
-    dq_h = flash_dq(q_h, k_h, v_h, q_ids, k_ids, lse, delta, do_h, lo, hi, BLOCK, BLOCK, kv_steps)
-    dk_h, dv_h = flash_dkv(q_h, k_h, v_h, q_ids, k_ids, lse, delta, do_h, qlo, qhi, BLOCK, BLOCK, q_steps)
+    heads = query.shape[1] // HEAD_DIM
+    delta = jnp.sum((grad_context.astype(jnp.float32) * ctx32).reshape(rows, heads, HEAD_DIM), axis=-1)
+    delta = delta.T.reshape(heads, rows, 1)
+    dq_h = flash_dq(query, key_w, value_w, q_ids, k_ids, lse, delta, grad_context, lo, hi, BLOCK, BLOCK, kv_steps)
+    dk_h, dv_h = flash_dkv(query, key_w, value_w, q_ids, k_ids, lse, delta, grad_context, qlo, qhi, BLOCK, BLOCK, q_steps)
     early_strip, dq_h, dk_h, dv_h = lax.optimization_barrier((early_strip, dq_h, dk_h, dv_h))
     early_sums = reduce_tensor(early_strip, early_widths, 3)
     g_out_t, g_inner, g_outer_t = early_sums[:3]
     late = early_sums[3:]
-    grad_query = from_heads(dq_h).astype(jnp.bfloat16)
-    grad_key = from_heads(dk_h).astype(jnp.bfloat16)
-    grad_value = from_heads(dv_h).astype(jnp.bfloat16)
+    grad_query = dq_h.astype(jnp.bfloat16)
+    grad_key = dk_h.astype(jnp.bfloat16)
+    grad_value = dv_h.astype(jnp.bfloat16)
     grad_query_w = contract_first(x_own, grad_query)
     grad_key_w = contract_first(x_win, grad_key)
     grad_value_w = contract_first(x_win, grad_value)

time: 689 us -> 736 us (1.068); the launches traced: 676 us -> 732 us
  starting transfers between devices: 82.2 us -> 210 us
  waiting for transfers between devices: 122 us -> 45.5 us
  Pallas kernels: 125 us -> 173 us
  local copies, waits for them, and re-layouts: 140 us -> 106 us
  other arithmetic: 60.1 us -> 42.8 us
    ppermute x6, starting transfers between devices: 45.3 us -> 151 us  [reduce_tensor(): lax.ppermute(send, 'tensor', [(s, (s + k) % count) for s in range(count)])]
    pallas_call x3, Pallas kernels: 125 us -> 173 us  [the longest x1 70.8 us: flash_dkv(): pl.pallas_call(_attn_dkv, grid_spec=grid_spec, out_shape=[jax.ShapeDtypeS...]
    ppermute x6, waiting for transfers between devices: 41.5 us -> 0.02 us  [reduce_tensor(): lax.ppermute(send, 'tensor', [(s, (s + k) % count) for s in range(count)])]
    convert_element_type x4 -> x0, other arithmetic: 25.5 us -> none  [the longest x1 9.26 us: shards(): grad_key = from_heads(dk_h).astype(jnp.bfloat16)]
    convert_element_type x4 -> x0, local copies, waits for them, and re-layouts: 25.2 us -> none  [the longest x1 9.58 us: shards(): grad_value = from_heads(dv_h).astype(jnp.bfloat16)]
    ppermute x8, waiting for transfers between devices: 33.3 us -> 12.5 us  [shift_rows(): return lax.ppermute(values, 'tensor', pairs)]
    reshape x5 -> x2, local copies, waits for them, and re-layouts: 25.1 us -> 4.59 us  [the longest x1 3.68 us: shards(): delta = delta.T.reshape(heads, rows, 1)]
    ppermute x8, starting transfers between devices: 27.5 us -> 47.2 us  [shift_rows(): return lax.ppermute(values, 'tensor', pairs)]
  transfers between devices with their start and end apart: 24 -> 24, of which waited for: 11 -> 7; matrix products, arithmetic and copies ran while one was open for 20% -> 18% of each run, Pallas kernels for 19% -> 24%
where the time goes in v5:
time: 736 us; the launch traced here: 732 us
  starting transfers between devices  210 us (29%)
  Pallas kernels  173 us (24%)
  matrix products  139 us (19%)
  local copies, waits for them, and re-layouts  106 us (14%)
  waiting for transfers between devices  45.5 us (6%)
  other arithmetic  42.8 us (6%)
  between operations  14.9 us (2%)
    ppermute x6, starting transfers between devices, reduce_tensor(): lax.ppermute(send, 'tensor', [(s, (s + k) % count) for s in range(count)])  151 us
    pallas_call x1, Pallas kernels, flash_dkv(): pl.pallas_call(_attn_dkv, grid_spec=grid_spec, out_shape=[jax.ShapeDtypeS...  70.8 us
    pallas_call x1, Pallas kernels, flash_forward(): pl.pallas_call(_attn_fwd, grid_spec=grid_spec, out_shape=[jax.ShapeDtypeS...  60.5 us
    ppermute x8, starting transfers between devices, shift_rows(): return lax.ppermute(values, 'tensor', pairs)  47.2 us
    dot_general x6, matrix products, contract_last(): lax.dot_general(left, right, (((1,), (1,)), ((), ())), preferred_element_...  42.6 us
    pallas_call x1, Pallas kernels, flash_dq(): pl.pallas_call(_attn_dq, grid_spec=grid_spec, out_shape=jax.ShapeDtypeStr...  42.1 us
    unnamed x120, local copies, waits for them, and re-layouts  37.6 us
    dot_general x6, matrix products, contract_first(): lax.dot_general(left, right, (((0,), (0,)), ((), ())), preferred_element_...  31.3 us
  transfers between devices with their start and end apart: 24, of which 7 were waited for; matrix products, arithmetic and copies ran while one was open for 18% of the time, Pallas kernels for 24%

profile of v5, /device:TPU:4, one launch (start us, length us, event | category | flops | bytes accessed | tf_op | source)
XLA Modules:
  0.0 731.8 jit_solution(1378419067493927191)
XLA Ops:
  16.3 4.2 collective-permute-done.1
  28.6 7.7 %collective-permute-done.7 = bf16[96,1728]{1,0:T(8,128)(2,1)S(1)} collective-permute-done((bf16[96,1728]{1,0:T(8,128)(2,1)S(1)}, bf16[96,1728]{1,0:T(8,128)(2,1)S(1)}, u32[]{:S(2)}, u32[]{:S(2)}) %collective-permute-start.7) | collective-permute-done | bytes 331808 | tf_op jit(solution)/shard_map/ppermute | solution.py:352
  36.3 13.3 %collective-permute-done.8 = bf16[96,1728]{1,0:T(8,128)(2,1)S(1)} collective-permute-done((bf16[96,1728]{1,0:T(8,128)(2,1)S(1)}, bf16[96,1728]{1,0:T(8,128)(2,1)S(1)}, u32[]{:S(2)}, u32[]{:S(2)}) %collective-permute-start.8) | collective-permute-done | bytes 331808 | tf_op jit(solution)/shard_map/ppermute | solution.py:352
  53.2 10.9 %collective-permute-start.4 = (bf16[768,768]{1,0:T(8,128)(2,1)S(1)}, bf16[768,768]{1,0:T(8,128)(2,1)}, u32[]{:S(2)}, u32[]{:S(2)}) collective-permute-start(bf16[768,768]{1,0:T(8,128)(2,1)S(1)} %copy-done.16), channel_id=1, source_target_pairs={{0,1},{1,2},{2,3},{4,5},{5,6},{6,7},{8,9},{9,10},{10,11},{12,13},{... | collective-permute-start | bytes 3538952 | tf_op jit(solution)/shard_map/ppermute | solution.py:433
  66.3 4.2 collective-permute-start.3
  73.8 3.9 select_subtract_fusion
  113.7 8.0 %convolution_convert_fusion.2.k_ref = bf16[2816,768]{1,0:T(8,128)(2,1)} fusion(bf16[2816,768]{1,0:T(8,128)(2,1)} %constant_dynamic-update-slice_fusion, bf16[768,2304]{1,0:T(8,128)(2,1)S(1)} %copy-done.20), kind=kOutput, calls=%fused_computation.23 | convolution fusion | flops 3324051456 | bytes 9830400 | tf_op jit(solution)/shard_map/dot_general | solution.py:501
  121.7 7.9 %add_convert_fusion.1.v_ref = bf16[2816,768]{1,0:T(8,128)(2,1)} fusion(bf16[2816,768]{1,0:T(8,128)(2,1)} %constant_dynamic-update-slice_fusion, f32[768]{0:T(1024)S(1)} %copy-done.35, bf16[768,2304]{1,0:T(8,128)(2,1)S(1)} %copy-done.20), kind=kOutput, calls=%fused_computation.19 | convolution fusion | flops 3326214144 | bytes 9834496 | tf_op jit(solution)/shard_map/dot_general | solution.py:502
  129.6 60.5 %shard_map.314 = (f32[768,768]{1,0:T(8,128)S(1)}, f32[12,768,1]{2,1,0:T(8,128)}) custom-call(s32[3]{0:T(128)S(1)} %copy-done.6, s32[3]{0:T(128)S(1)} %fusion.78.hi_ref, bf16[768,768]{1,0:T(8,128)(2,1)S(1)} %fusion.44.q_ref, bf16[2816,768]{1,0:T(8,128)(2,1)} %convolution_convert_fusion.2.k_ref, bf16[2816,768]{1,0:T(8,128)(2,1)} %add_convert_fusion.1.v_ref, ...), custom_call_target="tpu_custom_call" | custom-call | tf_op jit(solution)/shard_map/pallas_call | solution.py:217
  194.5 30.0 %multiply_convert_fusion = (bf16[768,3072]{1,0:T(8,128)(2,1)S(1)}, f32[768,3072]{1,0:T(8,128)}, f32[768,3072]{1,0:T(8,128)}) fusion(f32[3072]{0:T(1024)S(1)} %copy-done.30, bf16[768,6912]{1,0:T(8,128)(2,1)} %all-gather.5.cloned.1.call-done, f32[768,768]{0,1:T(8,128)S(1)} %get-tuple-element.294, f32[768]{0:T(1024)S(1)} %copy-done.33, f32[768]{0:T(1024)S(1)} %copy-done.27, ...), kind=kOutput, calls=%fused_computation.5 | convolution fusion | flops 3782541312 | bytes 30695424 | tf_op jit(solution)/shard_map/dot_general | solution.py:508
  224.5 6.0 fusion.103
  236.2 5.6 convolution_convert_fusion
  241.8 13.7 %fusion.104 = (bf16[3072]{0:T(1024)(128)(2,1)}, bf16[768,3072]{1,0:T(8,128)(2,1)S(1)}) fusion(f32[768,3072]{1,0:T(8,128)} %get-tuple-element.167, bf16[768,768]{0,1:T(8,128)(2,1)S(1)} %get-tuple-element.163, bf16[768,6912]{1,0:T(8,128)(2,1)} %all-gather.5.cloned.1.call-done, f32[768,3072]{1,0:T(8,128)} %get-tuple-element.295, f32[3072]{0:T(1024)S(1)} %copy-done.30), kind=kOutput, calls=%fused_computation.265 | convolution fusion | flops 3661624320 | bytes 29509632 | tf_op jit(solution)/shard_map/dot_general | solution.py:517
  255.5 5.8 convolution_convert_fusion.1
  261.3 7.9 %multiply_reduce_fusion = (bf16[768]{0:T(1024)(128)(2,1)}, f32[768]{0:T(1024)S(1)}, f32[768]{0:T(1024)S(1)}, bf16[768]{0:T(1024)(128)(2,1)}, f32[768,768]{0,1:T(8,128)S(1)}) fusion(f32[768,768]{0,1:T(8,128)S(1)} %get-tuple-element.294, f32[768]{0:T(1024)S(1)} %add_rsqrt_fusion.1, f32[768]{0:T(1024)S(1)} %broadcast_multiply_fusion.5, ...), kind=kOutput, calls=%fused_computation.48 | convolution fusion | flops 3634492416 | bytes 17728512 | tf_op jit(solution)/shard_map/dot_general | solution.py:325
  283.9 17.8 %concatenate.50 = bf16[768,7872]{1,0:T(8,128)(2,1)} concatenate(bf16[768,768]{1,0:T(8,128)(2,1)S(1)} %copy.159, bf16[768,3072]{1,0:T(8,128)(2,1)} %convolution_convert_fusion.1, bf16[768,3072]{1,0:T(8,128)(2,1)} %convolution_convert_fusion, bf16[768,96]{1,0:T(8,128)(2,1)S(1)} %bitcast.168, bf16[768,384]{1,0:T(8,128)(2,1)S(1)} %bitcast.165, bf16[768,96]{1,0:T(8,128)(2,1)} %bitcast.171, ...), dimensions={1} | concatenate | bytes 24182784 | tf_op jit(solution)/shard_map/concatenate | solution.py:388
  312.4 3.7 copy.162.dl_ref
  320.4 42.1 %shard_map.315 = f32[768,768]{1,0:T(8,128)S(1)} custom-call(s32[3]{0:T(128)S(1)} %copy-done.7, s32[3]{0:T(128)S(1)} %fusion.78.hi_ref, bf16[768,768]{1,0:T(8,128)(2,1)S(1)} %fusion.44.q_ref, bf16[2816,768]{1,0:T(8,128)(2,1)} %convolution_convert_fusion.2.k_ref, bf16[2816,768]{1,0:T(8,128)(2,1)} %add_convert_fusion.1.v_ref, s32[768,1]{1,0:T(8,128)S(1)} %copy-done.5, ...), custom_call_target="tpu_custom_call" | custom-call | tf_op jit(solution)/shard_map/pallas_call | solution.py:249
  362.6 70.8 %shard_map.316 = (f32[2816,768]{1,0:T(8,128)}, f32[2816,768]{1,0:T(8,128)}) custom-call(s32[11]{0:T(128)S(1)} %copy-done.9, s32[11]{0:T(128)S(1)} %copy-done.8, bf16[768,768]{1,0:T(8,128)(2,1)S(1)} %fusion.44.q_ref, bf16[2816,768]{1,0:T(8,128)(2,1)} %convolution_convert_fusion.2.k_ref, bf16[2816,768]{1,0:T(8,128)(2,1)} %add_convert_fusion.1.v_ref, ...), custom_call_target="tpu_custom_call" | custom-call | tf_op jit(solution)/shard_map/pallas_call | solution.py:280
  433.4 6.1 reduce-scatter.5.cloned.1.call-done
  447.2 7.0 fusion.40
  454.2 7.0 fusion.43
  463.6 6.5 copy.182
  492.8 102.6 %collective-permute-start.18 = (f32[96,1968]{1,0:T(8,128)S(1)}, f32[96,1968]{1,0:T(8,128)}, u32[]{:S(2)}, u32[]{:S(2)}) collective-permute-start(f32[96,1968]{1,0:T(8,128)S(1)} %get-tuple-element.181), channel_id=1, source_target_pairs={{0,2},{1,3},{2,0},{3,1},{4,6},{5,7},{6,4},{7,5},{8,10},{9,11},{10,... | collective-permute-start | bytes 2267144 | tf_op jit(solution)/shard_map/ppermute | solution.py:411
  598.3 10.8 %fusion.29 = f32[2816,768]{0,1:T(8,128)} fusion(f32[2816,768]{1,0:T(8,128)} %get-tuple-element.37, bf16[768,2304]{1,0:T(8,128)(2,1)} %all-gather.3.cloned.1.call-done), kind=kOutput, calls=%fused_computation.62 | convolution fusion | flops 3324051456 | bytes 18481152 | tf_op jit(solution)/shard_map/dot_general | solution.py:325
  609.1 8.8 %fusion.105 = (bf16[2816,768]{0,1:T(8,128)(2,1)S(1)}, f32[2816,768]{0,1:T(8,128)}) fusion(f32[2816,768]{0,1:T(8,128)} %fusion.29, bf16[768,2304]{1,0:T(8,128)(2,1)} %all-gather.3.cloned.1.call-done, f32[2816,768]{1,0:T(8,128)S(1)} %bitcast.159), kind=kOutput, calls=%fused_computation.266 | convolution fusion | flops 3328376832 | bytes 31457280 | tf_op jit(solution)/shard_map/dot_general | solution.py:325
  620.7 5.6 collective-permute-start.12
  628.6 21.1 %collective-permute-start.13 = (bf16[256,768]{0,1:T(8,128)(2,1)}, bf16[256,768]{0,1:T(8,128)(2,1)}, u32[]{:S(2)}, u32[]{:S(2)}) collective-permute-start(bf16[256,768]{0,1:T(8,128)(2,1)} %get-tuple-element.176), channel_id=1, source_target_pairs={{0,2},{1,3},{4,6},{5,7},{8,10},{9,11},{12,14},{13,15},{16,18},{17,... | collective-permute-start | bytes 1179656 | tf_op jit(solution)/shard_map/ppermute | solution.py:433
  658.3 24.7 %collective-permute-start.14 = (f32[96,624]{0,1:T(8,128)}, f32[96,624]{0,1:T(8,128)S(1)}, u32[]{:S(2)}, u32[]{:S(2)}) collective-permute-start(f32[96,624]{0,1:T(8,128)} %get-tuple-element.235), channel_id=1, source_target_pairs={{0,1},{1,2},{2,3},{3,0},{4,5},{5,6},{6,7},{7,4},{8,9},{9,10},{10,1... | collective-permute-start | bytes 718856 | tf_op jit(solution)/shard_map/ppermute | solution.py:411
  683.0 9.6 %collective-permute-done.11 = bf16[256,768]{0,1:T(8,128)(2,1)} collective-permute-done((bf16[256,768]{0,1:T(8,128)(2,1)}, bf16[256,768]{0,1:T(8,128)(2,1)}, u32[]{:S(2)}, u32[]{:S(2)}) %collective-permute-start.11) | collective-permute-done | bytes 393248 | tf_op jit(solution)/shard_map/ppermute | solution.py:433
  692.6 19.7 %collective-permute-start.16 = (f32[96,624]{0,1:T(8,128)S(1)}, f32[96,624]{0,1:T(8,128)}, u32[]{:S(2)}, u32[]{:S(2)}) collective-permute-start(f32[96,624]{0,1:T(8,128)S(1)} %get-tuple-element.236), channel_id=1, source_target_pairs={{0,3},{1,0},{2,1},{3,2},{4,7},{5,4},{6,5},{7,6},{8,11},{9,8},{10,9... | collective-permute-start | bytes 718856 | tf_op jit(solution)/shard_map/ppermute | solution.py:411
  712.3 5.5 fusion.26
  (277 shorter events, 157.7 us)
Async XLA Ops:
  7.2 103.9 %all-gather.3.cloned.1.call-start = ((), (), s32[]{:S(2)}) async-start(), calls=%async_computation.2 | async-start | bytes 3981312 | tf_op jit(solution)/shard_map/all_gather | solution.py:367
  8.2 8.1 %collective-permute-start = (bf16[96,576]{1,0:T(8,128)(2,1)S(1)}, bf16[96,576]{1,0:T(8,128)(2,1)S(1)}, u32[]{:S(2)}, u32[]{:S(2)}) collective-permute-start(bf16[96,576]{1,0:T(8,128)(2,1)S(1)} %pad_maximum_fusion.4), channel_id=1, source_target_pairs={{0,1},{1,2},{2,3},{3,0},{4,5},{5,6},{6,7},{7,4},{8,9},{9,10},{10,1... | collective-permute-start | bytes 331784 | tf_op jit(solution)/shard_map/ppermute | solution.py:352
  9.8 10.7 %collective-permute-start.1 = (bf16[96,576]{1,0:T(8,128)(2,1)S(1)}, bf16[96,576]{1,0:T(8,128)(2,1)S(1)}, u32[]{:S(2)}, u32[]{:S(2)}) collective-permute-start(bf16[96,576]{1,0:T(8,128)(2,1)S(1)} %pad_maximum_fusion.4), channel_id=1, source_target_pairs={{0,2},{1,3},{2,0},{3,1},{4,6},{5,7},{6,4},{7,5},{8,10},{9,11},{10,... | collective-permute-start | bytes 331784 | tf_op jit(solution)/shard_map/ppermute | solution.py:352
  12.4 8.1 %collective-permute-start.2 = (bf16[96,576]{1,0:T(8,128)(2,1)S(1)}, bf16[96,576]{1,0:T(8,128)(2,1)S(1)}, u32[]{:S(2)}, u32[]{:S(2)}) collective-permute-start(bf16[96,576]{1,0:T(8,128)(2,1)S(1)} %pad_maximum_fusion.4), channel_id=1, source_target_pairs={{0,3},{1,0},{2,1},{3,2},{4,7},{5,4},{6,5},{7,6},{8,11},{9,8},{10,9... | collective-permute-start | bytes 331784 | tf_op jit(solution)/shard_map/ppermute | solution.py:352
  22.6 167.5 %all-gather.5.cloned.1.call-start = ((), (), s32[]{:S(2)}) async-start(), calls=%async_computation.3 | async-start | bytes 11943936 | tf_op jit(solution)/shard_map/all_gather | solution.py:367
  23.0 13.3 %collective-permute-start.7 = (bf16[96,1728]{1,0:T(8,128)(2,1)S(1)}, bf16[96,1728]{1,0:T(8,128)(2,1)S(1)}, u32[]{:S(2)}, u32[]{:S(2)}) collective-permute-start(bf16[96,1728]{1,0:T(8,128)(2,1)S(1)} %concatenate.48), channel_id=1, source_target_pairs={{0,1},{1,2},{2,3},{3,0},{4,5},{5,6},{6,7},{7,4},{8,9},{9,10},{10,1... | collective-permute-start | bytes 995336 | tf_op jit(solution)/shard_map/ppermute | solution.py:352
  26.2 23.5 %collective-permute-start.8 = (bf16[96,1728]{1,0:T(8,128)(2,1)S(1)}, bf16[96,1728]{1,0:T(8,128)(2,1)S(1)}, u32[]{:S(2)}, u32[]{:S(2)}) collective-permute-start(bf16[96,1728]{1,0:T(8,128)(2,1)S(1)} %concatenate.48), channel_id=1, source_target_pairs={{0,2},{1,3},{2,0},{3,1},{4,6},{5,7},{6,4},{7,5},{8,10},{9,11},{10,... | collective-permute-start | bytes 995336 | tf_op jit(solution)/shard_map/ppermute | solution.py:352
  27.8 21.8 %collective-permute-start.9 = (bf16[96,1728]{1,0:T(8,128)(2,1)S(1)}, bf16[96,1728]{1,0:T(8,128)(2,1)S(1)}, u32[]{:S(2)}, u32[]{:S(2)}) collective-permute-start(bf16[96,1728]{1,0:T(8,128)(2,1)S(1)} %concatenate.48), channel_id=1, source_target_pairs={{0,3},{1,0},{2,1},{3,2},{4,7},{5,4},{6,5},{7,6},{8,11},{9,8},{10,9... | collective-permute-start | bytes 995336 | tf_op jit(solution)/shard_map/ppermute | solution.py:352
  53.1 42.5 %copy-start.18 = (bf16[768,768]{1,0:T(8,128)(2,1)S(1)}, bf16[768,768]{1,0:T(8,128)(2,1)}, u32[]{:S(2)}) copy-start(bf16[768,768]{1,0:T(8,128)(2,1)} %param.43) | copy-start | bytes 3538948
  53.1 386.4 %reduce-scatter.5.cloned.1.call-start = ((), (), s32[]{:S(2)}) async-start(), calls=%async_computation.4 | async-start | bytes 13713408 | tf_op jit(solution)/shard_map/reduce_scatter | solution.py:393
  53.2 48.7 %collective-permute-start.4 = (bf16[768,768]{1,0:T(8,128)(2,1)S(1)}, bf16[768,768]{1,0:T(8,128)(2,1)}, u32[]{:S(2)}, u32[]{:S(2)}) collective-permute-start(bf16[768,768]{1,0:T(8,128)(2,1)S(1)} %copy-done.16), channel_id=1, source_target_pairs={{0,1},{1,2},{2,3},{4,5},{5,6},{6,7},{8,9},{9,10},{10,11},{12,13},{... | collective-permute-start | bytes 3538952 | tf_op jit(solution)/shard_map/ppermute | solution.py:433
  64.1 41.3 %collective-permute-start.5 = (bf16[768,768]{1,0:T(8,128)(2,1)S(1)}, bf16[768,768]{1,0:T(8,128)(2,1)S(1)}, u32[]{:S(2)}, u32[]{:S(2)}) collective-permute-start(bf16[768,768]{1,0:T(8,128)(2,1)S(1)} %copy-done.16), channel_id=1, source_target_pairs={{1,0},{2,1},{3,2},{5,4},{6,5},{7,6},{9,8},{10,9},{11,10},{13,12},{... | collective-permute-start | bytes 3538952 | tf_op jit(solution)/shard_map/ppermute | solution.py:433
  66.3 33.7 %collective-permute-start.3 = (bf16[256,768]{1,0:T(8,128)(2,1)}, bf16[256,768]{1,0:T(8,128)(2,1)}, u32[]{:S(2)}, u32[]{:S(2)}) collective-permute-start(bf16[256,768]{1,0:T(8,128)(2,1)} %get-tuple-element.259), channel_id=1, source_target_pairs={{0,2},{1,3},{4,6},{5,7},{8,10},{9,11},{12,14},{13,15},{16,18},{17,... | collective-permute-start | bytes 1179656 | tf_op jit(solution)/shard_map/ppermute | solution.py:433
  70.6 38.8 %collective-permute-start.6 = (bf16[256,768]{1,0:T(8,128)(2,1)}, bf16[256,768]{1,0:T(8,128)(2,1)}, u32[]{:S(2)}, u32[]{:S(2)}) collective-permute-start(bf16[256,768]{1,0:T(8,128)(2,1)} %get-tuple-element.258), channel_id=1, source_target_pairs={{2,0},{3,1},{6,4},{7,5},{10,8},{11,9},{14,12},{15,13},{18,16},{19,... | collective-permute-start | bytes 1179656 | tf_op jit(solution)/shard_map/ppermute | solution.py:433
  190.1 80.6 %copy-start.3 = (f32[768,768]{1,0:T(8,128)}, f32[768,768]{1,0:T(8,128)S(1)}, u32[]{:S(2)}) copy-start(f32[768,768]{1,0:T(8,128)S(1)} %get-tuple-element.30) | copy-start | bytes 7077892
  194.5 30.1 %copy-start.34 = (f32[768]{0:T(1024)S(1)}, f32[768]{0:T(1024)}, u32[]{:S(2)}) copy-start(f32[768]{0:T(1024)} %convert_element_type.206) | copy-start | bytes 9220
  304.9 349.8 %reduce-scatter.7.cloned.1.call-start = ((), (), s32[]{:S(2)}) async-start(), calls=%async_computation.5 | async-start | bytes 4423680
  320.4 42.1 %copy-start.2 = (bf16[768,768]{1,0:T(8,128)(2,1)S(1)}, bf16[768,768]{1,0:T(8,128)(2,1)}, u32[]{:S(2)}) copy-start(bf16[768,768]{1,0:T(8,128)(2,1)} %copy-done) | copy-start | bytes 3538948
  320.4 42.1 %copy-start.8 = (s32[11]{0:T(128)S(1)}, s32[11]{0:T(128)}, u32[]{:S(2)}) copy-start(s32[11]{0:T(128)} %get-tuple-element.160.hi_ref) | copy-start | bytes 136
  320.4 42.2 %copy-start.9 = (s32[11]{0:T(128)S(1)}, s32[11]{0:T(128)}, u32[]{:S(2)}) copy-start(s32[11]{0:T(128)} %get-tuple-element.161.lo_ref) | copy-start | bytes 136
  489.3 119.8 %slice-start = ((s8[8650752]{0:T(1024)(128)(4,1)}), s8[4194304]{0:T(1024)(128)(4,1)S(1)}, s32[]{:S(2)}) async-start(s8[8650752]{0:T(1024)(128)(4,1)} %bitcast.158), calls=%async_computation.6 | async-start | bytes 8388608
  491.3 136.0 %collective-permute-start.17 = (f32[96,1968]{1,0:T(8,128)}, f32[96,1968]{1,0:T(8,128)}, u32[]{:S(2)}, u32[]{:S(2)}) collective-permute-start(f32[96,1968]{1,0:T(8,128)} %get-tuple-element.179), channel_id=1, source_target_pairs={{0,1},{1,2},{2,3},{3,0},{4,5},{5,6},{6,7},{7,4},{8,9},{9,10},{10,1... | collective-permute-start | bytes 2267144 | tf_op jit(solution)/shard_map/ppermute | solution.py:411
  492.8 135.8 %collective-permute-start.18 = (f32[96,1968]{1,0:T(8,128)S(1)}, f32[96,1968]{1,0:T(8,128)}, u32[]{:S(2)}, u32[]{:S(2)}) collective-permute-start(f32[96,1968]{1,0:T(8,128)S(1)} %get-tuple-element.181), channel_id=1, source_target_pairs={{0,2},{1,3},{2,0},{3,1},{4,6},{5,7},{6,4},{7,5},{8,10},{9,11},{10,... | collective-permute-start | bytes 2267144 | tf_op jit(solution)/shard_map/ppermute | solution.py:411
  595.4 54.4 %collective-permute-start.19 = (f32[96,1968]{1,0:T(8,128)S(1)}, f32[96,1968]{1,0:T(8,128)}, u32[]{:S(2)}, u32[]{:S(2)}) collective-permute-start(f32[96,1968]{1,0:T(8,128)S(1)} %get-tuple-element.180), channel_id=1, source_target_pairs={{0,3},{1,0},{2,1},{3,2},{4,7},{5,4},{6,5},{7,6},{8,11},{9,8},{10,9... | collective-permute-start | bytes 2267144 | tf_op jit(solution)/shard_map/ppermute | solution.py:411
  619.5 92.8 %collective-permute-start.10 = (bf16[768,768]{0,1:T(8,128)(2,1)}, bf16[768,768]{0,1:T(8,128)(2,1)}, u32[]{:S(2)}, u32[]{:S(2)}) collective-permute-start(bf16[768,768]{0,1:T(8,128)(2,1)} %get-tuple-element.177), channel_id=1, source_target_pairs={{1,0},{2,1},{3,2},{5,4},{6,5},{7,6},{9,8},{10,9},{11,10},{13,12},{... | collective-permute-start | bytes 3538952 | tf_op jit(solution)/shard_map/ppermute | solution.py:433
  620.7 91.6 %collective-permute-start.12 = (bf16[768,768]{0,1:T(8,128)(2,1)}, bf16[768,768]{0,1:T(8,128)(2,1)}, u32[]{:S(2)}, u32[]{:S(2)}) collective-permute-start(bf16[768,768]{0,1:T(8,128)(2,1)} %get-tuple-element.178), channel_id=1, source_target_pairs={{0,1},{1,2},{2,3},{4,5},{5,6},{6,7},{8,9},{9,10},{10,11},{12,13},{... | collective-permute-start | bytes 3538952 | tf_op jit(solution)/shard_map/ppermute | solution.py:433
  627.3 65.3 %collective-permute-start.11 = (bf16[256,768]{0,1:T(8,128)(2,1)}, bf16[256,768]{0,1:T(8,128)(2,1)}, u32[]{:S(2)}, u32[]{:S(2)}) collective-permute-start(bf16[256,768]{0,1:T(8,128)(2,1)} %get-tuple-element.175), channel_id=1, source_target_pairs={{2,0},{3,1},{6,4},{7,5},{10,8},{11,9},{14,12},{15,13},{18,16},{19,... | collective-permute-start | bytes 1179656 | tf_op jit(solution)/shard_map/ppermute | solution.py:433
  628.6 64.0 %collective-permute-start.13 = (bf16[256,768]{0,1:T(8,128)(2,1)}, bf16[256,768]{0,1:T(8,128)(2,1)}, u32[]{:S(2)}, u32[]{:S(2)}) collective-permute-start(bf16[256,768]{0,1:T(8,128)(2,1)} %get-tuple-element.176), channel_id=1, source_target_pairs={{0,2},{1,3},{4,6},{5,7},{8,10},{9,11},{12,14},{13,15},{16,18},{17,... | collective-permute-start | bytes 1179656 | tf_op jit(solution)/shard_map/ppermute | solution.py:433
  656.4 56.0 %copy-start.12 = (f32[768,768]{0,1:T(8,128)S(1)}, f32[768,768]{0,1:T(8,128)}, u32[]{:S(2)}) copy-start(f32[768,768]{0,1:T(8,128)} %copy-done.11) | copy-start | bytes 7077892
  658.3 62.5 %collective-permute-start.14 = (f32[96,624]{0,1:T(8,128)}, f32[96,624]{0,1:T(8,128)S(1)}, u32[]{:S(2)}, u32[]{:S(2)}) collective-permute-start(f32[96,624]{0,1:T(8,128)} %get-tuple-element.235), channel_id=1, source_target_pairs={{0,1},{1,2},{2,3},{3,0},{4,5},{5,6},{6,7},{7,4},{8,9},{9,10},{10,1... | collective-permute-start | bytes 718856 | tf_op jit(solution)/shard_map/ppermute | solution.py:411
  692.6 28.2 %collective-permute-start.15 = (f32[96,624]{0,1:T(8,128)S(1)}, f32[96,624]{0,1:T(8,128)}, u32[]{:S(2)}, u32[]{:S(2)}) collective-permute-start(f32[96,624]{0,1:T(8,128)S(1)} %get-tuple-element.237), channel_id=1, source_target_pairs={{0,2},{1,3},{2,0},{3,1},{4,6},{5,7},{6,4},{7,5},{8,10},{9,11},{10,... | collective-permute-start | bytes 718856 | tf_op jit(solution)/shard_map/ppermute | solution.py:411
  692.6 28.2 %collective-permute-start.16 = (f32[96,624]{0,1:T(8,128)S(1)}, f32[96,624]{0,1:T(8,128)}, u32[]{:S(2)}, u32[]{:S(2)}) collective-permute-start(f32[96,624]{0,1:T(8,128)S(1)} %get-tuple-element.236), channel_id=1, source_target_pairs={{0,3},{1,0},{2,1},{3,2},{4,7},{5,4},{6,5},{7,6},{8,11},{9,8},{10,9... | collective-permute-start | bytes 718856 | tf_op jit(solution)/shard_map/ppermute | solution.py:411
  (41 other events, 201.6 us)
Sparse Core Ops, SparseCore 0:
  22.7 35.4 all-gather.2
  60.1 63.3 all-gather.4
  305.0 134.4 reduce-scatter.4
  470.2 150.3 reduce-scatter.6

commit v6 on v5

--- a/solution.py
+++ b/solution.py
@@ -54,7 +54,7 @@
         lanes = _lanes(bq)
 
         def pair(p, carry):
-            cols = pl.ds(pl.multiple_of(p * LANES, LANES), LANES)
+            cols = pl.ds(p * LANES, LANES)
             q2 = q_ref[:, cols]
             k2 = k_ref[:, cols]
             v2 = v_ref[:, cols]
@@ -62,11 +62,11 @@
             alphas, pvs = [], []
             for h in range(2):
                 hq = _pick(q2, zero, lanes) if h == 0 else _pick(zero, q2, lanes)
-                s = jnp.where(mask, _nt(hq, k2) * 0.125, NEG)
+                s = jnp.where(mask, _nt(hq, k2), NEG)
                 m_old = m_sc[2 * p + h]
                 m_new = jnp.maximum(m_old, jnp.max(s, axis=-1, keepdims=True))
                 alpha = jnp.exp(m_old - m_new)
-                e = jnp.where(mask, jnp.exp(s - m_new), 0.0)
+                e = jnp.exp(s - m_new)
                 l_sc[2 * p + h] = alpha * l_sc[2 * p + h] + jnp.sum(e, axis=-1, keepdims=True)
                 m_sc[2 * p + h] = m_new
                 alphas.append(alpha)
@@ -74,21 +74,23 @@
             acc_sc[:, cols] = _pick(alphas[0], alphas[1], lanes) * acc_sc[:, cols] + _pick(pvs[0], pvs[1], lanes)
             return carry
 
-        lax.fori_loop(0, pairs, pair, 0)
+        for p in range(pairs):
+            pair(p, 0)
 
     @pl.when(j == pl.num_programs(1) - 1)
     def _():
         lanes = _lanes(bq)
 
         def pair(p, carry):
-            cols = pl.ds(pl.multiple_of(p * LANES, LANES), LANES)
+            cols = pl.ds(p * LANES, LANES)
             l0, l1 = l_sc[2 * p], l_sc[2 * p + 1]
             o_ref[:, cols] = acc_sc[:, cols] / _pick(l0, l1, lanes)
             lse_ref[2 * p] = m_sc[2 * p] + jnp.log(l0)
             lse_ref[2 * p + 1] = m_sc[2 * p + 1] + jnp.log(l1)
             return carry
 
-        lax.fori_loop(0, pairs, pair, 0)
+        for p in range(pairs):
+            pair(p, 0)
 
 
 def _attn_dq(lo_ref, hi_ref, q_ref, k_ref, v_ref, qs_ref, ks_ref, lse_ref, dl_ref, do_ref, dq_ref, acc_sc):
@@ -108,7 +110,7 @@
         lanes = _lanes(bq)
 
         def pair(p, carry):
-            cols = pl.ds(pl.multiple_of(p * LANES, LANES), LANES)
+            cols = pl.ds(p * LANES, LANES)
             q2 = q_ref[:, cols]
             k2 = k_ref[:, cols]
             v2 = v_ref[:, cols]
@@ -117,7 +119,7 @@
             parts = []
             for h in range(2):
                 sel = (lambda a: _pick(a, zero, lanes)) if h == 0 else (lambda a: _pick(zero, a, lanes))
-                s = _nt(sel(q2), k2) * 0.125
+                s = _nt(sel(q2), k2)
                 e = jnp.where(mask, jnp.exp(s - lse_ref[2 * p + h]), 0.0)
                 dp = _nt(sel(do2), v2)
                 ds = (e * (dp - dl_ref[2 * p + h])).astype(jnp.bfloat16)
@@ -125,7 +127,8 @@
             acc_sc[:, cols] += _pick(parts[0], parts[1], lanes)
             return carry
 
-        lax.fori_loop(0, pairs, pair, 0)
+        for p in range(pairs):
+            pair(p, 0)
 
     @pl.when(j == pl.num_programs(1) - 1)
     def _():
@@ -152,7 +155,7 @@
         lanes_k = _lanes(bk)
 
         def pair(p, carry):
-            cols = pl.ds(pl.multiple_of(p * LANES, LANES), LANES)
+            cols = pl.ds(p * LANES, LANES)
             q2 = q_ref[:, cols]
             k2 = k_ref[:, cols]
             v2 = v_ref[:, cols]
@@ -161,7 +164,7 @@
             dks, dvs = [], []
             for h in range(2):
                 sel = (lambda a: _pick(a, zero, lanes_q)) if h == 0 else (lambda a: _pick(zero, a, lanes_q))
-                s = _nt(sel(q2), k2) * 0.125
+                s = _nt(sel(q2), k2)
                 e = jnp.where(mask, jnp.exp(s - lse_ref[2 * p + h]), 0.0)
                 dp = _nt(sel(do2), v2)
                 ds = (e * (dp - dl_ref[2 * p + h])).astype(jnp.bfloat16)
@@ -171,11 +174,12 @@
             dk_sc[:, cols] += _pick(dks[0], dks[1], lanes_k)
             return carry
 
-        lax.fori_loop(0, pairs, pair, 0)
+        for p in range(pairs):
+            pair(p, 0)
 
     @pl.when(i == pl.num_programs(1) - 1)
     def _():
-        dk_ref[...] = dk_sc[...] * 0.125
+        dk_ref[...] = dk_sc[...]
         dv_ref[...] = dv_sc[...]
 
 
@@ -500,7 +504,8 @@
     query = (jnp.dot(x_own, wq, preferred_element_type=jnp.float32) + b_query.astype(jnp.float32)).astype(jnp.bfloat16)
     key_w = jnp.dot(x_win, wk, preferred_element_type=jnp.float32).astype(jnp.bfloat16)
     value_w = (jnp.dot(x_win, wv, preferred_element_type=jnp.float32) + b_value.astype(jnp.float32)).astype(jnp.bfloat16)
-    ctx32, lse = flash_forward(query, key_w, value_w, q_ids, k_ids, lo, hi, BLOCK, BLOCK, kv_steps)
+    scaled = query * jnp.asarray(1.0 / math.sqrt(HEAD_DIM), jnp.bfloat16)
+    ctx32, lse = flash_forward(scaled, key_w, value_w, q_ids, k_ids, lo, hi, BLOCK, BLOCK, kv_steps)
     context = ctx32.astype(jnp.bfloat16)
     attn = contract_last(context, wo_t) + b_out.astype(jnp.float32)
     hidden, norm_one, inverse_one = norm_forward(tokens.astype(jnp.float32) + attn, gain_one, shift_attn.astype(jnp.float32))
@@ -538,8 +543,8 @@
     heads = query.shape[1] // HEAD_DIM
     delta = jnp.sum((grad_context.astype(jnp.float32) * ctx32).reshape(rows, heads, HEAD_DIM), axis=-1)
     delta = delta.T.reshape(heads, rows, 1)
-    dq_h = flash_dq(query, key_w, value_w, q_ids, k_ids, lse, delta, grad_context, lo, hi, BLOCK, BLOCK, kv_steps)
-    dk_h, dv_h = flash_dkv(query, key_w, value_w, q_ids, k_ids, lse, delta, grad_context, qlo, qhi, BLOCK, BLOCK, q_steps)
+    dq_h = flash_dq(scaled, key_w, value_w, q_ids, k_ids, lse, delta, grad_context, lo, hi, BLOCK, BLOCK, kv_steps)
+    dk_h, dv_h = flash_dkv(scaled, key_w, value_w, q_ids, k_ids, lse, delta, grad_context, qlo, qhi, BLOCK, BLOCK, q_steps)
     early_strip, dq_h, dk_h, dv_h = lax.optimization_barrier((early_strip, dq_h, dk_h, dv_h))
     early_sums = reduce_tensor(early_strip, early_widths, 3)
     g_out_t, g_inner, g_outer_t = early_sums[:3]

time: 736 us -> 685 us (0.931)
  the two profiles are of different devices: /device:TPU:4 before, /device:TPU:2 now
where the time goes in v6:
time: 685 us
  starting transfers between devices  185 us (27%)
  Pallas kernels  141 us (21%)
  matrix products  139 us (20%)
  local copies, waits for them, and re-layouts  106 us (15%)
  waiting for transfers between devices  56.2 us (8%)
  other arithmetic  42.8 us (6%)
  between operations  14.9 us (2%)
    ppermute x6, starting transfers between devices, reduce_tensor(): lax.ppermute(send, 'tensor', [(s, (s + k) % count) for s in range(count)])  122 us
    pallas_call x1, Pallas kernels, flash_dkv(): pl.pallas_call(_attn_dkv, grid_spec=grid_spec, out_shape=[jax.ShapeDtypeS...  60.7 us
    ppermute x8, starting transfers between devices, shift_rows(): return lax.ppermute(values, 'tensor', pairs)  52.1 us
    pallas_call x1, Pallas kernels, flash_forward(): pl.pallas_call(_attn_fwd, grid_spec=grid_spec, out_shape=[jax.ShapeDtypeS...  47.4 us
    dot_general x6, matrix products, contract_last(): lax.dot_general(left, right, (((1,), (1,)), ((), ())), preferred_element_...  42.7 us
    unnamed x120, local copies, waits for them, and re-layouts  37.4 us
    pallas_call x1, Pallas kernels, flash_dq(): pl.pallas_call(_attn_dq, grid_spec=grid_spec, out_shape=jax.ShapeDtypeStr...  32.6 us
    dot_general x6, matrix products, contract_first(): lax.dot_general(left, right, (((0,), (0,)), ((), ())), preferred_element_...  31.3 us
  transfers between devices with their start and end apart: 24, of which 7 were waited for; matrix products, arithmetic and copies ran while one was open for 19% of the time, Pallas kernels for 21%

profile of v6, /device:TPU:2, one launch (start us, length us, event | category | flops | bytes accessed | tf_op | source)
XLA Modules:
  0.0 684.7 jit_solution(15875995999678971211)
XLA Ops:
  16.3 4.2 collective-permute-done.1
  28.6 7.7 %collective-permute-done.7 = bf16[96,1728]{1,0:T(8,128)(2,1)S(1)} collective-permute-done((bf16[96,1728]{1,0:T(8,128)(2,1)S(1)}, bf16[96,1728]{1,0:T(8,128)(2,1)S(1)}, u32[]{:S(2)}, u32[]{:S(2)}) %collective-permute-start.7) | collective-permute-done | bytes 331808 | tf_op jit(solution)/shard_map/ppermute | solution.py:356
  36.3 13.3 %collective-permute-done.8 = bf16[96,1728]{1,0:T(8,128)(2,1)S(1)} collective-permute-done((bf16[96,1728]{1,0:T(8,128)(2,1)S(1)}, bf16[96,1728]{1,0:T(8,128)(2,1)S(1)}, u32[]{:S(2)}, u32[]{:S(2)}) %collective-permute-start.8) | collective-permute-done | bytes 331808 | tf_op jit(solution)/shard_map/ppermute | solution.py:356
  53.2 10.9 %collective-permute-start.4 = (bf16[768,768]{1,0:T(8,128)(2,1)S(1)}, bf16[768,768]{1,0:T(8,128)(2,1)}, u32[]{:S(2)}, u32[]{:S(2)}) collective-permute-start(bf16[768,768]{1,0:T(8,128)(2,1)S(1)} %copy-done.16), channel_id=1, source_target_pairs={{0,1},{1,2},{2,3},{4,5},{5,6},{6,7},{8,9},{9,10},{10,11},{12,13},{... | collective-permute-start | bytes 3538952 | tf_op jit(solution)/shard_map/ppermute | solution.py:437
  66.3 4.2 collective-permute-start.3
  73.8 3.9 select_subtract_fusion
  113.7 7.9 %convolution_convert_fusion.2.k_ref = bf16[2816,768]{1,0:T(8,128)(2,1)} fusion(bf16[2816,768]{1,0:T(8,128)(2,1)} %constant_dynamic-update-slice_fusion, bf16[768,2304]{1,0:T(8,128)(2,1)S(1)} %copy-done.20), kind=kOutput, calls=%fused_computation.23 | convolution fusion | flops 3324051456 | bytes 9830400 | tf_op jit(solution)/shard_map/dot_general | solution.py:505
  121.6 8.0 %add_convert_fusion.1.v_ref = bf16[2816,768]{1,0:T(8,128)(2,1)} fusion(bf16[2816,768]{1,0:T(8,128)(2,1)} %constant_dynamic-update-slice_fusion, f32[768]{0:T(1024)S(1)} %copy-done.35, bf16[768,2304]{1,0:T(8,128)(2,1)S(1)} %copy-done.20), kind=kOutput, calls=%fused_computation.19 | convolution fusion | flops 3326214144 | bytes 9834496 | tf_op jit(solution)/shard_map/dot_general | solution.py:506
  129.6 47.4 %shard_map.314 = (f32[768,768]{1,0:T(8,128)S(1)}, f32[12,768,1]{2,1,0:T(8,128)}) custom-call(s32[3]{0:T(128)S(1)} %copy-done.6, s32[3]{0:T(128)S(1)} %fusion.79.hi_ref, bf16[768,768]{1,0:T(8,128)(2,1)S(1)} %fusion.45.q_ref, bf16[2816,768]{1,0:T(8,128)(2,1)} %convolution_convert_fusion.2.k_ref, bf16[2816,768]{1,0:T(8,128)(2,1)} %add_convert_fusion.1.v_ref, ...), custom_call_target="tpu_custom_call" | custom-call | tf_op jit(solution)/shard_map/pallas_call | solution.py:221
  181.3 29.6 %multiply_convert_fusion = (bf16[768,3072]{1,0:T(8,128)(2,1)S(1)}, f32[768,3072]{1,0:T(8,128)}, f32[768,3072]{1,0:T(8,128)}) fusion(f32[3072]{0:T(1024)S(1)} %copy-done.30, bf16[768,6912]{1,0:T(8,128)(2,1)} %all-gather.5.cloned.1.call-done, f32[768,768]{0,1:T(8,128)S(1)} %get-tuple-element.294, f32[768]{0:T(1024)S(1)} %copy-done.33, f32[768]{0:T(1024)S(1)} %copy-done.27, ...), kind=kOutput, calls=%fused_computation.5 | convolution fusion | flops 3782541312 | bytes 30695424 | tf_op jit(solution)/shard_map/dot_general | solution.py:513
  211.0 6.0 fusion.104
  222.6 5.6 convolution_convert_fusion
  228.2 13.7 %fusion.105 = (bf16[3072]{0:T(1024)(128)(2,1)}, bf16[768,3072]{1,0:T(8,128)(2,1)S(1)}) fusion(f32[768,3072]{1,0:T(8,128)} %get-tuple-element.167, bf16[768,768]{0,1:T(8,128)(2,1)S(1)} %get-tuple-element.163, bf16[768,6912]{1,0:T(8,128)(2,1)} %all-gather.5.cloned.1.call-done, f32[768,3072]{1,0:T(8,128)} %get-tuple-element.295, f32[3072]{0:T(1024)S(1)} %copy-done.30), kind=kOutput, calls=%fused_computation.266 | convolution fusion | flops 3661624320 | bytes 29509632 | tf_op jit(solution)/shard_map/dot_general | solution.py:522
  241.9 5.8 convolution_convert_fusion.1
  247.7 7.9 %multiply_reduce_fusion = (bf16[768]{0:T(1024)(128)(2,1)}, f32[768]{0:T(1024)S(1)}, f32[768]{0:T(1024)S(1)}, bf16[768]{0:T(1024)(128)(2,1)}, f32[768,768]{0,1:T(8,128)S(1)}) fusion(f32[768,768]{0,1:T(8,128)S(1)} %get-tuple-element.294, f32[768]{0:T(1024)S(1)} %add_rsqrt_fusion.1, f32[768]{0:T(1024)S(1)} %broadcast_multiply_fusion.5, ...), kind=kOutput, calls=%fused_computation.48 | convolution fusion | flops 3634492416 | bytes 17728512 | tf_op jit(solution)/shard_map/dot_general | solution.py:329
  270.4 17.8 %concatenate.50 = bf16[768,7872]{1,0:T(8,128)(2,1)} concatenate(bf16[768,768]{1,0:T(8,128)(2,1)S(1)} %copy.159, bf16[768,3072]{1,0:T(8,128)(2,1)} %convolution_convert_fusion.1, bf16[768,3072]{1,0:T(8,128)(2,1)} %convolution_convert_fusion, bf16[768,96]{1,0:T(8,128)(2,1)S(1)} %bitcast.168, bf16[768,384]{1,0:T(8,128)(2,1)S(1)} %bitcast.165, bf16[768,96]{1,0:T(8,128)(2,1)} %bitcast.171, ...), dimensions={1} | concatenate | bytes 24182784 | tf_op jit(solution)/shard_map/concatenate | solution.py:392
  307.1 32.6 %shard_map.315 = f32[768,768]{1,0:T(8,128)S(1)} custom-call(s32[3]{0:T(128)S(1)} %copy-done.7, s32[3]{0:T(128)S(1)} %fusion.79.hi_ref, bf16[768,768]{1,0:T(8,128)(2,1)S(1)} %fusion.45.q_ref, bf16[2816,768]{1,0:T(8,128)(2,1)} %convolution_convert_fusion.2.k_ref, bf16[2816,768]{1,0:T(8,128)(2,1)} %add_convert_fusion.1.v_ref, s32[768,1]{1,0:T(8,128)S(1)} %copy-done.5, ...), custom_call_target="tpu_custom_call" | custom-call | tf_op jit(solution)/shard_map/pallas_call | solution.py:253
  339.8 60.7 %shard_map.316 = (f32[2816,768]{1,0:T(8,128)}, f32[2816,768]{1,0:T(8,128)}) custom-call(s32[11]{0:T(128)S(1)} %copy-done.9, s32[11]{0:T(128)S(1)} %copy-done.8, bf16[768,768]{1,0:T(8,128)(2,1)S(1)} %fusion.45.q_ref, bf16[2816,768]{1,0:T(8,128)(2,1)} %convolution_convert_fusion.2.k_ref, bf16[2816,768]{1,0:T(8,128)(2,1)} %add_convert_fusion.1.v_ref, ...), custom_call_target="tpu_custom_call" | custom-call | tf_op jit(solution)/shard_map/pallas_call | solution.py:284
  400.5 17.5 %reduce-scatter.5.cloned.1.call-done = bf16[96,7872]{1,0:T(8,128)(2,1)} async-done(((bf16[768,7872]{1,0:T(8,128)(2,1)}), bf16[96,7872]{1,0:T(8,128)(2,1)}) %reduce-scatter.5.cloned.1.call-update) | async-done | bytes 1511440 | tf_op jit(solution)/shard_map/reduce_scatter | solution.py:397
  425.7 7.0 %fusion.40 = bf16[768,2496]{0,1:T(8,128)(2,1)} fusion(bf16[768,2496]{0,1:T(8,128)(2,1)} %fusion.47, bf16[2816,768]{1,0:T(8,128)(2,1)} %constant_dynamic-update-slice_fusion, f32[2816,768]{1,0:T(8,128)S(1)} %copy-done.43), kind=kOutput, calls=%fused_computation.68 | convolution fusion | flops 3324641280 | bytes 14155776 | tf_op jit(solution)/shard_map/dot_general | solution.py:333
  432.7 7.0 %fusion.43 = bf16[768,2496]{0,1:T(8,128)(2,1)} fusion(bf16[768,2496]{0,1:T(8,128)(2,1)} %fusion.40, bf16[2816,768]{1,0:T(8,128)(2,1)} %constant_dynamic-update-slice_fusion, f32[2816,768]{1,0:T(8,128)S(1)} %copy-done.10), kind=kOutput, calls=%fused_computation.70 | convolution fusion | flops 3324641280 | bytes 14155776 | tf_op jit(solution)/shard_map/dot_general | solution.py:333
  442.1 6.4 copy.182
  469.7 31.4 %collective-permute-start.17 = (f32[96,1968]{1,0:T(8,128)}, f32[96,1968]{1,0:T(8,128)}, u32[]{:S(2)}, u32[]{:S(2)}) collective-permute-start(f32[96,1968]{1,0:T(8,128)} %get-tuple-element.179), channel_id=1, source_target_pairs={{0,1},{1,2},{2,3},{3,0},{4,5},{5,6},{6,7},{7,4},{8,9},{9,10},{10,1... | collective-permute-start | bytes 2267144 | tf_op jit(solution)/shard_map/ppermute | solution.py:415
  501.1 42.1 %collective-permute-start.18 = (f32[96,1968]{1,0:T(8,128)S(1)}, f32[96,1968]{1,0:T(8,128)}, u32[]{:S(2)}, u32[]{:S(2)}) collective-permute-start(f32[96,1968]{1,0:T(8,128)S(1)} %get-tuple-element.181), channel_id=1, source_target_pairs={{0,2},{1,3},{2,0},{3,1},{4,6},{5,7},{6,4},{7,5},{8,10},{9,11},{10,... | collective-permute-start | bytes 2267144 | tf_op jit(solution)/shard_map/ppermute | solution.py:415
  546.2 10.8 %fusion.29 = f32[2816,768]{0,1:T(8,128)} fusion(f32[2816,768]{1,0:T(8,128)} %get-tuple-element.37, bf16[768,2304]{1,0:T(8,128)(2,1)} %all-gather.3.cloned.1.call-done), kind=kOutput, calls=%fused_computation.62 | convolution fusion | flops 3324051456 | bytes 18481152 | tf_op jit(solution)/shard_map/dot_general | solution.py:329
  556.9 8.8 %fusion.106 = (bf16[2816,768]{0,1:T(8,128)(2,1)S(1)}, f32[2816,768]{0,1:T(8,128)}) fusion(f32[2816,768]{0,1:T(8,128)} %fusion.29, bf16[768,2304]{1,0:T(8,128)(2,1)} %all-gather.3.cloned.1.call-done, f32[2816,768]{1,0:T(8,128)S(1)} %bitcast.159), kind=kOutput, calls=%fused_computation.267 | convolution fusion | flops 3328376832 | bytes 31457280 | tf_op jit(solution)/shard_map/dot_general | solution.py:329
  568.6 5.6 collective-permute-start.12
  576.5 26.0 %collective-permute-start.13 = (bf16[256,768]{0,1:T(8,128)(2,1)}, bf16[256,768]{0,1:T(8,128)(2,1)}, u32[]{:S(2)}, u32[]{:S(2)}) collective-permute-start(bf16[256,768]{0,1:T(8,128)(2,1)} %get-tuple-element.176), channel_id=1, source_target_pairs={{0,2},{1,3},{4,6},{5,7},{8,10},{9,11},{12,14},{13,15},{16,18},{17,... | collective-permute-start | bytes 1179656 | tf_op jit(solution)/shard_map/ppermute | solution.py:437
  611.0 24.7 %collective-permute-start.14 = (f32[96,624]{0,1:T(8,128)}, f32[96,624]{0,1:T(8,128)S(1)}, u32[]{:S(2)}, u32[]{:S(2)}) collective-permute-start(f32[96,624]{0,1:T(8,128)} %get-tuple-element.235), channel_id=1, source_target_pairs={{0,1},{1,2},{2,3},{3,0},{4,5},{5,6},{6,7},{7,4},{8,9},{9,10},{10,1... | collective-permute-start | bytes 718856 | tf_op jit(solution)/shard_map/ppermute | solution.py:415
  635.7 8.9 %collective-permute-done.11 = bf16[256,768]{0,1:T(8,128)(2,1)} collective-permute-done((bf16[256,768]{0,1:T(8,128)(2,1)}, bf16[256,768]{0,1:T(8,128)(2,1)}, u32[]{:S(2)}, u32[]{:S(2)}) %collective-permute-start.11) | collective-permute-done | bytes 393248 | tf_op jit(solution)/shard_map/ppermute | solution.py:437
  644.6 20.8 %collective-permute-start.16 = (f32[96,624]{0,1:T(8,128)S(1)}, f32[96,624]{0,1:T(8,128)}, u32[]{:S(2)}, u32[]{:S(2)}) collective-permute-start(f32[96,624]{0,1:T(8,128)S(1)} %get-tuple-element.236), channel_id=1, source_target_pairs={{0,3},{1,0},{2,1},{3,2},{4,7},{5,4},{6,5},{7,6},{8,11},{9,8},{10,9... | collective-permute-start | bytes 718856 | tf_op jit(solution)/shard_map/ppermute | solution.py:415
  665.4 5.5 fusion.26
  (277 shorter events, 160.1 us)
Async XLA Ops:
  7.2 103.9 %all-gather.3.cloned.1.call-start = ((), (), s32[]{:S(2)}) async-start(), calls=%async_computation.2 | async-start | bytes 3981312 | tf_op jit(solution)/shard_map/all_gather | solution.py:371
  8.2 8.1 %collective-permute-start = (bf16[96,576]{1,0:T(8,128)(2,1)S(1)}, bf16[96,576]{1,0:T(8,128)(2,1)S(1)}, u32[]{:S(2)}, u32[]{:S(2)}) collective-permute-start(bf16[96,576]{1,0:T(8,128)(2,1)S(1)} %pad_maximum_fusion.4), channel_id=1, source_target_pairs={{0,1},{1,2},{2,3},{3,0},{4,5},{5,6},{6,7},{7,4},{8,9},{9,10},{10,1... | collective-permute-start | bytes 331784 | tf_op jit(solution)/shard_map/ppermute | solution.py:356
  9.8 10.7 %collective-permute-start.1 = (bf16[96,576]{1,0:T(8,128)(2,1)S(1)}, bf16[96,576]{1,0:T(8,128)(2,1)S(1)}, u32[]{:S(2)}, u32[]{:S(2)}) collective-permute-start(bf16[96,576]{1,0:T(8,128)(2,1)S(1)} %pad_maximum_fusion.4), channel_id=1, source_target_pairs={{0,2},{1,3},{2,0},{3,1},{4,6},{5,7},{6,4},{7,5},{8,10},{9,11},{10,... | collective-permute-start | bytes 331784 | tf_op jit(solution)/shard_map/ppermute | solution.py:356
  12.4 8.1 %collective-permute-start.2 = (bf16[96,576]{1,0:T(8,128)(2,1)S(1)}, bf16[96,576]{1,0:T(8,128)(2,1)S(1)}, u32[]{:S(2)}, u32[]{:S(2)}) collective-permute-start(bf16[96,576]{1,0:T(8,128)(2,1)S(1)} %pad_maximum_fusion.4), channel_id=1, source_target_pairs={{0,3},{1,0},{2,1},{3,2},{4,7},{5,4},{6,5},{7,6},{8,11},{9,8},{10,9... | collective-permute-start | bytes 331784 | tf_op jit(solution)/shard_map/ppermute | solution.py:356
  22.6 154.4 %all-gather.5.cloned.1.call-start = ((), (), s32[]{:S(2)}) async-start(), calls=%async_computation.3 | async-start | bytes 11943936 | tf_op jit(solution)/shard_map/all_gather | solution.py:371
  23.0 13.3 %collective-permute-start.7 = (bf16[96,1728]{1,0:T(8,128)(2,1)S(1)}, bf16[96,1728]{1,0:T(8,128)(2,1)S(1)}, u32[]{:S(2)}, u32[]{:S(2)}) collective-permute-start(bf16[96,1728]{1,0:T(8,128)(2,1)S(1)} %concatenate.48), channel_id=1, source_target_pairs={{0,1},{1,2},{2,3},{3,0},{4,5},{5,6},{6,7},{7,4},{8,9},{9,10},{10,1... | collective-permute-start | bytes 995336 | tf_op jit(solution)/shard_map/ppermute | solution.py:356
  26.2 23.5 %collective-permute-start.8 = (bf16[96,1728]{1,0:T(8,128)(2,1)S(1)}, bf16[96,1728]{1,0:T(8,128)(2,1)S(1)}, u32[]{:S(2)}, u32[]{:S(2)}) collective-permute-start(bf16[96,1728]{1,0:T(8,128)(2,1)S(1)} %concatenate.48), channel_id=1, source_target_pairs={{0,2},{1,3},{2,0},{3,1},{4,6},{5,7},{6,4},{7,5},{8,10},{9,11},{10,... | collective-permute-start | bytes 995336 | tf_op jit(solution)/shard_map/ppermute | solution.py:356
  27.8 21.8 %collective-permute-start.9 = (bf16[96,1728]{1,0:T(8,128)(2,1)S(1)}, bf16[96,1728]{1,0:T(8,128)(2,1)S(1)}, u32[]{:S(2)}, u32[]{:S(2)}) collective-permute-start(bf16[96,1728]{1,0:T(8,128)(2,1)S(1)} %concatenate.48), channel_id=1, source_target_pairs={{0,3},{1,0},{2,1},{3,2},{4,7},{5,4},{6,5},{7,6},{8,11},{9,8},{10,9... | collective-permute-start | bytes 995336 | tf_op jit(solution)/shard_map/ppermute | solution.py:356
  53.1 42.5 %copy-start.18 = (bf16[768,768]{1,0:T(8,128)(2,1)S(1)}, bf16[768,768]{1,0:T(8,128)(2,1)}, u32[]{:S(2)}) copy-start(bf16[768,768]{1,0:T(8,128)(2,1)} %param.43) | copy-start | bytes 3538948
  53.1 364.9 %reduce-scatter.5.cloned.1.call-start = ((), (), s32[]{:S(2)}) async-start(), calls=%async_computation.4 | async-start | bytes 13713408 | tf_op jit(solution)/shard_map/reduce_scatter | solution.py:397
  53.2 48.6 %collective-permute-start.4 = (bf16[768,768]{1,0:T(8,128)(2,1)S(1)}, bf16[768,768]{1,0:T(8,128)(2,1)}, u32[]{:S(2)}, u32[]{:S(2)}) collective-permute-start(bf16[768,768]{1,0:T(8,128)(2,1)S(1)} %copy-done.16), channel_id=1, source_target_pairs={{0,1},{1,2},{2,3},{4,5},{5,6},{6,7},{8,9},{9,10},{10,11},{12,13},{... | collective-permute-start | bytes 3538952 | tf_op jit(solution)/shard_map/ppermute | solution.py:437
  64.1 41.3 %collective-permute-start.5 = (bf16[768,768]{1,0:T(8,128)(2,1)S(1)}, bf16[768,768]{1,0:T(8,128)(2,1)S(1)}, u32[]{:S(2)}, u32[]{:S(2)}) collective-permute-start(bf16[768,768]{1,0:T(8,128)(2,1)S(1)} %copy-done.16), channel_id=1, source_target_pairs={{1,0},{2,1},{3,2},{5,4},{6,5},{7,6},{9,8},{10,9},{11,10},{13,12},{... | collective-permute-start | bytes 3538952 | tf_op jit(solution)/shard_map/ppermute | solution.py:437
  66.3 33.7 %collective-permute-start.3 = (bf16[256,768]{1,0:T(8,128)(2,1)}, bf16[256,768]{1,0:T(8,128)(2,1)}, u32[]{:S(2)}, u32[]{:S(2)}) collective-permute-start(bf16[256,768]{1,0:T(8,128)(2,1)} %get-tuple-element.259), channel_id=1, source_target_pairs={{0,2},{1,3},{4,6},{5,7},{8,10},{9,11},{12,14},{13,15},{16,18},{17,... | collective-permute-start | bytes 1179656 | tf_op jit(solution)/shard_map/ppermute | solution.py:437
  70.6 38.8 %collective-permute-start.6 = (bf16[256,768]{1,0:T(8,128)(2,1)}, bf16[256,768]{1,0:T(8,128)(2,1)}, u32[]{:S(2)}, u32[]{:S(2)}) collective-permute-start(bf16[256,768]{1,0:T(8,128)(2,1)} %get-tuple-element.258), channel_id=1, source_target_pairs={{2,0},{3,1},{6,4},{7,5},{10,8},{11,9},{14,12},{15,13},{18,16},{19,... | collective-permute-start | bytes 1179656 | tf_op jit(solution)/shard_map/ppermute | solution.py:437
  177.0 80.2 %copy-start.3 = (f32[768,768]{1,0:T(8,128)}, f32[768,768]{1,0:T(8,128)S(1)}, u32[]{:S(2)}) copy-start(f32[768,768]{1,0:T(8,128)S(1)} %get-tuple-element.30) | copy-start | bytes 7077892
  181.3 29.6 %copy-start.34 = (f32[768]{0:T(1024)S(1)}, f32[768]{0:T(1024)}, u32[]{:S(2)}) copy-start(f32[768]{0:T(1024)} %convert_element_type.204) | copy-start | bytes 9220
  291.4 316.1 %reduce-scatter.7.cloned.1.call-start = ((), (), s32[]{:S(2)}) async-start(), calls=%async_computation.5 | async-start | bytes 4423680
  307.1 32.6 %copy-start.2 = (bf16[768,768]{1,0:T(8,128)(2,1)S(1)}, bf16[768,768]{1,0:T(8,128)(2,1)}, u32[]{:S(2)}) copy-start(bf16[768,768]{1,0:T(8,128)(2,1)} %copy-done) | copy-start | bytes 3538948
  307.1 32.6 %copy-start.8 = (s32[11]{0:T(128)S(1)}, s32[11]{0:T(128)}, u32[]{:S(2)}) copy-start(s32[11]{0:T(128)} %get-tuple-element.160.hi_ref) | copy-start | bytes 136
  307.1 32.6 %copy-start.9 = (s32[11]{0:T(128)S(1)}, s32[11]{0:T(128)}, u32[]{:S(2)}) copy-start(s32[11]{0:T(128)} %get-tuple-element.161.lo_ref) | copy-start | bytes 136
  467.7 89.2 %slice-start = ((s8[8650752]{0:T(1024)(128)(4,1)}), s8[4194304]{0:T(1024)(128)(4,1)S(1)}, s32[]{:S(2)}) async-start(s8[8650752]{0:T(1024)(128)(4,1)} %bitcast.158), calls=%async_computation.6 | async-start | bytes 8388608
  469.7 105.5 %collective-permute-start.17 = (f32[96,1968]{1,0:T(8,128)}, f32[96,1968]{1,0:T(8,128)}, u32[]{:S(2)}, u32[]{:S(2)}) collective-permute-start(f32[96,1968]{1,0:T(8,128)} %get-tuple-element.179), channel_id=1, source_target_pairs={{0,1},{1,2},{2,3},{3,0},{4,5},{5,6},{6,7},{7,4},{8,9},{9,10},{10,1... | collective-permute-start | bytes 2267144 | tf_op jit(solution)/shard_map/ppermute | solution.py:415
  501.1 75.3 %collective-permute-start.18 = (f32[96,1968]{1,0:T(8,128)S(1)}, f32[96,1968]{1,0:T(8,128)}, u32[]{:S(2)}, u32[]{:S(2)}) collective-permute-start(f32[96,1968]{1,0:T(8,128)S(1)} %get-tuple-element.181), channel_id=1, source_target_pairs={{0,2},{1,3},{2,0},{3,1},{4,6},{5,7},{6,4},{7,5},{8,10},{9,11},{10,... | collective-permute-start | bytes 2267144 | tf_op jit(solution)/shard_map/ppermute | solution.py:415
  543.2 59.2 %collective-permute-start.19 = (f32[96,1968]{1,0:T(8,128)S(1)}, f32[96,1968]{1,0:T(8,128)}, u32[]{:S(2)}, u32[]{:S(2)}) collective-permute-start(f32[96,1968]{1,0:T(8,128)S(1)} %get-tuple-element.180), channel_id=1, source_target_pairs={{0,3},{1,0},{2,1},{3,2},{4,7},{5,4},{6,5},{7,6},{8,11},{9,8},{10,9... | collective-permute-start | bytes 2267144 | tf_op jit(solution)/shard_map/ppermute | solution.py:415
  567.3 98.1 %collective-permute-start.10 = (bf16[768,768]{0,1:T(8,128)(2,1)}, bf16[768,768]{0,1:T(8,128)(2,1)}, u32[]{:S(2)}, u32[]{:S(2)}) collective-permute-start(bf16[768,768]{0,1:T(8,128)(2,1)} %get-tuple-element.177), channel_id=1, source_target_pairs={{1,0},{2,1},{3,2},{5,4},{6,5},{7,6},{9,8},{10,9},{11,10},{13,12},{... | collective-permute-start | bytes 3538952 | tf_op jit(solution)/shard_map/ppermute | solution.py:437
  568.6 96.8 %collective-permute-start.12 = (bf16[768,768]{0,1:T(8,128)(2,1)}, bf16[768,768]{0,1:T(8,128)(2,1)}, u32[]{:S(2)}, u32[]{:S(2)}) collective-permute-start(bf16[768,768]{0,1:T(8,128)(2,1)} %get-tuple-element.178), channel_id=1, source_target_pairs={{0,1},{1,2},{2,3},{4,5},{5,6},{6,7},{8,9},{9,10},{10,11},{12,13},{... | collective-permute-start | bytes 3538952 | tf_op jit(solution)/shard_map/ppermute | solution.py:437
  575.2 69.4 %collective-permute-start.11 = (bf16[256,768]{0,1:T(8,128)(2,1)}, bf16[256,768]{0,1:T(8,128)(2,1)}, u32[]{:S(2)}, u32[]{:S(2)}) collective-permute-start(bf16[256,768]{0,1:T(8,128)(2,1)} %get-tuple-element.175), channel_id=1, source_target_pairs={{2,0},{3,1},{6,4},{7,5},{10,8},{11,9},{14,12},{15,13},{18,16},{19,... | collective-permute-start | bytes 1179656 | tf_op jit(solution)/shard_map/ppermute | solution.py:437
  576.5 68.1 %collective-permute-start.13 = (bf16[256,768]{0,1:T(8,128)(2,1)}, bf16[256,768]{0,1:T(8,128)(2,1)}, u32[]{:S(2)}, u32[]{:S(2)}) collective-permute-start(bf16[256,768]{0,1:T(8,128)(2,1)} %get-tuple-element.176), channel_id=1, source_target_pairs={{0,2},{1,3},{4,6},{5,7},{8,10},{9,11},{12,14},{13,15},{16,18},{17,... | collective-permute-start | bytes 1179656 | tf_op jit(solution)/shard_map/ppermute | solution.py:437
  609.1 56.3 %copy-start.12 = (f32[768,768]{0,1:T(8,128)S(1)}, f32[768,768]{0,1:T(8,128)}, u32[]{:S(2)}) copy-start(f32[768,768]{0,1:T(8,128)} %copy-done.11) | copy-start | bytes 7077892
  611.0 62.9 %collective-permute-start.14 = (f32[96,624]{0,1:T(8,128)}, f32[96,624]{0,1:T(8,128)S(1)}, u32[]{:S(2)}, u32[]{:S(2)}) collective-permute-start(f32[96,624]{0,1:T(8,128)} %get-tuple-element.235), channel_id=1, source_target_pairs={{0,1},{1,2},{2,3},{3,0},{4,5},{5,6},{6,7},{7,4},{8,9},{9,10},{10,1... | collective-permute-start | bytes 718856 | tf_op jit(solution)/shard_map/ppermute | solution.py:415
  644.6 29.3 %collective-permute-start.15 = (f32[96,624]{0,1:T(8,128)S(1)}, f32[96,624]{0,1:T(8,128)}, u32[]{:S(2)}, u32[]{:S(2)}) collective-permute-start(f32[96,624]{0,1:T(8,128)S(1)} %get-tuple-element.237), channel_id=1, source_target_pairs={{0,2},{1,3},{2,0},{3,1},{4,6},{5,7},{6,4},{7,5},{8,10},{9,11},{10,... | collective-permute-start | bytes 718856 | tf_op jit(solution)/shard_map/ppermute | solution.py:415
  644.6 29.3 %collective-permute-start.16 = (f32[96,624]{0,1:T(8,128)S(1)}, f32[96,624]{0,1:T(8,128)}, u32[]{:S(2)}, u32[]{:S(2)}) collective-permute-start(f32[96,624]{0,1:T(8,128)S(1)} %get-tuple-element.236), channel_id=1, source_target_pairs={{0,3},{1,0},{2,1},{3,2},{4,7},{5,4},{6,5},{7,6},{8,11},{9,8},{10,9... | collective-permute-start | bytes 718856 | tf_op jit(solution)/shard_map/ppermute | solution.py:415
  (41 other events, 201.7 us)
Sparse Core Ops, SparseCore 0:
  22.7 35.6 all-gather.2
  60.2 63.7 all-gather.4
  291.5 126.4 reduce-scatter.4
  448.6 119.7 reduce-scatter.6
